TPU v7x, 768 devices: a whole 4x8x12 slice. The times are simulated.
768 devices in a mesh: gx: 64 (over y, x, core), gy: 12 (over z).
Axes of the slice: x: 4, y: 8, z: 12, core: 2. Of those that a mesh axis runs over, the one named last changes fastest.
Arguments:
- rhs_field: float32 [3, 128, 384, 128], P(None, 'gx', 'gy'), may hold values from -6 to 6
- shear_modulus: float32 [128, 384, 128], P('gx', 'gy'), may hold values from 0.3 to 3
- lame_lambda: float32 [128, 384, 128], P('gx', 'gy'), may hold values from 0.3 to 3
- group_start: int32 [64, 12], P('gx'), may hold values from 0 to 1, as said below
Outputs:
- solution_field: float32 [3, 128, 384, 128], P(None, 'gx', 'gy')
- residual_field: float32 [3, 128, 384, 128], P(None, 'gx', 'gy')
Inputs may be any that keep to these rules, and one draw needn't show every extreme that they name: `group_start`: each index of gx has exactly one 1, at an index of gy from 1 to 11.
All inputs are finite; a program needn't handle non-finite values.
Results may differ from a plain program's by a relative error of at most 0.00011.
Values sent between devices are 32-bit elements; how exact they have to be, the bound alone decides.
No kernel may reach another device: no remote copies, remote signals or barrier semaphores. Data moves between devices by JAX's collectives and lax.ppermute only.
A program may use at most 32 MiB of HBM per device.

v0:
```python
import jax
import jax.numpy as jnp
from jax import lax
from jax.sharding import PartitionSpec as P

SWEEPS = 3
COARSE_SWEEPS = 4


LOW_BOUND = 0.5
HIGH_BOUND = 6.0
SHIFT_SCALE = 48.0
UNITS = ((1, 0, 0), (0, 1, 0), (0, 0, 1))


def padded_2(block, sides, width):
    for axis, dim in sides:
        count = lax.axis_size(axis)
        forward = [(i, i + 1) for i in range(count - 1)]
        backward = [(target, source) for source, target in forward]
        low = lax.ppermute(
            lax.slice_in_dim(block, block.shape[dim] - width, None, axis=dim), axis, forward
        )
        high = lax.ppermute(lax.slice_in_dim(block, 0, width, axis=dim), axis, backward)
        block = jnp.concatenate([low, block, high], axis=dim)
    return block


def shifted(array, step_x, step_y, step_z):
    size_x = array.shape[-3] - 2
    size_y = array.shape[-2] - 2
    size_z = array.shape[-1] - 2
    return array[
        ...,
        1 + step_x : 1 + step_x + size_x,
        1 + step_y : 1 + step_y + size_y,
        1 + step_z : 1 + step_z + size_z,
    ]


def diagonal(mu_pad, lam_pad, scale):
    mu_centre = shifted(mu_pad, 0, 0, 0)
    lam_centre = shifted(lam_pad, 0, 0, 0)
    faces = 0.0
    for unit in UNITS:
        backward = tuple((-value for value in unit))
        faces = (
            faces
            + 0.5 * (mu_centre + shifted(mu_pad, *unit))
            + 0.5 * (mu_centre + shifted(mu_pad, *backward))
        )
    results = []
    for unit in UNITS:
        backward = tuple((-value for value in unit))
        results.append(scale * (faces + lam_centre + shifted(lam_pad, *backward)))
    return jnp.stack(results)


def operate(field_pad, mu_pad, lam_pad, scale):
    mu_centre = shifted(mu_pad, 0, 0, 0)
    lam_centre = shifted(lam_pad, 0, 0, 0)
    components = [field_pad[0], field_pad[1], field_pad[2]]
    centres = [shifted(value, 0, 0, 0) for value in components]
    laplace = [0.0, 0.0, 0.0]
    for unit in UNITS:
        backward = tuple((-value for value in unit))
        face_up = 0.5 * (mu_centre + shifted(mu_pad, *unit))
        face_down = 0.5 * (mu_centre + shifted(mu_pad, *backward))
        for comp_id in range(3):
            laplace[comp_id] = (
                laplace[comp_id]
                + face_up * (shifted(components[comp_id], *unit) - centres[comp_id])
                - face_down * (centres[comp_id] - shifted(components[comp_id], *backward))
            )

    def spread(offset):
        total = 0.0
        for comp_id in range(3):
            ahead = tuple((offset[axis_id] + UNITS[comp_id][axis_id] for axis_id in range(3)))
            total = total + (
                shifted(components[comp_id], *ahead) - shifted(components[comp_id], *offset)
            )
        return total

    stress_here = lam_centre * spread((0, 0, 0))
    results = []
    for comp_id in range(3):
        backward = tuple((-value for value in UNITS[comp_id]))
        grad_term = stress_here - shifted(lam_pad, *backward) * spread(backward)
        results.append(scale * (-laplace[comp_id] - grad_term))
    return jnp.stack(results)


def smooth(solution, residual, inverse_diag, apply_fn, steps):
    midpoint = 0.5 * (HIGH_BOUND + LOW_BOUND)
    halfwidth = 0.5 * (HIGH_BOUND - LOW_BOUND)
    sharpness = midpoint / halfwidth
    weight_old = 1.0 / sharpness
    direction = inverse_diag * residual / midpoint
    solution = solution + direction
    residual = residual - apply_fn(direction)
    for step_id in range(steps - 1):
        weight_new = 1.0 / (2.0 * sharpness - weight_old)
        direction = weight_new * weight_old * direction + 2.0 * weight_new / halfwidth * (
            inverse_diag * residual
        )
        solution = solution + direction
        residual = residual - apply_fn(direction)
        weight_old = weight_new
    return (solution, residual)


def pad_groups(array, starts):
    cont = jnp.where(starts[..., 1:] == 0, 1.0, 0.0)
    closed = jnp.zeros_like(cont[..., :1])
    lower = jnp.concatenate([closed, cont], axis=-1)[..., None, None, None]
    upper = jnp.concatenate([cont, closed], axis=-1)[..., None, None, None]
    below = (
        jnp.concatenate(
            [jnp.zeros_like(array[..., :1, :, :1, :]), array[..., :-1, :, -1:, :]], axis=-4
        )
        * lower
    )
    above = (
        jnp.concatenate(
            [array[..., 1:, :, :1, :], jnp.zeros_like(array[..., :1, :, :1, :])], axis=-4
        )
        * upper
    )
    joined = jnp.concatenate([below, array, above], axis=-2)
    widths = [(0, 0)] * (joined.ndim - 3) + [(1, 1), (0, 0), (1, 1)]
    return jnp.pad(joined, widths)


def same_group(starts):
    count = starts.shape[-1]
    marks = jnp.where(jnp.arange(count, dtype=jnp.int32) > 0, starts, 0)
    labels = jnp.cumsum(marks, axis=-1)
    return jnp.where(labels[..., :, None] == labels[..., None, :], 1.0, 0.0).astype(jnp.float32)


def shards(rhs_field, shear_modulus, lame_lambda, group_start):
    coefficients = jnp.stack([shear_modulus, lame_lambda])
    padded = padded_2(coefficients, (("gx", 1), ("gy", 2)), 1)
    padded = jnp.pad(padded, ((0, 0), (0, 0), (0, 0), (1, 1)))
    mu_pad = padded[0]
    lam_pad = padded[1]
    inverse_diag = 1.0 / diagonal(mu_pad, lam_pad, 1.0)

    def fine_apply(field):
        extended = padded_2(field, (("gx", 1), ("gy", 2)), 1)
        extended = jnp.pad(extended, ((0, 0), (0, 0), (0, 0), (1, 1)))
        return operate(extended, mu_pad, lam_pad, 1.0)

    solution, residual = smooth(
        jnp.zeros_like(rhs_field), rhs_field, inverse_diag, fine_apply, SWEEPS
    )
    coarse_x = rhs_field.shape[1] // 2
    coarse_y = rhs_field.shape[2] // 2
    coarse_z = rhs_field.shape[3] // 2
    coarse_res = residual.reshape(3, coarse_x, 2, coarse_y, 2, coarse_z, 2).sum(axis=(2, 4, 6))
    coarse_mu = shear_modulus.reshape(coarse_x, 2, coarse_y, 2, coarse_z, 2).mean(axis=(1, 3, 5))
    coarse_lam = lame_lambda.reshape(coarse_x, 2, coarse_y, 2, coarse_z, 2).mean(axis=(1, 3, 5))
    starts = group_start[0]
    position = lax.axis_index("gy")
    members = same_group(starts)
    my_members = lax.dynamic_index_in_dim(members, position, 0, keepdims=False)
    cells_dev = coarse_x * coarse_y * coarse_z
    group_cells = jnp.sum(my_members) * cells_dev
    packed = jnp.concatenate([coarse_res, jnp.stack([coarse_mu, coarse_lam])], axis=0)[:, None]
    column = lax.all_gather(packed, "gy", axis=1, tiled=True)
    coef_pad = pad_groups(column[3:5], starts)
    coarse_inverse = 1.0 / diagonal(coef_pad[0], coef_pad[1], 4.0)

    def coarse_apply(field):
        return operate(pad_groups(field, starts), coef_pad[0], coef_pad[1], 4.0)

    column_res = column[0:3]
    smoothed, coarse_left = smooth(
        jnp.zeros_like(column_res), column_res, coarse_inverse, coarse_apply, COARSE_SWEEPS
    )
    mine = lax.dynamic_index_in_dim(smoothed, position, 1, keepdims=False)
    device_sums = column_res.sum(axis=(2, 3, 4))
    totals = jnp.sum(device_sums * my_members[None, :], axis=1)
    group_shift = totals / (SHIFT_SCALE * group_cells)
    mine = mine + group_shift[:, None, None, None]
    fine_corr = jnp.broadcast_to(
        mine[:, :, None, :, None, :, None], (3, coarse_x, 2, coarse_y, 2, coarse_z, 2)
    ).reshape(rhs_field.shape)
    solution = solution + fine_corr
    residual = residual - fine_apply(fine_corr)
    solution, residual = smooth(solution, residual, inverse_diag, fine_apply, SWEEPS)
    return (solution, residual)


def solution(mesh):
    return jax.shard_map(
        shards,
        mesh=mesh,
        in_specs=(
            P(None, "gx", "gy", None),
            P("gx", "gy", None),
            P("gx", "gy", None),
            P("gx", None),
        ),
        out_specs=(P(None, "gx", "gy", None), P(None, "gx", "gy", None)),
        check_vma=False,
    )
```

profile of v0, /device:TPU:31, one launch (start us, length us, event | category | flops | bytes accessed | tf_op | source)
XLA Modules:
  0.0 227.0 jit_solution(6632730894957272489)
XLA Ops:
  1.5 4.9 %collective-permute-start = (f32[2,1,32,128]{3,2,1,0:T(8,128)S(1)}, f32[2,1,32,128]{3,2,1,0:T(8,128)S(1)}, u32[]{:S(2)}, u32[]{:S(2)}) collective-permute-start(f32[2,1,32,128]{3,2,1,0:T(8,128)S(1)} %get-tuple-element.123), channel_id=1, source_target_pairs={{0,12},{12,24},{24,36},{36,48},{48,60},{60,72},{72,84},{84,96},{96... | collective-permute-start | bytes 98312 | tf_op jit(solution)/shard_map/ppermute | solution.py:21
  8.3 6.6 %collective-permute-done.1 = f32[2,1,32,128]{3,2,1,0:T(8,128)S(1)} collective-permute-done((f32[2,1,32,128]{3,2,1,0:T(8,128)S(1)}, f32[2,1,32,128]{3,2,1,0:T(8,128)S(1)}, u32[]{:S(2)}, u32[]{:S(2)}) %collective-permute-start.1) | collective-permute-done | bytes 32800 | tf_op jit(solution)/shard_map/ppermute | solution.py:24
  15.7 4.0 %collective-permute-start.2 = (f32[2,4,1,128]{3,2,1,0:T(1,128)S(1)}, f32[2,4,1,128]{3,2,1,0:T(1,128)S(1)}, u32[]{:S(2)}, u32[]{:S(2)}) collective-permute-start(f32[2,4,1,128]{3,2,1,0:T(1,128)S(1)} %get-tuple-element.109), channel_id=1, source_target_pairs={{0,1},{1,2},{2,3},{3,4},{4,5},{5,6},{6,7},{7,8},{8,9},{9,10},{10,1... | collective-permute-start | bytes 12296 | tf_op jit(solution)/shard_map/ppermute | solution.py:21
  21.0 3.7 %collective-permute-done.3 = f32[2,4,1,128]{3,2,1,0:T(1,128)S(1)} collective-permute-done((f32[2,4,1,128]{3,2,1,0:T(1,128)S(1)}, f32[2,4,1,128]{3,2,1,0:T(1,128)S(1)}, u32[]{:S(2)}, u32[]{:S(2)}) %collective-permute-start.3) | collective-permute-done | bytes 4128 | tf_op jit(solution)/shard_map/ppermute | solution.py:24
  25.9 3.1 %collective-permute-start.4 = (f32[3,1,32,128]{3,2,1,0:T(8,128)S(1)}, f32[3,1,32,128]{3,2,1,0:T(8,128)S(1)}, u32[]{:S(2)}, u32[]{:S(2)}) collective-permute-start(f32[3,1,32,128]{3,2,1,0:T(8,128)S(1)} %get-tuple-element.121), channel_id=1, source_target_pairs={{0,12},{12,24},{24,36},{36,48},{48,60},{60,72},{72,84},{84,96},{96... | collective-permute-start | bytes 147464 | tf_op jit(solution)/shard_map/ppermute | solution.py:21
  33.5 4.3 %collective-permute-done.5 = f32[3,1,32,128]{3,2,1,0:T(8,128)S(1)} collective-permute-done((f32[3,1,32,128]{3,2,1,0:T(8,128)S(1)}, f32[3,1,32,128]{3,2,1,0:T(8,128)S(1)}, u32[]{:S(2)}, u32[]{:S(2)}) %collective-permute-start.5) | collective-permute-done | bytes 49184 | tf_op jit(solution)/shard_map/ppermute | solution.py:24
  37.8 4.0 %collective-permute-start.6 = (f32[3,4,1,128]{3,2,1,0:T(1,128)S(1)}, f32[3,4,1,128]{3,2,1,0:T(1,128)S(1)}, u32[]{:S(2)}, u32[]{:S(2)}) collective-permute-start(f32[3,4,1,128]{3,2,1,0:T(1,128)S(1)} %get-tuple-element.105), channel_id=1, source_target_pairs={{0,1},{1,2},{2,3},{3,4},{4,5},{5,6},{6,7},{7,8},{8,9},{9,10},{10,1... | collective-permute-start | bytes 18440 | tf_op jit(solution)/shard_map/ppermute | solution.py:21
  43.1 4.9 %collective-permute-done.7 = f32[3,4,1,128]{3,2,1,0:T(1,128)S(1)} collective-permute-done((f32[3,4,1,128]{3,2,1,0:T(1,128)S(1)}, f32[3,4,1,128]{3,2,1,0:T(1,128)S(1)}, u32[]{:S(2)}, u32[]{:S(2)}) %collective-permute-start.7) | collective-permute-done | bytes 6176 | tf_op jit(solution)/shard_map/ppermute | solution.py:24
  48.9 3.8 %collective-permute-start.8 = (f32[3,1,32,128]{3,2,1,0:T(8,128)S(1)}, f32[3,1,32,128]{3,2,1,0:T(8,128)S(1)}, u32[]{:S(2)}, u32[]{:S(2)}) collective-permute-start(f32[3,1,32,128]{3,2,1,0:T(8,128)S(1)} %get-tuple-element.119), channel_id=1, source_target_pairs={{0,12},{12,24},{24,36},{36,48},{48,60},{60,72},{72,84},{84,96},{96... | collective-permute-start | bytes 147464 | tf_op jit(solution)/shard_map/ppermute | solution.py:21
  54.8 6.7 %collective-permute-done.9 = f32[3,1,32,128]{3,2,1,0:T(8,128)S(1)} collective-permute-done((f32[3,1,32,128]{3,2,1,0:T(8,128)S(1)}, f32[3,1,32,128]{3,2,1,0:T(8,128)S(1)}, u32[]{:S(2)}, u32[]{:S(2)}) %collective-permute-start.9) | collective-permute-done | bytes 49184 | tf_op jit(solution)/shard_map/ppermute | solution.py:24
  61.5 4.8 %collective-permute-start.10 = (f32[3,4,1,128]{3,2,1,0:T(1,128)S(1)}, f32[3,4,1,128]{3,2,1,0:T(1,128)S(1)}, u32[]{:S(2)}, u32[]{:S(2)}) collective-permute-start(f32[3,4,1,128]{3,2,1,0:T(1,128)S(1)} %get-tuple-element.103), channel_id=1, source_target_pairs={{0,1},{1,2},{2,3},{3,4},{4,5},{5,6},{6,7},{7,8},{8,9},{9,10},{10,1... | collective-permute-start | bytes 18440 | tf_op jit(solution)/shard_map/ppermute | solution.py:21
  72.0 3.0 %collective-permute-start.12 = (f32[3,1,32,128]{3,2,1,0:T(8,128)S(1)}, f32[3,1,32,128]{3,2,1,0:T(8,128)S(1)}, u32[]{:S(2)}, u32[]{:S(2)}) collective-permute-start(f32[3,1,32,128]{3,2,1,0:T(8,128)S(1)} %get-tuple-element.117), channel_id=1, source_target_pairs={{0,12},{12,24},{24,36},{36,48},{48,60},{60,72},{72,84},{84,96},{96... | collective-permute-start | bytes 147464 | tf_op jit(solution)/shard_map/ppermute | solution.py:21
  78.7 5.1 %collective-permute-done.13 = f32[3,1,32,128]{3,2,1,0:T(8,128)S(1)} collective-permute-done((f32[3,1,32,128]{3,2,1,0:T(8,128)S(1)}, f32[3,1,32,128]{3,2,1,0:T(8,128)S(1)}, u32[]{:S(2)}, u32[]{:S(2)}) %collective-permute-start.13) | collective-permute-done | bytes 49184 | tf_op jit(solution)/shard_map/ppermute | solution.py:24
  83.8 4.4 %collective-permute-start.14 = (f32[3,4,1,128]{3,2,1,0:T(1,128)S(1)}, f32[3,4,1,128]{3,2,1,0:T(1,128)S(1)}, u32[]{:S(2)}, u32[]{:S(2)}) collective-permute-start(f32[3,4,1,128]{3,2,1,0:T(1,128)S(1)} %get-tuple-element.101), channel_id=1, source_target_pairs={{0,1},{1,2},{2,3},{3,4},{4,5},{5,6},{6,7},{7,8},{8,9},{9,10},{10,1... | collective-permute-start | bytes 18440 | tf_op jit(solution)/shard_map/ppermute | solution.py:21
  94.9 3.9 %reduce_sum.62 = f32[3,16,2,64,2]{4,3,2,1,0:T(8,128)S(1)} reshape(f32[3,32,128]{2,1,0:T(8,128)} %fusion.448) | data formatting | bytes 98304 | tf_op jit(solution)/shard_map/reduce_sum | solution.py:161
  100.6 21.6 %all-gather = f32[5,12,16,64]{3,2,1,0:T(8,128)S(1)} all-gather(f32[5,1,16,64]{3,2,1,0:T(8,128)S(1)} %pad_maximum_fusion), channel_id=2, replica_groups=mesh['gx'=64,'gy'=12] {'gy'}, dimensions={1}, use_global_device_ids=true | all-gather | bytes 266240 | tf_op jit(solution)/shard_map/all_gather | solution.py:171
  131.1 2.7 %slice.1640 = f32[3,1,32,128]{3,2,0,1:T(8,128)} reshape(f32[3,16,2,64,2]{4,3,2,1,0:T(8,128)S(1)} %broadcast_in_dim.46) | data formatting | bytes 98304 | tf_op jit(solution)/shard_map/slice | solution.py:22
  133.8 8.2 %collective-permute-start.16 = (f32[3,1,32,128]{3,2,0,1:T(8,128)}, f32[3,1,32,128]{3,2,0,1:T(8,128)}, u32[]{:S(2)}, u32[]{:S(2)}) collective-permute-start(f32[3,1,32,128]{3,2,0,1:T(8,128)} %slice.1640), channel_id=1, source_target_pairs={{0,12},{12,24},{24,36},{36,48},{48,60},{60,72},{72,84},{84,96},{96... | collective-permute-start | bytes 147464 | tf_op jit(solution)/shard_map/ppermute | solution.py:21
  146.6 4.4 %collective-permute-done.17 = f32[3,1,32,128]{3,2,0,1:T(8,128)} collective-permute-done((f32[3,1,32,128]{3,2,0,1:T(8,128)}, f32[3,1,32,128]{3,2,0,1:T(8,128)}, u32[]{:S(2)}, u32[]{:S(2)}) %collective-permute-start.17) | collective-permute-done | bytes 49184 | tf_op jit(solution)/shard_map/ppermute | solution.py:24
  155.2 3.1 %collective-permute-done.19 = f32[3,4,1,128]{3,2,1,0:T(1,128)S(1)} collective-permute-done((f32[3,4,1,128]{3,2,1,0:T(1,128)S(1)}, f32[3,4,1,128]{3,2,1,0:T(1,128)S(1)}, u32[]{:S(2)}, u32[]{:S(2)}) %collective-permute-start.19) | collective-permute-done | bytes 6176 | tf_op jit(solution)/shard_map/ppermute | solution.py:24
  160.3 3.7 %collective-permute-start.20 = (f32[3,1,32,128]{3,2,1,0:T(8,128)S(1)}, f32[3,1,32,128]{3,2,1,0:T(8,128)S(1)}, u32[]{:S(2)}, u32[]{:S(2)}) collective-permute-start(f32[3,1,32,128]{3,2,1,0:T(8,128)S(1)} %get-tuple-element.115), channel_id=1, source_target_pairs={{0,12},{12,24},{24,36},{36,48},{48,60},{60,72},{72,84},{84,96},{96... | collective-permute-start | bytes 147464 | tf_op jit(solution)/shard_map/ppermute | solution.py:21
  166.0 6.8 %collective-permute-done.21 = f32[3,1,32,128]{3,2,1,0:T(8,128)S(1)} collective-permute-done((f32[3,1,32,128]{3,2,1,0:T(8,128)S(1)}, f32[3,1,32,128]{3,2,1,0:T(8,128)S(1)}, u32[]{:S(2)}, u32[]{:S(2)}) %collective-permute-start.21) | collective-permute-done | bytes 49184 | tf_op jit(solution)/shard_map/ppermute | solution.py:24
  172.8 3.6 %collective-permute-start.22 = (f32[3,4,1,128]{3,2,1,0:T(1,128)S(1)}, f32[3,4,1,128]{3,2,1,0:T(1,128)S(1)}, u32[]{:S(2)}, u32[]{:S(2)}) collective-permute-start(f32[3,4,1,128]{3,2,1,0:T(1,128)S(1)} %get-tuple-element.97), channel_id=1, source_target_pairs={{0,1},{1,2},{2,3},{3,4},{4,5},{5,6},{6,7},{7,8},{8,9},{9,10},{10,1... | collective-permute-start | bytes 18440 | tf_op jit(solution)/shard_map/ppermute | solution.py:21
  177.8 3.8 %collective-permute-done.23 = f32[3,4,1,128]{3,2,1,0:T(1,128)S(1)} collective-permute-done((f32[3,4,1,128]{3,2,1,0:T(1,128)S(1)}, f32[3,4,1,128]{3,2,1,0:T(1,128)S(1)}, u32[]{:S(2)}, u32[]{:S(2)}) %collective-permute-start.23) | collective-permute-done | bytes 6176 | tf_op jit(solution)/shard_map/ppermute | solution.py:24
  182.4 3.0 %collective-permute-start.24 = (f32[3,1,32,128]{3,2,1,0:T(8,128)S(1)}, f32[3,1,32,128]{3,2,1,0:T(8,128)S(1)}, u32[]{:S(2)}, u32[]{:S(2)}) collective-permute-start(f32[3,1,32,128]{3,2,1,0:T(8,128)S(1)} %get-tuple-element.113), channel_id=1, source_target_pairs={{0,12},{12,24},{24,36},{36,48},{48,60},{60,72},{72,84},{84,96},{96... | collective-permute-start | bytes 147464 | tf_op jit(solution)/shard_map/ppermute | solution.py:21
  187.4 6.8 %collective-permute-done.25 = f32[3,1,32,128]{3,2,1,0:T(8,128)S(1)} collective-permute-done((f32[3,1,32,128]{3,2,1,0:T(8,128)S(1)}, f32[3,1,32,128]{3,2,1,0:T(8,128)S(1)}, u32[]{:S(2)}, u32[]{:S(2)}) %collective-permute-start.25) | collective-permute-done | bytes 49184 | tf_op jit(solution)/shard_map/ppermute | solution.py:24
  194.2 4.8 %collective-permute-start.26 = (f32[3,4,1,128]{3,2,1,0:T(1,128)S(1)}, f32[3,4,1,128]{3,2,1,0:T(1,128)S(1)}, u32[]{:S(2)}, u32[]{:S(2)}) collective-permute-start(f32[3,4,1,128]{3,2,1,0:T(1,128)S(1)} %get-tuple-element.95), channel_id=1, source_target_pairs={{0,1},{1,2},{2,3},{3,4},{4,5},{5,6},{6,7},{7,8},{8,9},{9,10},{10,1... | collective-permute-start | bytes 18440 | tf_op jit(solution)/shard_map/ppermute | solution.py:21
  200.4 3.3 %collective-permute-done.27 = f32[3,4,1,128]{3,2,1,0:T(1,128)S(1)} collective-permute-done((f32[3,4,1,128]{3,2,1,0:T(1,128)S(1)}, f32[3,4,1,128]{3,2,1,0:T(1,128)S(1)}, u32[]{:S(2)}, u32[]{:S(2)}) %collective-permute-start.27) | collective-permute-done | bytes 6176 | tf_op jit(solution)/shard_map/ppermute | solution.py:24
  205.7 3.0 %collective-permute-start.28 = (f32[3,1,32,128]{3,2,1,0:T(8,128)S(1)}, f32[3,1,32,128]{3,2,1,0:T(8,128)S(1)}, u32[]{:S(2)}, u32[]{:S(2)}) collective-permute-start(f32[3,1,32,128]{3,2,1,0:T(8,128)S(1)} %get-tuple-element.111), channel_id=1, source_target_pairs={{0,12},{12,24},{24,36},{36,48},{48,60},{60,72},{72,84},{84,96},{96... | collective-permute-start | bytes 147464 | tf_op jit(solution)/shard_map/ppermute | solution.py:21
  210.6 6.8 %collective-permute-done.29 = f32[3,1,32,128]{3,2,1,0:T(8,128)S(1)} collective-permute-done((f32[3,1,32,128]{3,2,1,0:T(8,128)S(1)}, f32[3,1,32,128]{3,2,1,0:T(8,128)S(1)}, u32[]{:S(2)}, u32[]{:S(2)}) %collective-permute-start.29) | collective-permute-done | bytes 49184 | tf_op jit(solution)/shard_map/ppermute | solution.py:24
  217.4 3.6 %collective-permute-start.30 = (f32[3,4,1,128]{3,2,1,0:T(1,128)S(1)}, f32[3,4,1,128]{3,2,1,0:T(1,128)S(1)}, u32[]{:S(2)}, u32[]{:S(2)}) collective-permute-start(f32[3,4,1,128]{3,2,1,0:T(1,128)S(1)} %get-tuple-element.93), channel_id=1, source_target_pairs={{0,1},{1,2},{2,3},{3,4},{4,5},{5,6},{6,7},{7,8},{8,9},{9,10},{10,1... | collective-permute-start | bytes 18440 | tf_op jit(solution)/shard_map/ppermute | solution.py:21
  222.4 3.1 %collective-permute-done.31 = f32[3,4,1,128]{3,2,1,0:T(1,128)S(1)} collective-permute-done((f32[3,4,1,128]{3,2,1,0:T(1,128)S(1)}, f32[3,4,1,128]{3,2,1,0:T(1,128)S(1)}, u32[]{:S(2)}, u32[]{:S(2)}) %collective-permute-start.31) | collective-permute-done | bytes 6176 | tf_op jit(solution)/shard_map/ppermute | solution.py:24
  (213 shorter events, 64.7 us)
Async XLA Ops:
  1.5 6.8 %collective-permute-start = (f32[2,1,32,128]{3,2,1,0:T(8,128)S(1)}, f32[2,1,32,128]{3,2,1,0:T(8,128)S(1)}, u32[]{:S(2)}, u32[]{:S(2)}) collective-permute-start(f32[2,1,32,128]{3,2,1,0:T(8,128)S(1)} %get-tuple-element.123), channel_id=1, source_target_pairs={{0,12},{12,24},{24,36},{36,48},{48,60},{60,72},{72,84},{84,96},{96... | collective-permute-start | bytes 98312 | tf_op jit(solution)/shard_map/ppermute | solution.py:21
  6.4 8.6 %collective-permute-start.1 = (f32[2,1,32,128]{3,2,1,0:T(8,128)S(1)}, f32[2,1,32,128]{3,2,1,0:T(8,128)S(1)}, u32[]{:S(2)}, u32[]{:S(2)}) collective-permute-start(f32[2,1,32,128]{3,2,1,0:T(8,128)S(1)} %get-tuple-element.124), channel_id=1, source_target_pairs={{12,0},{24,12},{36,24},{48,36},{60,48},{72,60},{84,72},{96,84},{10... | collective-permute-start | bytes 98312 | tf_op jit(solution)/shard_map/ppermute | solution.py:24
  15.7 5.3 %collective-permute-start.2 = (f32[2,4,1,128]{3,2,1,0:T(1,128)S(1)}, f32[2,4,1,128]{3,2,1,0:T(1,128)S(1)}, u32[]{:S(2)}, u32[]{:S(2)}) collective-permute-start(f32[2,4,1,128]{3,2,1,0:T(1,128)S(1)} %get-tuple-element.109), channel_id=1, source_target_pairs={{0,1},{1,2},{2,3},{3,4},{4,5},{5,6},{6,7},{7,8},{8,9},{9,10},{10,1... | collective-permute-start | bytes 12296 | tf_op jit(solution)/shard_map/ppermute | solution.py:21
  19.7 5.0 %collective-permute-start.3 = (f32[2,4,1,128]{3,2,1,0:T(1,128)S(1)}, f32[2,4,1,128]{3,2,1,0:T(1,128)S(1)}, u32[]{:S(2)}, u32[]{:S(2)}) collective-permute-start(f32[2,4,1,128]{3,2,1,0:T(1,128)S(1)} %get-tuple-element.110), channel_id=1, source_target_pairs={{1,0},{2,1},{3,2},{4,3},{5,4},{6,5},{7,6},{8,7},{9,8},{10,9},{11,1... | collective-permute-start | bytes 12296 | tf_op jit(solution)/shard_map/ppermute | solution.py:24
  25.9 7.5 %collective-permute-start.4 = (f32[3,1,32,128]{3,2,1,0:T(8,128)S(1)}, f32[3,1,32,128]{3,2,1,0:T(8,128)S(1)}, u32[]{:S(2)}, u32[]{:S(2)}) collective-permute-start(f32[3,1,32,128]{3,2,1,0:T(8,128)S(1)} %get-tuple-element.121), channel_id=1, source_target_pairs={{0,12},{12,24},{24,36},{36,48},{48,60},{60,72},{72,84},{84,96},{96... | collective-permute-start | bytes 147464 | tf_op jit(solution)/shard_map/ppermute | solution.py:21
  29.0 8.7 %collective-permute-start.5 = (f32[3,1,32,128]{3,2,1,0:T(8,128)S(1)}, f32[3,1,32,128]{3,2,1,0:T(8,128)S(1)}, u32[]{:S(2)}, u32[]{:S(2)}) collective-permute-start(f32[3,1,32,128]{3,2,1,0:T(8,128)S(1)} %get-tuple-element.122), channel_id=1, source_target_pairs={{12,0},{24,12},{36,24},{48,36},{60,48},{72,60},{84,72},{96,84},{10... | collective-permute-start | bytes 147464 | tf_op jit(solution)/shard_map/ppermute | solution.py:24
  37.8 5.3 %collective-permute-start.6 = (f32[3,4,1,128]{3,2,1,0:T(1,128)S(1)}, f32[3,4,1,128]{3,2,1,0:T(1,128)S(1)}, u32[]{:S(2)}, u32[]{:S(2)}) collective-permute-start(f32[3,4,1,128]{3,2,1,0:T(1,128)S(1)} %get-tuple-element.105), channel_id=1, source_target_pairs={{0,1},{1,2},{2,3},{3,4},{4,5},{5,6},{6,7},{7,8},{8,9},{9,10},{10,1... | collective-permute-start | bytes 18440 | tf_op jit(solution)/shard_map/ppermute | solution.py:21
  41.8 6.2 %collective-permute-start.7 = (f32[3,4,1,128]{3,2,1,0:T(1,128)S(1)}, f32[3,4,1,128]{3,2,1,0:T(1,128)S(1)}, u32[]{:S(2)}, u32[]{:S(2)}) collective-permute-start(f32[3,4,1,128]{3,2,1,0:T(1,128)S(1)} %get-tuple-element.106), channel_id=1, source_target_pairs={{1,0},{2,1},{3,2},{4,3},{5,4},{6,5},{7,6},{8,7},{9,8},{10,9},{11,1... | collective-permute-start | bytes 18440 | tf_op jit(solution)/shard_map/ppermute | solution.py:24
  48.9 5.9 %collective-permute-start.8 = (f32[3,1,32,128]{3,2,1,0:T(8,128)S(1)}, f32[3,1,32,128]{3,2,1,0:T(8,128)S(1)}, u32[]{:S(2)}, u32[]{:S(2)}) collective-permute-start(f32[3,1,32,128]{3,2,1,0:T(8,128)S(1)} %get-tuple-element.119), channel_id=1, source_target_pairs={{0,12},{12,24},{24,36},{36,48},{48,60},{60,72},{72,84},{84,96},{96... | collective-permute-start | bytes 147464 | tf_op jit(solution)/shard_map/ppermute | solution.py:21
  52.7 8.7 %collective-permute-start.9 = (f32[3,1,32,128]{3,2,1,0:T(8,128)S(1)}, f32[3,1,32,128]{3,2,1,0:T(8,128)S(1)}, u32[]{:S(2)}, u32[]{:S(2)}) collective-permute-start(f32[3,1,32,128]{3,2,1,0:T(8,128)S(1)} %get-tuple-element.120), channel_id=1, source_target_pairs={{12,0},{24,12},{36,24},{48,36},{60,48},{72,60},{84,72},{96,84},{10... | collective-permute-start | bytes 147464 | tf_op jit(solution)/shard_map/ppermute | solution.py:24
  61.5 6.9 %collective-permute-start.10 = (f32[3,4,1,128]{3,2,1,0:T(1,128)S(1)}, f32[3,4,1,128]{3,2,1,0:T(1,128)S(1)}, u32[]{:S(2)}, u32[]{:S(2)}) collective-permute-start(f32[3,4,1,128]{3,2,1,0:T(1,128)S(1)} %get-tuple-element.103), channel_id=1, source_target_pairs={{0,1},{1,2},{2,3},{3,4},{4,5},{5,6},{6,7},{7,8},{8,9},{9,10},{10,1... | collective-permute-start | bytes 18440 | tf_op jit(solution)/shard_map/ppermute | solution.py:21
  66.3 4.7 %collective-permute-start.11 = (f32[3,4,1,128]{3,2,1,0:T(1,128)S(1)}, f32[3,4,1,128]{3,2,1,0:T(1,128)S(1)}, u32[]{:S(2)}, u32[]{:S(2)}) collective-permute-start(f32[3,4,1,128]{3,2,1,0:T(1,128)S(1)} %get-tuple-element.104), channel_id=1, source_target_pairs={{1,0},{2,1},{3,2},{4,3},{5,4},{6,5},{7,6},{8,7},{9,8},{10,9},{11,1... | collective-permute-start | bytes 18440 | tf_op jit(solution)/shard_map/ppermute | solution.py:24
  72.0 6.7 %collective-permute-start.12 = (f32[3,1,32,128]{3,2,1,0:T(8,128)S(1)}, f32[3,1,32,128]{3,2,1,0:T(8,128)S(1)}, u32[]{:S(2)}, u32[]{:S(2)}) collective-permute-start(f32[3,1,32,128]{3,2,1,0:T(8,128)S(1)} %get-tuple-element.117), channel_id=1, source_target_pairs={{0,12},{12,24},{24,36},{36,48},{48,60},{60,72},{72,84},{84,96},{96... | collective-permute-start | bytes 147464 | tf_op jit(solution)/shard_map/ppermute | solution.py:21
  75.0 8.7 %collective-permute-start.13 = (f32[3,1,32,128]{3,2,1,0:T(8,128)S(1)}, f32[3,1,32,128]{3,2,1,0:T(8,128)S(1)}, u32[]{:S(2)}, u32[]{:S(2)}) collective-permute-start(f32[3,1,32,128]{3,2,1,0:T(8,128)S(1)} %get-tuple-element.118), channel_id=1, source_target_pairs={{12,0},{24,12},{36,24},{48,36},{60,48},{72,60},{84,72},{96,84},{10... | collective-permute-start | bytes 147464 | tf_op jit(solution)/shard_map/ppermute | solution.py:24
  83.8 7.0 %collective-permute-start.14 = (f32[3,4,1,128]{3,2,1,0:T(1,128)S(1)}, f32[3,4,1,128]{3,2,1,0:T(1,128)S(1)}, u32[]{:S(2)}, u32[]{:S(2)}) collective-permute-start(f32[3,4,1,128]{3,2,1,0:T(1,128)S(1)} %get-tuple-element.101), channel_id=1, source_target_pairs={{0,1},{1,2},{2,3},{3,4},{4,5},{5,6},{6,7},{7,8},{8,9},{9,10},{10,1... | collective-permute-start | bytes 18440 | tf_op jit(solution)/shard_map/ppermute | solution.py:21
  88.1 4.7 %collective-permute-start.15 = (f32[3,4,1,128]{3,2,1,0:T(1,128)S(1)}, f32[3,4,1,128]{3,2,1,0:T(1,128)S(1)}, u32[]{:S(2)}, u32[]{:S(2)}) collective-permute-start(f32[3,4,1,128]{3,2,1,0:T(1,128)S(1)} %get-tuple-element.102), channel_id=1, source_target_pairs={{1,0},{2,1},{3,2},{4,3},{5,4},{6,5},{7,6},{8,7},{9,8},{10,9},{11,1... | collective-permute-start | bytes 18440 | tf_op jit(solution)/shard_map/ppermute | solution.py:24
  133.8 12.8 %collective-permute-start.16 = (f32[3,1,32,128]{3,2,0,1:T(8,128)}, f32[3,1,32,128]{3,2,0,1:T(8,128)}, u32[]{:S(2)}, u32[]{:S(2)}) collective-permute-start(f32[3,1,32,128]{3,2,0,1:T(8,128)} %slice.1640), channel_id=1, source_target_pairs={{0,12},{12,24},{24,36},{36,48},{48,60},{60,72},{72,84},{84,96},{96... | collective-permute-start | bytes 147464 | tf_op jit(solution)/shard_map/ppermute | solution.py:21
  142.0 9.0 %collective-permute-start.17 = (f32[3,1,32,128]{3,2,0,1:T(8,128)}, f32[3,1,32,128]{3,2,0,1:T(8,128)}, u32[]{:S(2)}, u32[]{:S(2)}) collective-permute-start(f32[3,1,32,128]{3,2,0,1:T(8,128)} %slice.1640), channel_id=1, source_target_pairs={{12,0},{24,12},{36,24},{48,36},{60,48},{72,60},{84,72},{96,84},{10... | collective-permute-start | bytes 147464 | tf_op jit(solution)/shard_map/ppermute | solution.py:24
  152.6 2.6 %collective-permute-start.18 = (f32[3,4,1,128]{3,2,1,0:T(1,128)S(1)}, f32[3,4,1,128]{3,2,1,0:T(1,128)S(1)}, u32[]{:S(2)}, u32[]{:S(2)}) collective-permute-start(f32[3,4,1,128]{3,2,1,0:T(1,128)S(1)} %get-tuple-element.99), channel_id=1, source_target_pairs={{0,1},{1,2},{2,3},{3,4},{4,5},{5,6},{6,7},{7,8},{8,9},{9,10},{10,1... | collective-permute-start | bytes 18440 | tf_op jit(solution)/shard_map/ppermute | solution.py:21
  153.9 4.4 %collective-permute-start.19 = (f32[3,4,1,128]{3,2,1,0:T(1,128)S(1)}, f32[3,4,1,128]{3,2,1,0:T(1,128)S(1)}, u32[]{:S(2)}, u32[]{:S(2)}) collective-permute-start(f32[3,4,1,128]{3,2,1,0:T(1,128)S(1)} %get-tuple-element.100), channel_id=1, source_target_pairs={{1,0},{2,1},{3,2},{4,3},{5,4},{6,5},{7,6},{8,7},{9,8},{10,9},{11,1... | collective-permute-start | bytes 18440 | tf_op jit(solution)/shard_map/ppermute | solution.py:24
  160.3 5.7 %collective-permute-start.20 = (f32[3,1,32,128]{3,2,1,0:T(8,128)S(1)}, f32[3,1,32,128]{3,2,1,0:T(8,128)S(1)}, u32[]{:S(2)}, u32[]{:S(2)}) collective-permute-start(f32[3,1,32,128]{3,2,1,0:T(8,128)S(1)} %get-tuple-element.115), channel_id=1, source_target_pairs={{0,12},{12,24},{24,36},{36,48},{48,60},{60,72},{72,84},{84,96},{96... | collective-permute-start | bytes 147464 | tf_op jit(solution)/shard_map/ppermute | solution.py:21
  164.1 8.7 %collective-permute-start.21 = (f32[3,1,32,128]{3,2,1,0:T(8,128)S(1)}, f32[3,1,32,128]{3,2,1,0:T(8,128)S(1)}, u32[]{:S(2)}, u32[]{:S(2)}) collective-permute-start(f32[3,1,32,128]{3,2,1,0:T(8,128)S(1)} %get-tuple-element.116), channel_id=1, source_target_pairs={{12,0},{24,12},{36,24},{48,36},{60,48},{72,60},{84,72},{96,84},{10... | collective-permute-start | bytes 147464 | tf_op jit(solution)/shard_map/ppermute | solution.py:24
  172.8 4.9 %collective-permute-start.22 = (f32[3,4,1,128]{3,2,1,0:T(1,128)S(1)}, f32[3,4,1,128]{3,2,1,0:T(1,128)S(1)}, u32[]{:S(2)}, u32[]{:S(2)}) collective-permute-start(f32[3,4,1,128]{3,2,1,0:T(1,128)S(1)} %get-tuple-element.97), channel_id=1, source_target_pairs={{0,1},{1,2},{2,3},{3,4},{4,5},{5,6},{6,7},{7,8},{8,9},{9,10},{10,1... | collective-permute-start | bytes 18440 | tf_op jit(solution)/shard_map/ppermute | solution.py:21
  176.4 5.1 %collective-permute-start.23 = (f32[3,4,1,128]{3,2,1,0:T(1,128)S(1)}, f32[3,4,1,128]{3,2,1,0:T(1,128)S(1)}, u32[]{:S(2)}, u32[]{:S(2)}) collective-permute-start(f32[3,4,1,128]{3,2,1,0:T(1,128)S(1)} %get-tuple-element.98), channel_id=1, source_target_pairs={{1,0},{2,1},{3,2},{4,3},{5,4},{6,5},{7,6},{8,7},{9,8},{10,9},{11,1... | collective-permute-start | bytes 18440 | tf_op jit(solution)/shard_map/ppermute | solution.py:24
  182.4 5.0 %collective-permute-start.24 = (f32[3,1,32,128]{3,2,1,0:T(8,128)S(1)}, f32[3,1,32,128]{3,2,1,0:T(8,128)S(1)}, u32[]{:S(2)}, u32[]{:S(2)}) collective-permute-start(f32[3,1,32,128]{3,2,1,0:T(8,128)S(1)} %get-tuple-element.113), channel_id=1, source_target_pairs={{0,12},{12,24},{24,36},{36,48},{48,60},{60,72},{72,84},{84,96},{96... | collective-permute-start | bytes 147464 | tf_op jit(solution)/shard_map/ppermute | solution.py:21
  185.4 8.7 %collective-permute-start.25 = (f32[3,1,32,128]{3,2,1,0:T(8,128)S(1)}, f32[3,1,32,128]{3,2,1,0:T(8,128)S(1)}, u32[]{:S(2)}, u32[]{:S(2)}) collective-permute-start(f32[3,1,32,128]{3,2,1,0:T(8,128)S(1)} %get-tuple-element.114), channel_id=1, source_target_pairs={{12,0},{24,12},{36,24},{48,36},{60,48},{72,60},{84,72},{96,84},{10... | collective-permute-start | bytes 147464 | tf_op jit(solution)/shard_map/ppermute | solution.py:24
  194.2 6.2 %collective-permute-start.26 = (f32[3,4,1,128]{3,2,1,0:T(1,128)S(1)}, f32[3,4,1,128]{3,2,1,0:T(1,128)S(1)}, u32[]{:S(2)}, u32[]{:S(2)}) collective-permute-start(f32[3,4,1,128]{3,2,1,0:T(1,128)S(1)} %get-tuple-element.95), channel_id=1, source_target_pairs={{0,1},{1,2},{2,3},{3,4},{4,5},{5,6},{6,7},{7,8},{8,9},{9,10},{10,1... | collective-permute-start | bytes 18440 | tf_op jit(solution)/shard_map/ppermute | solution.py:21
  199.0 4.7 %collective-permute-start.27 = (f32[3,4,1,128]{3,2,1,0:T(1,128)S(1)}, f32[3,4,1,128]{3,2,1,0:T(1,128)S(1)}, u32[]{:S(2)}, u32[]{:S(2)}) collective-permute-start(f32[3,4,1,128]{3,2,1,0:T(1,128)S(1)} %get-tuple-element.96), channel_id=1, source_target_pairs={{1,0},{2,1},{3,2},{4,3},{5,4},{6,5},{7,6},{8,7},{9,8},{10,9},{11,1... | collective-permute-start | bytes 18440 | tf_op jit(solution)/shard_map/ppermute | solution.py:24
  205.7 5.0 %collective-permute-start.28 = (f32[3,1,32,128]{3,2,1,0:T(8,128)S(1)}, f32[3,1,32,128]{3,2,1,0:T(8,128)S(1)}, u32[]{:S(2)}, u32[]{:S(2)}) collective-permute-start(f32[3,1,32,128]{3,2,1,0:T(8,128)S(1)} %get-tuple-element.111), channel_id=1, source_target_pairs={{0,12},{12,24},{24,36},{36,48},{48,60},{60,72},{72,84},{84,96},{96... | collective-permute-start | bytes 147464 | tf_op jit(solution)/shard_map/ppermute | solution.py:21
  208.7 8.7 %collective-permute-start.29 = (f32[3,1,32,128]{3,2,1,0:T(8,128)S(1)}, f32[3,1,32,128]{3,2,1,0:T(8,128)S(1)}, u32[]{:S(2)}, u32[]{:S(2)}) collective-permute-start(f32[3,1,32,128]{3,2,1,0:T(8,128)S(1)} %get-tuple-element.112), channel_id=1, source_target_pairs={{12,0},{24,12},{36,24},{48,36},{60,48},{72,60},{84,72},{96,84},{10... | collective-permute-start | bytes 147464 | tf_op jit(solution)/shard_map/ppermute | solution.py:24
  217.4 4.9 %collective-permute-start.30 = (f32[3,4,1,128]{3,2,1,0:T(1,128)S(1)}, f32[3,4,1,128]{3,2,1,0:T(1,128)S(1)}, u32[]{:S(2)}, u32[]{:S(2)}) collective-permute-start(f32[3,4,1,128]{3,2,1,0:T(1,128)S(1)} %get-tuple-element.93), channel_id=1, source_target_pairs={{0,1},{1,2},{2,3},{3,4},{4,5},{5,6},{6,7},{7,8},{8,9},{9,10},{10,1... | collective-permute-start | bytes 18440 | tf_op jit(solution)/shard_map/ppermute | solution.py:21
  221.1 4.4 %collective-permute-start.31 = (f32[3,4,1,128]{3,2,1,0:T(1,128)S(1)}, f32[3,4,1,128]{3,2,1,0:T(1,128)S(1)}, u32[]{:S(2)}, u32[]{:S(2)}) collective-permute-start(f32[3,4,1,128]{3,2,1,0:T(1,128)S(1)} %get-tuple-element.94), channel_id=1, source_target_pairs={{1,0},{2,1},{3,2},{4,3},{5,4},{6,5},{7,6},{8,7},{9,8},{10,9},{11,1... | collective-permute-start | bytes 18440 | tf_op jit(solution)/shard_map/ppermute | solution.py:24
  (29 other events, 311.3 us)
where the time goes:
time: 228 us; the launch traced here: 227 us
  starting transfers between devices  89.1 us (39%)
  waiting for transfers between devices  74 us (32%)
  other arithmetic  24.1 us (11%)
  blocking collectives  21.6 us (9%)
  local copies, waits for them, and re-layouts  15.6 us (7%)
  between operations  2.61 us (1%)
    ppermute x16, waiting for transfers between devices, padded_2(): lax.ppermute(lax.slice_in_dim(block, 0, width, axis=dim), axis, backward)  73.9 us
    ppermute x16, starting transfers between devices, padded_2(): lax.ppermute(lax.slice_in_dim(block, block.shape[dim] - width, None, axis...  63.4 us
    ppermute x16, starting transfers between devices, padded_2(): lax.ppermute(lax.slice_in_dim(block, 0, width, axis=dim), axis, backward)  25.7 us
    all_gather x1, blocking collectives, shards(): column = lax.all_gather(packed, 'gy', axis=1, tiled=True)  21.6 us
    another operation x30, other arithmetic, operate(): return jnp.stack(results)  6.69 us
  transfers between devices with their start and end apart: 32, of which 16 were waited for; matrix products, arithmetic and copies ran while one was open for 4% of the time, Pallas kernels for 0%

commit v1 on v0

--- a/solution.py
+++ b/solution.py
@@ -11,19 +11,6 @@
 HIGH_BOUND = 6.0
 SHIFT_SCALE = 48.0
 UNITS = ((1, 0, 0), (0, 1, 0), (0, 0, 1))
-
-
-def padded_2(block, sides, width):
-    for axis, dim in sides:
-        count = lax.axis_size(axis)
-        forward = [(i, i + 1) for i in range(count - 1)]
-        backward = [(target, source) for source, target in forward]
-        low = lax.ppermute(
-            lax.slice_in_dim(block, block.shape[dim] - width, None, axis=dim), axis, forward
-        )
-        high = lax.ppermute(lax.slice_in_dim(block, 0, width, axis=dim), axis, backward)
-        block = jnp.concatenate([low, block, high], axis=dim)
-    return block
 
 
 def shifted(array, step_x, step_y, step_z):
@@ -139,57 +126,259 @@
     return jnp.where(labels[..., :, None] == labels[..., None, :], 1.0, 0.0).astype(jnp.float32)
 
 
+def crop(array, cut):
+    if cut == 0:
+        return array
+    return array[..., cut:-cut, cut:-cut, :]
+
+
+def shifted_ext(array, step_x, step_y, step_z):
+    size_x = array.shape[-3] - 2
+    size_y = array.shape[-2] - 2
+    inner = array[..., 1 + step_x : 1 + step_x + size_x, 1 + step_y : 1 + step_y + size_y, :]
+    if step_z == 0:
+        return inner
+    zero = jnp.zeros_like(inner[..., :1])
+    if step_z > 0:
+        return jnp.concatenate([inner[..., 1:], zero], axis=-1)
+    return jnp.concatenate([zero, inner[..., :-1]], axis=-1)
+
+
+def diagonal_ext(mu_pad, lam_pad, scale):
+    mu_centre = shifted_ext(mu_pad, 0, 0, 0)
+    lam_centre = shifted_ext(lam_pad, 0, 0, 0)
+    faces = 0.0
+    for unit in UNITS:
+        backward = tuple((-value for value in unit))
+        faces = (
+            faces
+            + 0.5 * (mu_centre + shifted_ext(mu_pad, *unit))
+            + 0.5 * (mu_centre + shifted_ext(mu_pad, *backward))
+        )
+    results = []
+    for unit in UNITS:
+        backward = tuple((-value for value in unit))
+        results.append(scale * (faces + lam_centre + shifted_ext(lam_pad, *backward)))
+    return jnp.stack(results)
+
+
+def apply_ext(field_pad, mu_pad, lam_pad, scale):
+    mu_centre = shifted_ext(mu_pad, 0, 0, 0)
+    lam_centre = shifted_ext(lam_pad, 0, 0, 0)
+    components = [field_pad[0], field_pad[1], field_pad[2]]
+    centres = [shifted_ext(value, 0, 0, 0) for value in components]
+    laplace = [0.0, 0.0, 0.0]
+    for unit in UNITS:
+        backward = tuple((-value for value in unit))
+        face_up = 0.5 * (mu_centre + shifted_ext(mu_pad, *unit))
+        face_down = 0.5 * (mu_centre + shifted_ext(mu_pad, *backward))
+        for comp_id in range(3):
+            laplace[comp_id] = (
+                laplace[comp_id]
+                + face_up * (shifted_ext(components[comp_id], *unit) - centres[comp_id])
+                - face_down * (centres[comp_id] - shifted_ext(components[comp_id], *backward))
+            )
+
+    def spread(offset):
+        total = 0.0
+        for comp_id in range(3):
+            ahead = tuple((offset[axis_id] + UNITS[comp_id][axis_id] for axis_id in range(3)))
+            total = total + (
+                shifted_ext(components[comp_id], *ahead)
+                - shifted_ext(components[comp_id], *offset)
+            )
+        return total
+
+    stress_here = lam_centre * spread((0, 0, 0))
+    results = []
+    for comp_id in range(3):
+        backward = tuple((-value for value in UNITS[comp_id]))
+        grad_term = stress_here - shifted_ext(lam_pad, *backward) * spread(backward)
+        results.append(scale * (-laplace[comp_id] - grad_term))
+    return jnp.stack(results)
+
+
+def halo_x(parts):
+    count = lax.axis_size("gx")
+    reach = max((d + a.shape[-3] - 1) // a.shape[-3] for a, d in parts)
+    lows = [[] for _ in parts]
+    highs = [[] for _ in parts]
+    for dx in range(reach, 0, -1):
+        send_low, send_high, keys = [], [], []
+        for index, (array, d) in enumerate(parts):
+            width = array.shape[-3]
+            need = min(width, d - (dx - 1) * width)
+            if need <= 0:
+                continue
+            keys.append((index, array.shape[:-3] + (need,) + array.shape[-2:]))
+            send_low.append(array[..., width - need :, :, :].reshape(-1))
+            send_high.append(array[..., :need, :, :].reshape(-1))
+        forward = [(i, i + dx) for i in range(count - dx)]
+        backward = [(i + dx, i) for i in range(count - dx)]
+        got_low = lax.ppermute(jnp.concatenate(send_low), "gx", forward)
+        got_high = lax.ppermute(jnp.concatenate(send_high), "gx", backward)
+        offset = 0
+        for index, shape in keys:
+            size = 1
+            for value in shape:
+                size *= value
+            lows[index].append(got_low[offset : offset + size].reshape(shape))
+            highs[index].append(got_high[offset : offset + size].reshape(shape))
+            offset += size
+    out = []
+    for index, (array, d) in enumerate(parts):
+        out.append(jnp.concatenate(lows[index] + [array] + highs[index][::-1], axis=-3))
+    return out
+
+
+def halo_y(array, depth):
+    count = lax.axis_size("gy")
+    forward = [(i, i + 1) for i in range(count - 1)]
+    backward = [(i + 1, i) for i in range(count - 1)]
+    low = lax.ppermute(array[..., -depth:, :], "gy", forward)
+    high = lax.ppermute(array[..., :depth, :], "gy", backward)
+    return jnp.concatenate([low, array, high], axis=-2)
+
+
+def inside_mask(width_x, width_y, depth):
+    gx = lax.axis_index("gx")
+    gy = lax.axis_index("gy")
+    total_x = width_x * lax.axis_size("gx")
+    total_y = width_y * lax.axis_size("gy")
+    xs = gx * width_x + jnp.arange(width_x + 2 * depth) - depth
+    ys = gy * width_y + jnp.arange(width_y + 2 * depth) - depth
+    ok_x = (xs >= 0) & (xs < total_x)
+    ok_y = (ys >= 0) & (ys < total_y)
+    return (ok_x[:, None] & ok_y[None, :])[:, :, None]
+
+
+def smooth_ext(solution, residual, inverse_diag, mu, lam, depth, steps):
+    midpoint = 0.5 * (HIGH_BOUND + LOW_BOUND)
+    halfwidth = 0.5 * (HIGH_BOUND - LOW_BOUND)
+    sharpness = midpoint / halfwidth
+    weight_old = 1.0 / sharpness
+    level = depth
+    direction = inverse_diag * residual / midpoint
+    solution = solution + crop(direction, level)
+    cut = depth + 1 - level
+    residual = crop(residual, 1) - apply_ext(direction, crop(mu, cut), crop(lam, cut), 1.0)
+    level -= 1
+    for step_id in range(steps - 1):
+        weight_new = 1.0 / (2.0 * sharpness - weight_old)
+        direction = weight_new * weight_old * crop(direction, 1) + 2.0 * weight_new / halfwidth * (
+            crop(inverse_diag, depth - level) * residual
+        )
+        solution = solution + crop(direction, level)
+        cut = depth + 1 - level
+        residual = crop(residual, 1) - apply_ext(direction, crop(mu, cut), crop(lam, cut), 1.0)
+        level -= 1
+        weight_old = weight_new
+    return (solution, residual)
+
+
+def pair_matrix(coarse_z):
+    fine = jnp.arange(2 * coarse_z) // 2
+    return (fine[None, :] == jnp.arange(coarse_z)[:, None]).astype(jnp.float32)
+
+
+def upsample_z(array, pairs):
+    return jnp.einsum("...k,kj->...j", array, pairs, precision=lax.Precision.HIGHEST)
+
+
+def restrict_z(array, pairs):
+    return jnp.einsum("...j,kj->...k", array, pairs, precision=lax.Precision.HIGHEST)
+
+
 def shards(rhs_field, shear_modulus, lame_lambda, group_start):
-    coefficients = jnp.stack([shear_modulus, lame_lambda])
-    padded = padded_2(coefficients, (("gx", 1), ("gy", 2)), 1)
-    padded = jnp.pad(padded, ((0, 0), (0, 0), (0, 0), (1, 1)))
-    mu_pad = padded[0]
-    lam_pad = padded[1]
-    inverse_diag = 1.0 / diagonal(mu_pad, lam_pad, 1.0)
-
-    def fine_apply(field):
-        extended = padded_2(field, (("gx", 1), ("gy", 2)), 1)
-        extended = jnp.pad(extended, ((0, 0), (0, 0), (0, 0), (1, 1)))
-        return operate(extended, mu_pad, lam_pad, 1.0)
-
-    solution, residual = smooth(
-        jnp.zeros_like(rhs_field), rhs_field, inverse_diag, fine_apply, SWEEPS
-    )
-    coarse_x = rhs_field.shape[1] // 2
-    coarse_y = rhs_field.shape[2] // 2
-    coarse_z = rhs_field.shape[3] // 2
-    coarse_res = residual.reshape(3, coarse_x, 2, coarse_y, 2, coarse_z, 2).sum(axis=(2, 4, 6))
-    coarse_mu = shear_modulus.reshape(coarse_x, 2, coarse_y, 2, coarse_z, 2).mean(axis=(1, 3, 5))
-    coarse_lam = lame_lambda.reshape(coarse_x, 2, coarse_y, 2, coarse_z, 2).mean(axis=(1, 3, 5))
+    width_x = rhs_field.shape[1]
+    width_y = rhs_field.shape[2]
+    width_z = rhs_field.shape[3]
+    depth = SWEEPS
+    gy = lax.axis_index("gy")
+    count_y = lax.axis_size("gy")
+
+    stacked = jnp.concatenate([rhs_field, shear_modulus[None], lame_lambda[None]], axis=0)
+    (stacked,) = halo_x([(stacked, depth + 1)])
+    stacked = halo_y(stacked, depth + 1)
+    mu_ext = stacked[3]
+    lam_ext = stacked[4]
+    rhs_ext = crop(stacked[0:3], 1)
+    inside = inside_mask(width_x, width_y, depth)
+    inverse_diag = jnp.where(inside[None], 1.0 / diagonal_ext(mu_ext, lam_ext, 1.0), 0.0)
+
+    solution, residual = smooth_ext(
+        jnp.zeros_like(rhs_field), rhs_ext, inverse_diag, mu_ext, lam_ext, depth, SWEEPS
+    )
+    coarse_x = width_x // 2
+    coarse_y = width_y // 2
+    coarse_z = width_z // 2
+    pairs = pair_matrix(coarse_z)
+    coarse_res = restrict_z(residual, pairs).reshape(3, coarse_x, 2, coarse_y, 2, coarse_z)
+    coarse_res = coarse_res.sum(axis=(2, 4))
+    coarse_coef = restrict_z(jnp.stack([shear_modulus, lame_lambda]), pairs)
+    coarse_coef = coarse_coef.reshape(2, coarse_x, 2, coarse_y, 2, coarse_z).sum(axis=(2, 4)) / 8.0
+    coarse_mu = coarse_coef[0]
+    coarse_lam = coarse_coef[1]
     starts = group_start[0]
-    position = lax.axis_index("gy")
     members = same_group(starts)
-    my_members = lax.dynamic_index_in_dim(members, position, 0, keepdims=False)
     cells_dev = coarse_x * coarse_y * coarse_z
-    group_cells = jnp.sum(my_members) * cells_dev
-    packed = jnp.concatenate([coarse_res, jnp.stack([coarse_mu, coarse_lam])], axis=0)[:, None]
-    column = lax.all_gather(packed, "gy", axis=1, tiled=True)
-    coef_pad = pad_groups(column[3:5], starts)
+
+    edge_low = residual[:, :, :depth, :]
+    edge_high = residual[:, :, -depth:, :]
+    coarse_pack = jnp.concatenate([coarse_res, coarse_mu[None], coarse_lam[None]], axis=0)
+    package = jnp.concatenate(
+        [coarse_pack.reshape(-1), edge_low.reshape(-1), edge_high.reshape(-1)]
+    )
+    column = lax.all_gather(package, "gy", axis=0, tiled=False)
+    coarse_size = coarse_pack.size
+    edge_size = edge_low.size
+    column_pack = column[:, :coarse_size].reshape((count_y,) + coarse_pack.shape)
+    column_pack = jnp.moveaxis(column_pack, 0, 1)
+    column_low = column[:, coarse_size : coarse_size + edge_size].reshape(
+        (count_y,) + edge_low.shape
+    )
+    column_high = column[:, coarse_size + edge_size :].reshape((count_y,) + edge_high.shape)
+    below = lax.dynamic_index_in_dim(column_high, jnp.maximum(gy - 1, 0), 0, keepdims=False)
+    above = lax.dynamic_index_in_dim(
+        column_low, jnp.minimum(gy + 1, count_y - 1), 0, keepdims=False
+    )
+    below = jnp.where(gy > 0, below, 0.0)
+    above = jnp.where(gy < count_y - 1, above, 0.0)
+    residual_y = jnp.concatenate([below, residual, above], axis=2)
+
+    coef_pad = pad_groups(column_pack[3:5], starts)
     coarse_inverse = 1.0 / diagonal(coef_pad[0], coef_pad[1], 4.0)
 
     def coarse_apply(field):
         return operate(pad_groups(field, starts), coef_pad[0], coef_pad[1], 4.0)
 
-    column_res = column[0:3]
+    column_res = column_pack[0:3]
     smoothed, coarse_left = smooth(
         jnp.zeros_like(column_res), column_res, coarse_inverse, coarse_apply, COARSE_SWEEPS
     )
-    mine = lax.dynamic_index_in_dim(smoothed, position, 1, keepdims=False)
     device_sums = column_res.sum(axis=(2, 3, 4))
-    totals = jnp.sum(device_sums * my_members[None, :], axis=1)
-    group_shift = totals / (SHIFT_SCALE * group_cells)
-    mine = mine + group_shift[:, None, None, None]
+    totals = jnp.sum(device_sums[:, None, :] * members[None, :, :], axis=2)
+    group_cells = jnp.sum(members, axis=1) * cells_dev
+    group_shift = totals / (SHIFT_SCALE * group_cells[None, :])
+    correction = smoothed + group_shift[:, :, None, None, None]
+    correction = jnp.moveaxis(correction, 1, 2).reshape(3, coarse_x, count_y * coarse_y, coarse_z)
+    reach_c = (depth + 2) // 2
+    correction = jnp.pad(correction, ((0, 0), (0, 0), (reach_c, reach_c), (0, 0)))
+    corr_y = lax.dynamic_slice_in_dim(correction, gy * coarse_y, coarse_y + 2 * reach_c, axis=2)
+
+    residual_ext, corr_ext = halo_x([(residual_y, depth), (corr_y, reach_c)])
+    corr_z = upsample_z(corr_ext, pairs)
     fine_corr = jnp.broadcast_to(
-        mine[:, :, None, :, None, :, None], (3, coarse_x, 2, coarse_y, 2, coarse_z, 2)
-    ).reshape(rhs_field.shape)
-    solution = solution + fine_corr
-    residual = residual - fine_apply(fine_corr)
-    solution, residual = smooth(solution, residual, inverse_diag, fine_apply, SWEEPS)
+        corr_z[:, :, None, :, None, :],
+        (3, corr_ext.shape[1], 2, corr_ext.shape[2], 2, width_z),
+    ).reshape(3, 2 * corr_ext.shape[1], 2 * corr_ext.shape[2], width_z)
+    fine_depth = 2 * reach_c
+    fine_corr = crop(fine_corr, fine_depth - (depth + 1))
+    solution = solution + crop(fine_corr, depth + 1)
+    residual_ext = residual_ext - apply_ext(fine_corr, mu_ext, lam_ext, 1.0)
+    solution, residual = smooth_ext(
+        solution, residual_ext, inverse_diag, mu_ext, lam_ext, depth, SWEEPS
+    )
     return (solution, residual)
 
 

time: 228 us -> 144 us (0.63)
  waiting for transfers between devices: 74 us -> 5.32 us
  starting transfers between devices: 89.1 us -> 41.3 us
  local copies, waits for them, and re-layouts: 15.6 us -> 37.9 us
  blocking collectives: 21.6 us -> 26.2 us
  other arithmetic: 24.1 us -> 28 us
  matrix products: 0 us -> 2.38 us
    ppermute x32 -> x10, waiting for transfers between devices: 74 us -> 5.32 us  [the longest x1 4.75 us: halo_y(): high = lax.ppermute(array[..., :depth, :], 'gy', backward)]
    ppermute x32 -> x10, starting transfers between devices: 89.1 us -> 41.3 us  [the longest x4 18.8 us: halo_x(): got_low = lax.ppermute(jnp.concatenate(send_low), 'gx', forward)]
    reshape x0 -> x18, local copies, waits for them, and re-layouts: none -> 11 us  [the longest x4 3.03 us: halo_x(): lows[index].append(got_low[offset:offset + size].reshape(shape))]
    unnamed x58 -> x89, local copies, waits for them, and re-layouts: 1.66 us -> 11.1 us
    slice x8 -> x41, local copies, waits for them, and re-layouts: 2.78 us -> 10.5 us  [the longest x4 3.66 us: halo_x(): highs[index].append(got_high[offset:offset + size].reshape(shape))]
    reduce_sum x3 -> x1, local copies, waits for them, and re-layouts: 5.89 us -> 0.78 us  [shards(): device_sums = column_res.sum(axis=(2, 3, 4))]
    all_gather x1, blocking collectives: 21.6 us -> 26.2 us  [shards(): column = lax.all_gather(package, 'gy', axis=0, tiled=False)]
    another operation x2 -> x24, other arithmetic: 0.99 us -> 5.29 us  [the longest x21 3.91 us: apply_ext(): return jnp.stack(results)]
  transfers between devices with their start and end apart: 32 -> 10, of which waited for: 16 -> 2; matrix products, arithmetic and copies ran while one was open for 4% -> 11% of each run, Pallas kernels for 0% -> 0%
where the time goes in v1:
time: 144 us; the launch traced here: 143 us
  starting transfers between devices  41.3 us (29%)
  local copies, waits for them, and re-layouts  37.9 us (26%)
  other arithmetic  28 us (19%)
  blocking collectives  26.2 us (18%)
  waiting for transfers between devices  5.32 us (4%)
  matrix products  2.38 us (2%)
  between operations  1.89 us (1%)
    all_gather x1, blocking collectives, shards(): column = lax.all_gather(package, 'gy', axis=0, tiled=False)  26.2 us
    ppermute x4, starting transfers between devices, halo_x(): got_low = lax.ppermute(jnp.concatenate(send_low), 'gx', forward)  18.8 us
    ppermute x4, starting transfers between devices, halo_x(): got_high = lax.ppermute(jnp.concatenate(send_high), 'gx', backward)  17.2 us
    unnamed x89, local copies, waits for them, and re-layouts  11.1 us
    another operation x9, other arithmetic, operate(): return jnp.stack(results)  5.1 us
    ppermute x1, waiting for transfers between devices, halo_y(): high = lax.ppermute(array[..., :depth, :], 'gy', backward)  4.75 us
    ppermute x1, starting transfers between devices, halo_y(): low = lax.ppermute(array[..., -depth:, :], 'gy', forward)  4 us
    another operation x21, other arithmetic, apply_ext(): return jnp.stack(results)  3.91 us
  transfers between devices with their start and end apart: 10, of which 2 were waited for; matrix products, arithmetic and copies ran while one was open for 11% of the time, Pallas kernels for 0%

profile of v1, /device:TPU:31, one launch (start us, length us, event | category | flops | bytes accessed | tf_op | source)
XLA Modules:
  0.0 142.9 jit_solution(10636239734010122771)
XLA Ops:
  1.6 2.5 %collective-permute-start.3 = (f32[40960]{0:T(1024)S(1)}, f32[40960]{0:T(1024)S(1)}, u32[]{:S(2)}, u32[]{:S(2)}) collective-permute-start(f32[40960]{0:T(1024)S(1)} %bitcast.227), channel_id=1, source_target_pairs={{24,0},{36,12},{48,24},{60,36},{72,48},{84,60},{96,72},{108,84},{1... | collective-permute-start | bytes 491528 | tf_op jit(solution)/shard_map/ppermute | solution.py:219
  4.0 2.9 %collective-permute-start.2 = (f32[40960]{0:T(1024)S(1)}, f32[40960]{0:T(1024)S(1)}, u32[]{:S(2)}, u32[]{:S(2)}) collective-permute-start(f32[40960]{0:T(1024)S(1)} %bitcast.228), channel_id=1, source_target_pairs={{12,0},{24,12},{36,24},{48,36},{60,48},{72,60},{84,72},{96,84},{10... | collective-permute-start | bytes 491528 | tf_op jit(solution)/shard_map/ppermute | solution.py:219
  6.9 6.0 %collective-permute-start.1 = (f32[40960]{0:T(1024)S(1)}, f32[40960]{0:T(1024)S(1)}, u32[]{:S(2)}, u32[]{:S(2)}) collective-permute-start(f32[40960]{0:T(1024)S(1)} %bitcast.229), channel_id=1, source_target_pairs={{0,12},{12,24},{24,36},{36,48},{48,60},{60,72},{72,84},{84,96},{96... | collective-permute-start | bytes 491528 | tf_op jit(solution)/shard_map/ppermute | solution.py:218
  13.0 2.8 %collective-permute-start = (f32[40960]{0:T(1024)S(1)}, f32[40960]{0:T(1024)S(1)}, u32[]{:S(2)}, u32[]{:S(2)}) collective-permute-start(f32[40960]{0:T(1024)S(1)} %bitcast.230), channel_id=1, source_target_pairs={{0,24},{12,36},{24,48},{36,60},{48,72},{60,84},{72,96},{84,108},{9... | collective-permute-start | bytes 491528 | tf_op jit(solution)/shard_map/ppermute | solution.py:218
  21.0 4.0 %collective-permute-start.4 = (f32[5,10,4,128]{3,2,1,0:T(4,128)S(1)}, f32[5,10,4,128]{3,2,1,0:T(4,128)S(1)}, u32[]{:S(2)}, u32[]{:S(2)}) collective-permute-start(f32[5,10,4,128]{3,2,1,0:T(4,128)S(1)} %get-tuple-element.83), channel_id=1, source_target_pairs={{0,1},{1,2},{2,3},{3,4},{4,5},{5,6},{6,7},{7,8},{8,9},{9,10},{10,1... | collective-permute-start | bytes 307208 | tf_op jit(solution)/shard_map/ppermute | solution.py:238
  25.0 1.3 collective-permute-start.5
  26.9 4.8 %collective-permute-done.5 = f32[5,10,4,128]{3,2,1,0:T(4,128)S(1)} collective-permute-done((f32[5,10,4,128]{3,2,1,0:T(4,128)S(1)}, f32[5,10,4,128]{3,2,1,0:T(4,128)S(1)}, u32[]{:S(2)}, u32[]{:S(2)}) %collective-permute-start.5) | collective-permute-done | bytes 102432 | tf_op jit(solution)/shard_map/ppermute | solution.py:239
  37.4 26.2 %all-gather.1 = f32[12,1,9728]{2,1,0:T(1,128)S(1)} all-gather(f32[1,1,9728]{2,1,0:T(1,128)S(1)} %reshape.364), channel_id=2, replica_groups=mesh['gx'=64,'gy'=12] {'gy'}, dimensions={0}, use_global_device_ids=true | all-gather | bytes 505856 | tf_op jit(solution)/shard_map/all_gather | solution.py:332
  66.0 1.1 reshape.349
  74.4 1.1 fusion.171
  77.4 1.5 %reshape.356 = f32[14592]{0:T(1024)} reshape(f32[3,1,38,128]{3,2,1,0:T(8,128)} %get-tuple-element.172) | data formatting | bytes 116736 | tf_op jit(solution)/shard_map/reshape | solution.py:215
  78.9 1.4 %reshape.348 = f32[14592]{0:T(1024)} reshape(f32[3,1,38,128]{3,2,1,0:T(8,128)} %get-tuple-element.173) | data formatting | bytes 116736 | tf_op jit(solution)/shard_map/reshape | solution.py:214
  83.3 1.3 fusion.17
  84.7 1.5 %pad_maximum_fusion.7 = (f32[18432]{0:T(1024)S(1)}, f32[18432]{0:T(1024)}) fusion(f32[3840]{0:T(1024)S(1)} %reshape.351, f32[14592]{0:T(1024)} %reshape.356, f32[14592]{0:T(1024)} %reshape.348), kind=kLoop, calls=%fused_computation.480 | loop fusion | flops 36864 | bytes 279552 | tf_op jit(solution)/shard_map/concatenate | solution.py:219
  86.2 2.6 %collective-permute-start.9 = (f32[18432]{0:T(1024)S(1)}, f32[18432]{0:T(1024)S(1)}, u32[]{:S(2)}, u32[]{:S(2)}) collective-permute-start(f32[18432]{0:T(1024)S(1)} %get-tuple-element.206), channel_id=1, source_target_pairs={{24,0},{36,12},{48,24},{60,36},{72,48},{84,60},{96,72},{108,84},{1... | collective-permute-start | bytes 221192 | tf_op jit(solution)/shard_map/ppermute | solution.py:219
  88.7 6.3 %collective-permute-start.6 = (f32[18432]{0:T(1024)}, f32[18432]{0:T(1024)S(1)}, u32[]{:S(2)}, u32[]{:S(2)}) collective-permute-start(f32[18432]{0:T(1024)} %get-tuple-element.207), channel_id=1, source_target_pairs={{0,24},{12,36},{24,48},{36,60},{48,72},{60,84},{72,96},{84,108},{9... | collective-permute-start | bytes 221192 | tf_op jit(solution)/shard_map/ppermute | solution.py:218
  95.0 1.5 %constant_dynamic-update-slice_fusion.5 = f32[33024]{0:T(1024)} fusion(f32[33024]{0:T(1024)} %custom-call.2, f32[29184]{0:T(1024)S(1)} %copy-done.28), kind=kLoop, calls=%fused_computation.611 | loop fusion | bytes 235520
  96.6 1.3 constant_dynamic-update-slice_fusion.10
  97.9 9.3 %collective-permute-start.8 = (f32[33024]{0:T(1024)}, f32[33024]{0:T(1024)}, u32[]{:S(2)}, u32[]{:S(2)}) collective-permute-start(f32[33024]{0:T(1024)} %constant_dynamic-update-slice_fusion.10), channel_id=1, source_target_pairs={{12,0},{24,12},{36,24},{48,36},{60,48},{72,60},{84,72},{96,84},{10... | collective-permute-start | bytes 396296 | tf_op jit(solution)/shard_map/ppermute | solution.py:219
  107.2 3.7 %collective-permute-start.7 = (f32[33024]{0:T(1024)}, f32[33024]{0:T(1024)}, u32[]{:S(2)}, u32[]{:S(2)}) collective-permute-start(f32[33024]{0:T(1024)} %constant_dynamic-update-slice_fusion.10), channel_id=1, source_target_pairs={{0,12},{12,24},{24,36},{36,48},{48,60},{60,72},{72,84},{84,96},{96... | collective-permute-start | bytes 396296 | tf_op jit(solution)/shard_map/ppermute | solution.py:218
  114.4 1.6 %slice.2432 = f32[29184]{0:T(1024)} slice(f32[33024]{0:T(1024)} %collective-permute-done.8), slice={[0:29184]} | slice | bytes 233472 | tf_op jit(solution)/shard_map/slice | solution.py:226
  116.9 1.3 slice.2426
  118.2 1.4 reshape.355
  119.6 1.5 %slice.2431 = f32[29184]{0:T(1024)} slice(f32[33024]{0:T(1024)} %collective-permute-done.7), slice={[0:29184]} | slice | bytes 233472 | tf_op jit(solution)/shard_map/slice | solution.py:225
  121.2 1.5 %reshape.360 = f32[3,2,38,128]{3,2,1,0:T(8,128)} reshape(f32[29184]{0:T(1024)} %slice.2431) | data formatting | bytes 233472 | tf_op jit(solution)/shard_map/reshape | solution.py:225
  122.7 1.3 slice.2425
  124.0 1.4 reshape.354
  125.5 1.4 bitcast_dynamic-update-slice_fusion.4
  127.5 1.4 bitcast_dynamic-update-slice_fusion.3
  128.9 1.4 bitcast_dynamic-update-slice_fusion.2
  130.3 1.2 fusion.426
  140.0 1.6 %slice_add_fusion.8 = f32[3,2,32,128]{3,2,1,0:T(8,128)} fusion(f32[3,4,34,128]{3,2,1,0:T(8,128)S(1)} %get-tuple-element.4, f32[3,6,36,128]{3,2,1,0:T(8,128)S(1)} %get-tuple-element.8, f32[3,8,38,128]{3,2,1,0:T(8,128)S(1)} %get-tuple-element.12, f32[3,10,40,128]{3,2,1,0:T(8,128)S(1)} %bitcast.218, f32[3,4,34,128]{3,2,1,0:T(8,128)} %copy-done.9, ...), kind=kLoop, calls=%fused_computation.268 | loop fusion | flops 147456 | bytes 786432 | tf_op jit(solution)/shard_map/add | solution.py:271
  (254 shorter events, 40.8 us)
Async XLA Ops:
  1.6 19.3 %collective-permute-start.3 = (f32[40960]{0:T(1024)S(1)}, f32[40960]{0:T(1024)S(1)}, u32[]{:S(2)}, u32[]{:S(2)}) collective-permute-start(f32[40960]{0:T(1024)S(1)} %bitcast.227), channel_id=1, source_target_pairs={{24,0},{36,12},{48,24},{60,36},{72,48},{84,60},{96,72},{108,84},{1... | collective-permute-start | bytes 491528 | tf_op jit(solution)/shard_map/ppermute | solution.py:219
  4.0 16.8 %collective-permute-start.2 = (f32[40960]{0:T(1024)S(1)}, f32[40960]{0:T(1024)S(1)}, u32[]{:S(2)}, u32[]{:S(2)}) collective-permute-start(f32[40960]{0:T(1024)S(1)} %bitcast.228), channel_id=1, source_target_pairs={{12,0},{24,12},{36,24},{48,36},{60,48},{72,60},{84,72},{96,84},{10... | collective-permute-start | bytes 491528 | tf_op jit(solution)/shard_map/ppermute | solution.py:219
  6.9 13.0 %collective-permute-start.1 = (f32[40960]{0:T(1024)S(1)}, f32[40960]{0:T(1024)S(1)}, u32[]{:S(2)}, u32[]{:S(2)}) collective-permute-start(f32[40960]{0:T(1024)S(1)} %bitcast.229), channel_id=1, source_target_pairs={{0,12},{12,24},{24,36},{36,48},{48,60},{60,72},{72,84},{84,96},{96... | collective-permute-start | bytes 491528 | tf_op jit(solution)/shard_map/ppermute | solution.py:218
  13.0 6.9 %collective-permute-start = (f32[40960]{0:T(1024)S(1)}, f32[40960]{0:T(1024)S(1)}, u32[]{:S(2)}, u32[]{:S(2)}) collective-permute-start(f32[40960]{0:T(1024)S(1)} %bitcast.230), channel_id=1, source_target_pairs={{0,24},{12,36},{24,48},{36,60},{48,72},{60,84},{72,96},{84,108},{9... | collective-permute-start | bytes 491528 | tf_op jit(solution)/shard_map/ppermute | solution.py:218
  15.8 21.2 %copy-start.36 = (s32[128]{0:T(128)}, s32[128]{0:T(128)S(1)}, u32[]{:S(2)}) copy-start(s32[128]{0:T(128)S(1)} %and_select_fusion) | copy-start | bytes 1540
  21.0 5.9 %collective-permute-start.4 = (f32[5,10,4,128]{3,2,1,0:T(4,128)S(1)}, f32[5,10,4,128]{3,2,1,0:T(4,128)S(1)}, u32[]{:S(2)}, u32[]{:S(2)}) collective-permute-start(f32[5,10,4,128]{3,2,1,0:T(4,128)S(1)} %get-tuple-element.83), channel_id=1, source_target_pairs={{0,1},{1,2},{2,3},{3,4},{4,5},{5,6},{6,7},{7,8},{8,9},{9,10},{10,1... | collective-permute-start | bytes 307208 | tf_op jit(solution)/shard_map/ppermute | solution.py:238
  25.0 6.7 %collective-permute-start.5 = (f32[5,10,4,128]{3,2,1,0:T(4,128)S(1)}, f32[5,10,4,128]{3,2,1,0:T(4,128)S(1)}, u32[]{:S(2)}, u32[]{:S(2)}) collective-permute-start(f32[5,10,4,128]{3,2,1,0:T(4,128)S(1)} %get-tuple-element.84), channel_id=1, source_target_pairs={{1,0},{2,1},{3,2},{4,3},{5,4},{6,5},{7,6},{8,7},{9,8},{10,9},{11,1... | collective-permute-start | bytes 307208 | tf_op jit(solution)/shard_map/ppermute | solution.py:239
  26.4 45.0 %copy-start.34 = (f32[12]{0:T(128)}, f32[12]{0:T(128)S(1)}, u32[]{:S(2)}) copy-start(f32[12]{0:T(128)S(1)} %get-tuple-element.211) | copy-start | bytes 148
  31.7 4.9 %copy-start.29 = (f32[2,32,127]{2,1,0:T(8,128)}, f32[2,32,127]{2,1,0:T(8,128)S(1)}, u32[]{:S(2)}) copy-start(f32[2,32,127]{2,1,0:T(8,128)S(1)} %slice.2302) | copy-start | bytes 97540
  31.8 3.8 %copy-start.24 = (f32[4,34,127]{2,1,0:T(8,128)}, f32[4,34,127]{2,1,0:T(8,128)S(1)}, u32[]{:S(2)}) copy-start(f32[4,34,127]{2,1,0:T(8,128)S(1)} %slice.2259) | copy-start | bytes 207268
  31.8 2.6 %copy-start.22 = (f32[6,36,127]{2,1,0:T(8,128)}, f32[6,36,127]{2,1,0:T(8,128)S(1)}, u32[]{:S(2)}) copy-start(f32[6,36,127]{2,1,0:T(8,128)S(1)} %slice.2214) | copy-start | bytes 329188
  31.8 1.4 copy-start.7
  36.9 27.7 %copy-start.5 = (f32[3,2,32,128]{3,2,1,0:T(8,128)}, f32[3,2,32,128]{3,2,1,0:T(8,128)S(1)}, u32[]{:S(2)}) copy-start(f32[3,2,32,128]{3,2,1,0:T(8,128)S(1)} %slice_subtract_fusion.88) | copy-start | bytes 294916
  84.5 10.5 %copy-start.28 = (f32[29184]{0:T(1024)S(1)}, f32[29184]{0:T(1024)}, u32[]{:S(2)}) copy-start(f32[29184]{0:T(1024)} %reshape.353) | copy-start | bytes 350212
  86.2 24.8 %collective-permute-start.9 = (f32[18432]{0:T(1024)S(1)}, f32[18432]{0:T(1024)S(1)}, u32[]{:S(2)}, u32[]{:S(2)}) collective-permute-start(f32[18432]{0:T(1024)S(1)} %get-tuple-element.206), channel_id=1, source_target_pairs={{24,0},{36,12},{48,24},{60,36},{72,48},{84,60},{96,72},{108,84},{1... | collective-permute-start | bytes 221192 | tf_op jit(solution)/shard_map/ppermute | solution.py:219
  88.7 24.3 %collective-permute-start.6 = (f32[18432]{0:T(1024)}, f32[18432]{0:T(1024)S(1)}, u32[]{:S(2)}, u32[]{:S(2)}) collective-permute-start(f32[18432]{0:T(1024)} %get-tuple-element.207), channel_id=1, source_target_pairs={{0,24},{12,36},{24,48},{36,60},{48,72},{60,84},{72,96},{84,108},{9... | collective-permute-start | bytes 221192 | tf_op jit(solution)/shard_map/ppermute | solution.py:218
  96.6 33.7 %copy-start.37 = (s32[128]{0:T(128)S(1)}, s32[128]{0:T(128)}, u32[]{:S(2)}) copy-start(s32[128]{0:T(128)} %copy-done.36) | copy-start | bytes 1540
  97.9 16.5 %collective-permute-start.8 = (f32[33024]{0:T(1024)}, f32[33024]{0:T(1024)}, u32[]{:S(2)}, u32[]{:S(2)}) collective-permute-start(f32[33024]{0:T(1024)} %constant_dynamic-update-slice_fusion.10), channel_id=1, source_target_pairs={{12,0},{24,12},{36,24},{48,36},{60,48},{72,60},{84,72},{96,84},{10... | collective-permute-start | bytes 396296 | tf_op jit(solution)/shard_map/ppermute | solution.py:219
  107.2 12.4 %collective-permute-start.7 = (f32[33024]{0:T(1024)}, f32[33024]{0:T(1024)}, u32[]{:S(2)}, u32[]{:S(2)}) collective-permute-start(f32[33024]{0:T(1024)} %constant_dynamic-update-slice_fusion.10), channel_id=1, source_target_pairs={{0,12},{12,24},{24,36},{36,48},{48,60},{60,72},{72,84},{84,96},{96... | collective-permute-start | bytes 396296 | tf_op jit(solution)/shard_map/ppermute | solution.py:218
  114.4 17.9 %copy-start.6 = (f32[3,2,32,128]{3,2,1,0:T(8,128)S(1)}, f32[3,2,32,128]{3,2,1,0:T(8,128)}, u32[]{:S(2)}) copy-start(f32[3,2,32,128]{3,2,1,0:T(8,128)} %copy-done.5) | copy-start | bytes 294916
  114.4 17.9 %copy-start.32 = (f32[3,2,3,128]{3,2,1,0:T(4,128)S(1)}, f32[3,2,3,128]{3,2,1,0:T(4,128)}, u32[]{:S(2)}) copy-start(f32[3,2,3,128]{3,2,1,0:T(4,128)} %copy-done.31) | copy-start | bytes 27652
  125.5 6.1 %copy-start.27 = (f32[3,2,38,128]{3,2,1,0:T(8,128)S(1)}, f32[3,2,38,128]{3,2,1,0:T(8,128)}, u32[]{:S(2)}) copy-start(f32[3,2,38,128]{3,2,1,0:T(8,128)} %reshape.360) | copy-start | bytes 350212
  133.2 1.2 copy-start.2
  133.2 1.2 copy-start.3
  133.2 1.2 copy-start.4
  139.7 2.1 %copy-start.11 = (f32[2,32,128]{2,1,0:T(8,128)S(1)}, f32[2,32,128]{2,1,0:T(8,128)}, u32[]{:S(2)}) copy-start(f32[2,32,128]{2,1,0:T(8,128)} %copy-done.10) | copy-start | bytes 98308
  139.8 2.1 %copy-start.13 = (f32[2,32,128]{2,1,0:T(8,128)S(1)}, f32[2,32,128]{2,1,0:T(8,128)}, u32[]{:S(2)}) copy-start(f32[2,32,128]{2,1,0:T(8,128)} %copy-done.12) | copy-start | bytes 98308
  139.8 2.1 %copy-start.15 = (f32[2,32,128]{2,1,0:T(8,128)S(1)}, f32[2,32,128]{2,1,0:T(8,128)}, u32[]{:S(2)}) copy-start(f32[2,32,128]{2,1,0:T(8,128)} %copy-done.14) | copy-start | bytes 98308
  139.8 2.1 %copy-start.17 = (f32[2,32,128]{2,1,0:T(8,128)S(1)}, f32[2,32,128]{2,1,0:T(8,128)}, u32[]{:S(2)}) copy-start(f32[2,32,128]{2,1,0:T(8,128)} %copy-done.16) | copy-start | bytes 98308
  139.8 2.1 %copy-start.19 = (f32[2,32,128]{2,1,0:T(8,128)S(1)}, f32[2,32,128]{2,1,0:T(8,128)}, u32[]{:S(2)}) copy-start(f32[2,32,128]{2,1,0:T(8,128)} %copy-done.18) | copy-start | bytes 98308
  139.8 2.1 %copy-start.21 = (f32[2,32,128]{2,1,0:T(8,128)S(1)}, f32[2,32,128]{2,1,0:T(8,128)}, u32[]{:S(2)}) copy-start(f32[2,32,128]{2,1,0:T(8,128)} %copy-done.20) | copy-start | bytes 98308
  140.0 2.1 %copy-start.30 = (f32[2,32,127]{2,1,0:T(8,128)S(1)}, f32[2,32,127]{2,1,0:T(8,128)}, u32[]{:S(2)}) copy-start(f32[2,32,127]{2,1,0:T(8,128)} %copy-done.29) | copy-start | bytes 97540
  (16 other events, 13.0 us)

commit v2 on v1

--- a/solution.py
+++ b/solution.py
@@ -198,37 +198,18 @@
     return jnp.stack(results)
 
 
-def halo_x(parts):
+def halo_x(array, depth):
     count = lax.axis_size("gx")
-    reach = max((d + a.shape[-3] - 1) // a.shape[-3] for a, d in parts)
-    lows = [[] for _ in parts]
-    highs = [[] for _ in parts]
+    width = array.shape[-3]
+    reach = (depth + width - 1) // width
+    lows, highs = [], []
     for dx in range(reach, 0, -1):
-        send_low, send_high, keys = [], [], []
-        for index, (array, d) in enumerate(parts):
-            width = array.shape[-3]
-            need = min(width, d - (dx - 1) * width)
-            if need <= 0:
-                continue
-            keys.append((index, array.shape[:-3] + (need,) + array.shape[-2:]))
-            send_low.append(array[..., width - need :, :, :].reshape(-1))
-            send_high.append(array[..., :need, :, :].reshape(-1))
+        need = min(width, depth - (dx - 1) * width)
         forward = [(i, i + dx) for i in range(count - dx)]
         backward = [(i + dx, i) for i in range(count - dx)]
-        got_low = lax.ppermute(jnp.concatenate(send_low), "gx", forward)
-        got_high = lax.ppermute(jnp.concatenate(send_high), "gx", backward)
-        offset = 0
-        for index, shape in keys:
-            size = 1
-            for value in shape:
-                size *= value
-            lows[index].append(got_low[offset : offset + size].reshape(shape))
-            highs[index].append(got_high[offset : offset + size].reshape(shape))
-            offset += size
-    out = []
-    for index, (array, d) in enumerate(parts):
-        out.append(jnp.concatenate(lows[index] + [array] + highs[index][::-1], axis=-3))
-    return out
+        lows.append(lax.ppermute(array[..., width - need :, :, :], "gx", forward))
+        highs.append(lax.ppermute(array[..., :need, :, :], "gx", backward))
+    return jnp.concatenate(lows + [array] + highs[::-1], axis=-3)
 
 
 def halo_y(array, depth):
@@ -298,7 +279,7 @@
     count_y = lax.axis_size("gy")
 
     stacked = jnp.concatenate([rhs_field, shear_modulus[None], lame_lambda[None]], axis=0)
-    (stacked,) = halo_x([(stacked, depth + 1)])
+    stacked = halo_x(stacked, depth + 1)
     stacked = halo_y(stacked, depth + 1)
     mu_ext = stacked[3]
     lam_ext = stacked[4]
@@ -323,58 +304,59 @@
     members = same_group(starts)
     cells_dev = coarse_x * coarse_y * coarse_z
 
-    edge_low = residual[:, :, :depth, :]
-    edge_high = residual[:, :, -depth:, :]
+    sums = coarse_res.sum(axis=(1, 2, 3))
+    slots = jnp.where(jnp.arange(count_y)[:, None] == gy, sums[None, :], 0.0)
+    all_sums = lax.psum(slots, "gy")
+
+    forward = [(i, i + 1) for i in range(count_y - 1)]
+    backward = [(i + 1, i) for i in range(count_y - 1)]
+    fine_reach = depth + 1
+    below = lax.ppermute(residual[:, :, -fine_reach:, :], "gy", forward)
+    above = lax.ppermute(residual[:, :, :fine_reach, :], "gy", backward)
     coarse_pack = jnp.concatenate([coarse_res, coarse_mu[None], coarse_lam[None]], axis=0)
-    package = jnp.concatenate(
-        [coarse_pack.reshape(-1), edge_low.reshape(-1), edge_high.reshape(-1)]
-    )
-    column = lax.all_gather(package, "gy", axis=0, tiled=False)
-    coarse_size = coarse_pack.size
-    edge_size = edge_low.size
-    column_pack = column[:, :coarse_size].reshape((count_y,) + coarse_pack.shape)
-    column_pack = jnp.moveaxis(column_pack, 0, 1)
-    column_low = column[:, coarse_size : coarse_size + edge_size].reshape(
-        (count_y,) + edge_low.shape
-    )
-    column_high = column[:, coarse_size + edge_size :].reshape((count_y,) + edge_high.shape)
-    below = lax.dynamic_index_in_dim(column_high, jnp.maximum(gy - 1, 0), 0, keepdims=False)
-    above = lax.dynamic_index_in_dim(
-        column_low, jnp.minimum(gy + 1, count_y - 1), 0, keepdims=False
-    )
-    below = jnp.where(gy > 0, below, 0.0)
-    above = jnp.where(gy < count_y - 1, above, 0.0)
+    pack_below = lax.ppermute(coarse_pack, "gy", forward)
+    pack_above = lax.ppermute(coarse_pack, "gy", backward)
     residual_y = jnp.concatenate([below, residual, above], axis=2)
 
-    coef_pad = pad_groups(column_pack[3:5], starts)
-    coarse_inverse = 1.0 / diagonal(coef_pad[0], coef_pad[1], 4.0)
+    window = jnp.stack([pack_below, coarse_pack, pack_above], axis=1)
+    next_start = lax.dynamic_index_in_dim(starts, jnp.minimum(gy + 1, count_y - 1), 0, keepdims=False)
+    own_start = lax.dynamic_index_in_dim(starts, gy, 0, keepdims=False)
+    window_starts = jnp.stack([jnp.zeros_like(own_start), own_start, next_start])
+    coef_pad = pad_groups(window[3:5], window_starts)
+    coarse_diag = diagonal(coef_pad[0], coef_pad[1], 4.0)
+    owners = gy - 1 + jnp.arange(3)
+    valid = (owners >= 0) & (owners < count_y)
+    usable = valid[None, :, None, None, None] & (coarse_diag > 0.0)
+    coarse_inverse = jnp.where(usable, 1.0 / coarse_diag, 0.0)
 
     def coarse_apply(field):
-        return operate(pad_groups(field, starts), coef_pad[0], coef_pad[1], 4.0)
-
-    column_res = column_pack[0:3]
+        return operate(pad_groups(field, window_starts), coef_pad[0], coef_pad[1], 4.0)
+
+    window_res = window[0:3]
     smoothed, coarse_left = smooth(
-        jnp.zeros_like(column_res), column_res, coarse_inverse, coarse_apply, COARSE_SWEEPS
-    )
-    device_sums = column_res.sum(axis=(2, 3, 4))
-    totals = jnp.sum(device_sums[:, None, :] * members[None, :, :], axis=2)
+        jnp.zeros_like(window_res), window_res, coarse_inverse, coarse_apply, COARSE_SWEEPS
+    )
+    totals = jnp.sum(members[:, :, None] * all_sums[None, :, :], axis=1)
     group_cells = jnp.sum(members, axis=1) * cells_dev
-    group_shift = totals / (SHIFT_SCALE * group_cells[None, :])
-    correction = smoothed + group_shift[:, :, None, None, None]
-    correction = jnp.moveaxis(correction, 1, 2).reshape(3, coarse_x, count_y * coarse_y, coarse_z)
+    group_shift = totals / (SHIFT_SCALE * group_cells[:, None])
+    window_shift = jnp.take(group_shift, jnp.clip(owners, 0, count_y - 1), axis=0)
+    window_shift = jnp.where(valid[:, None], window_shift, 0.0)
+    correction = smoothed + window_shift.T[:, :, None, None, None]
+    correction = jnp.moveaxis(correction, 1, 2).reshape(3, coarse_x, 3 * coarse_y, coarse_z)
     reach_c = (depth + 2) // 2
-    correction = jnp.pad(correction, ((0, 0), (0, 0), (reach_c, reach_c), (0, 0)))
-    corr_y = lax.dynamic_slice_in_dim(correction, gy * coarse_y, coarse_y + 2 * reach_c, axis=2)
-
-    residual_ext, corr_ext = halo_x([(residual_y, depth), (corr_y, reach_c)])
-    corr_z = upsample_z(corr_ext, pairs)
+    corr_y = correction[:, :, coarse_y - reach_c : 2 * coarse_y + reach_c, :]
+    corr_z = upsample_z(corr_y, pairs)
     fine_corr = jnp.broadcast_to(
         corr_z[:, :, None, :, None, :],
-        (3, corr_ext.shape[1], 2, corr_ext.shape[2], 2, width_z),
-    ).reshape(3, 2 * corr_ext.shape[1], 2 * corr_ext.shape[2], width_z)
+        (3, coarse_x, 2, corr_y.shape[2], 2, width_z),
+    ).reshape(3, width_x, 2 * corr_y.shape[2], width_z)
     fine_depth = 2 * reach_c
-    fine_corr = crop(fine_corr, fine_depth - (depth + 1))
-    solution = solution + crop(fine_corr, depth + 1)
+    fine_corr = fine_corr[:, :, fine_depth - fine_reach : fine_corr.shape[2] - (fine_depth - fine_reach), :]
+
+    joined = halo_x(jnp.concatenate([residual_y, fine_corr], axis=0), fine_reach)
+    residual_ext = crop(joined[0:3], 1)
+    fine_corr = joined[3:6]
+    solution = solution + crop(fine_corr, fine_reach)
     residual_ext = residual_ext - apply_ext(fine_corr, mu_ext, lam_ext, 1.0)
     solution, residual = smooth_ext(
         solution, residual_ext, inverse_diag, mu_ext, lam_ext, depth, SWEEPS

time: 144 us -> 136 us (0.944)
  the two profiles are of different devices: /device:TPU:31 before, /device:TPU:30 now
where the time goes in v2:
time: 136 us; the launch traced here: 135 us
  starting transfers between devices  45.4 us (33%)
  blocking collectives  31.7 us (23%)
  other arithmetic  27.6 us (20%)
  waiting for transfers between devices  14.1 us (10%)
  local copies, waits for them, and re-layouts  12 us (9%)
  matrix products  2.04 us (2%)
  between operations  1.84 us (1%)
    psum x1, blocking collectives, shards(): all_sums = lax.psum(slots, 'gy')  31.7 us
    ppermute x4, starting transfers between devices, halo_x(): lows.append(lax.ppermute(array[..., width - need:, :, :], 'gx', forward))  14.6 us
    ppermute x4, waiting for transfers between devices, halo_x(): highs.append(lax.ppermute(array[..., :need, :, :], 'gx', backward))  12.4 us
    ppermute x4, starting transfers between devices, halo_x(): highs.append(lax.ppermute(array[..., :need, :, :], 'gx', backward))  11.3 us
    ppermute x1, starting transfers between devices, shards(): pack_below = lax.ppermute(coarse_pack, 'gy', forward)  5.55 us
    ppermute x1, starting transfers between devices, shards(): below = lax.ppermute(residual[:, :, -fine_reach:, :], 'gy', forward)  5.15 us
    ppermute x1, starting transfers between devices, halo_y(): low = lax.ppermute(array[..., -depth:, :], 'gy', forward)  4.91 us
    another operation x21, other arithmetic, apply_ext(): return jnp.stack(results)  3.99 us
  transfers between devices with their start and end apart: 14, of which 5 were waited for; matrix products, arithmetic and copies ran while one was open for 16% of the time, Pallas kernels for 0%

profile of v2, /device:TPU:30, one launch (start us, length us, event | category | flops | bytes accessed | tf_op | source)
XLA Modules:
  0.0 134.5 jit_solution(15586516477610217338)
XLA Ops:
  0.7 1.0 pad_maximum_fusion.3
  1.6 4.6 %collective-permute-start = (f32[5,2,32,128]{3,2,1,0:T(8,128)S(1)}, f32[5,2,32,128]{3,2,1,0:T(8,128)S(1)}, u32[]{:S(2)}, u32[]{:S(2)}) collective-permute-start(f32[5,2,32,128]{3,2,1,0:T(8,128)S(1)} %pad_maximum_fusion.3), channel_id=1, source_target_pairs={{0,24},{12,36},{24,48},{36,60},{48,72},{60,84},{72,96},{84,108},{9... | collective-permute-start | bytes 491528 | tf_op jit(solution)/shard_map/ppermute | solution.py:210
  6.3 1.9 %collective-permute-start.1 = (f32[5,2,32,128]{3,2,1,0:T(8,128)S(1)}, f32[5,2,32,128]{3,2,1,0:T(8,128)S(1)}, u32[]{:S(2)}, u32[]{:S(2)}) collective-permute-start(f32[5,2,32,128]{3,2,1,0:T(8,128)S(1)} %pad_maximum_fusion.3), channel_id=1, source_target_pairs={{0,12},{12,24},{24,36},{36,48},{48,60},{60,72},{72,84},{84,96},{96... | collective-permute-start | bytes 491528 | tf_op jit(solution)/shard_map/ppermute | solution.py:210
  8.2 3.6 %collective-permute-start.2 = (f32[5,2,32,128]{3,2,1,0:T(8,128)S(1)}, f32[5,2,32,128]{3,2,1,0:T(8,128)S(1)}, u32[]{:S(2)}, u32[]{:S(2)}) collective-permute-start(f32[5,2,32,128]{3,2,1,0:T(8,128)S(1)} %pad_maximum_fusion.3), channel_id=1, source_target_pairs={{12,0},{24,12},{36,24},{48,36},{60,48},{72,60},{84,72},{96,84},{10... | collective-permute-start | bytes 491528 | tf_op jit(solution)/shard_map/ppermute | solution.py:211
  11.8 1.9 %collective-permute-start.3 = (f32[5,2,32,128]{3,2,1,0:T(8,128)S(1)}, f32[5,2,32,128]{3,2,1,0:T(8,128)S(1)}, u32[]{:S(2)}, u32[]{:S(2)}) collective-permute-start(f32[5,2,32,128]{3,2,1,0:T(8,128)S(1)} %pad_maximum_fusion.3), channel_id=1, source_target_pairs={{24,0},{36,12},{48,24},{60,36},{72,48},{84,60},{96,72},{108,84},{1... | collective-permute-start | bytes 491528 | tf_op jit(solution)/shard_map/ppermute | solution.py:211
  13.8 1.0 convolution_reduce_fusion
  17.8 1.3 constant_dynamic-slice_fusion.1
  19.1 1.4 %compare_select_fusion.6 = f32[2]{0:T(128)S(1)} fusion(s32[1]{0:T(128)} %bitcast.36, s32[1]{0:T(128)} %bitcast.35), kind=kLoop, calls=%fused_computation.759 | loop fusion | flops 6 | bytes 16 | tf_op jit(solution)/shard_map/jit(_where)/select_n | solution.py:101
  22.3 1.1 collective-permute-done.3
  23.5 1.3 collective-permute-start.5
  24.8 4.9 %collective-permute-start.4 = (f32[5,10,4,128]{3,2,1,0:T(4,128)S(1)}, f32[5,10,4,128]{3,2,1,0:T(4,128)S(1)}, u32[]{:S(2)}, u32[]{:S(2)}) collective-permute-start(f32[5,10,4,128]{3,2,1,0:T(4,128)S(1)} %get-tuple-element.79), channel_id=1, source_target_pairs={{0,1},{1,2},{2,3},{3,4},{4,5},{5,6},{6,7},{7,8},{8,9},{9,10},{10,1... | collective-permute-start | bytes 307208 | tf_op jit(solution)/shard_map/ppermute | solution.py:219
  30.4 1.5 %collective-permute-done.4 = f32[5,10,4,128]{3,2,1,0:T(4,128)S(1)} collective-permute-done((f32[5,10,4,128]{3,2,1,0:T(4,128)S(1)}, f32[5,10,4,128]{3,2,1,0:T(4,128)S(1)}, u32[]{:S(2)}, u32[]{:S(2)}) %collective-permute-start.4) | collective-permute-done | bytes 102432 | tf_op jit(solution)/shard_map/ppermute | solution.py:219
  32.4 0.9 add_bitcast_fusion.2
  37.1 0.9 fusion.452
  38.0 1.5 %reduce_sum.63 = f32[3,16,64]{2,1,0:T(8,128)} reduce(f32[3,16,2,64]{3,2,1,0:T(2,128)} %bitcast.338, f32[]{:T(128)} %constant.45.clone.1), dimensions={2}, to_apply=%region_1.2 | reduce | flops 3072 | bytes 36868 | tf_op jit(solution)/shard_map/reduce_sum | solution.py:298
  39.5 1.4 %fusion.451 = (f32[5,1,1,16,64]{4,3,1,2,0:T(8,128)}, f32[5,1,16,64]{3,2,0,1:T(8,128)}) fusion(f32[2,1,16,64]{3,2,0,1:T(8,128)S(1)} %multiply_bitcast_fusion.3, f32[3,1,16,64]{3,2,0,1:T(8,128)} %bitcast.340), kind=kLoop, calls=%fused_computation.779 | loop fusion | flops 5120 | bytes 61440 | tf_op jit(solution)/shard_map/stack | solution.py:321
  40.9 1.3 collective-permute-start.7
  42.1 5.6 %collective-permute-start.6 = (f32[5,1,16,64]{3,2,0,1:T(8,128)}, f32[5,1,16,64]{3,2,0,1:T(8,128)}, u32[]{:S(2)}, u32[]{:S(2)}) collective-permute-start(f32[5,1,16,64]{3,2,0,1:T(8,128)} %get-tuple-element.201), channel_id=1, source_target_pairs={{0,1},{1,2},{2,3},{3,4},{4,5},{5,6},{6,7},{7,8},{8,9},{9,10},{10,1... | collective-permute-start | bytes 61448 | tf_op jit(solution)/shard_map/ppermute | solution.py:317
  49.0 31.7 %psum.7 = f32[12,3]{0,1:T(4,128)S(1)} all-reduce(f32[12,3]{0,1:T(4,128)S(1)} %broadcast_select_fusion), channel_id=1, replica_groups=mesh['gx'=64,'gy'=12] {'gy'}, use_global_device_ids=true, to_apply=%region_6.7 | all-reduce | flops 36 | bytes 288 | tf_op jit(solution)/shard_map/psum | solution.py:309
  82.2 1.3 collective-permute-start.9
  83.5 5.2 %collective-permute-start.8 = (f32[3,2,4,128]{3,2,1,0:T(4,128)}, f32[3,2,4,128]{3,2,1,0:T(4,128)}, u32[]{:S(2)}, u32[]{:S(2)}) collective-permute-start(f32[3,2,4,128]{3,2,1,0:T(4,128)} %get-tuple-element.172), channel_id=1, source_target_pairs={{0,1},{1,2},{2,3},{3,4},{4,5},{5,6},{6,7},{7,8},{8,9},{9,10},{10,1... | collective-permute-start | bytes 36872 | tf_op jit(solution)/shard_map/ppermute | solution.py:314
  90.0 0.8 copy.94
  90.9 0.8 copy.93
  91.7 0.8 copy.193
  93.3 0.8 fusion.447
  98.7 6.1 %collective-permute-start.10 = (f32[6,2,40,128]{3,2,1,0:T(8,128)S(1)}, f32[6,2,40,128]{3,2,1,0:T(8,128)S(1)}, u32[]{:S(2)}, u32[]{:S(2)}) collective-permute-start(f32[6,2,40,128]{3,2,1,0:T(8,128)S(1)} %pad_maximum_fusion.2), channel_id=1, source_target_pairs={{0,24},{12,36},{24,48},{36,60},{48,72},{60,84},{72,96},{84,108},{9... | collective-permute-start | bytes 737288 | tf_op jit(solution)/shard_map/ppermute | solution.py:210
  104.8 1.9 %collective-permute-start.11 = (f32[6,2,40,128]{3,2,1,0:T(8,128)S(1)}, f32[6,2,40,128]{3,2,1,0:T(8,128)S(1)}, u32[]{:S(2)}, u32[]{:S(2)}) collective-permute-start(f32[6,2,40,128]{3,2,1,0:T(8,128)S(1)} %pad_maximum_fusion.2), channel_id=1, source_target_pairs={{0,12},{12,24},{24,36},{36,48},{48,60},{60,72},{72,84},{84,96},{96... | collective-permute-start | bytes 737288 | tf_op jit(solution)/shard_map/ppermute | solution.py:210
  106.7 3.6 %collective-permute-start.12 = (f32[6,2,40,128]{3,2,1,0:T(8,128)S(1)}, f32[6,2,40,128]{3,2,1,0:T(8,128)S(1)}, u32[]{:S(2)}, u32[]{:S(2)}) collective-permute-start(f32[6,2,40,128]{3,2,1,0:T(8,128)S(1)} %pad_maximum_fusion.2), channel_id=1, source_target_pairs={{12,0},{24,12},{36,24},{48,36},{60,48},{72,60},{84,72},{96,84},{10... | collective-permute-start | bytes 737288 | tf_op jit(solution)/shard_map/ppermute | solution.py:211
  110.4 2.1 %collective-permute-start.13 = (f32[6,2,40,128]{3,2,1,0:T(8,128)S(1)}, f32[6,2,40,128]{3,2,1,0:T(8,128)S(1)}, u32[]{:S(2)}, u32[]{:S(2)}) collective-permute-start(f32[6,2,40,128]{3,2,1,0:T(8,128)S(1)} %pad_maximum_fusion.2), channel_id=1, source_target_pairs={{24,0},{36,12},{48,24},{60,36},{72,48},{84,60},{96,72},{108,84},{1... | collective-permute-start | bytes 737288 | tf_op jit(solution)/shard_map/ppermute | solution.py:211
  113.3 2.0 %collective-permute-done.12 = f32[6,2,40,128]{3,2,1,0:T(8,128)S(1)} collective-permute-done((f32[6,2,40,128]{3,2,1,0:T(8,128)S(1)}, f32[6,2,40,128]{3,2,1,0:T(8,128)S(1)}, u32[]{:S(2)}, u32[]{:S(2)}) %collective-permute-start.12) | collective-permute-done | bytes 245792 | tf_op jit(solution)/shard_map/ppermute | solution.py:211
  115.4 9.2 %collective-permute-done.13 = f32[6,2,40,128]{3,2,1,0:T(8,128)S(1)} collective-permute-done((f32[6,2,40,128]{3,2,1,0:T(8,128)S(1)}, f32[6,2,40,128]{3,2,1,0:T(8,128)S(1)}, u32[]{:S(2)}, u32[]{:S(2)}) %collective-permute-start.13) | collective-permute-done | bytes 245792 | tf_op jit(solution)/shard_map/ppermute | solution.py:211
  131.4 1.6 %slice_add_fusion.8 = f32[3,2,32,128]{3,2,1,0:T(8,128)} fusion(f32[3,4,34,128]{3,2,1,0:T(8,128)S(1)} %get-tuple-element.6, f32[3,6,36,128]{3,2,1,0:T(8,128)S(1)} %get-tuple-element.10, f32[3,8,38,128]{3,2,1,0:T(8,128)S(1)} %get-tuple-element.14, f32[3,4,34,128]{3,2,1,0:T(8,128)} %copy-done.4, f32[3,6,36,128]{3,2,1,0:T(8,128)S(1)} %get-tuple-element.54, ...), kind=kLoop, calls=%fused_computation.247 | loop fusion | flops 147456 | bytes 737280 | tf_op jit(solution)/shard_map/add | solution.py:252
  (230 shorter events, 27.7 us)
Async XLA Ops:
  0.6 21.6 %copy-start.22 = (f32[2,32,128]{2,1,0:T(8,128)S(1)}, f32[2,32,128]{2,1,0:T(8,128)}, u32[]{:S(2)}) copy-start(f32[2,32,128]{2,1,0:T(8,128)} %param.6) | copy-start | bytes 98308
  0.6 21.6 %copy-start.23 = (f32[2,32,128]{2,1,0:T(8,128)S(1)}, f32[2,32,128]{2,1,0:T(8,128)}, u32[]{:S(2)}) copy-start(f32[2,32,128]{2,1,0:T(8,128)} %param.5) | copy-start | bytes 98308
  0.7 21.6 %copy-start.21 = (f32[3,2,32,128]{3,2,1,0:T(8,128)S(1)}, f32[3,2,32,128]{3,2,1,0:T(8,128)}, u32[]{:S(2)}) copy-start(f32[3,2,32,128]{3,2,1,0:T(8,128)} %param.4) | copy-start | bytes 294916
  1.6 20.5 %collective-permute-start = (f32[5,2,32,128]{3,2,1,0:T(8,128)S(1)}, f32[5,2,32,128]{3,2,1,0:T(8,128)S(1)}, u32[]{:S(2)}, u32[]{:S(2)}) collective-permute-start(f32[5,2,32,128]{3,2,1,0:T(8,128)S(1)} %pad_maximum_fusion.3), channel_id=1, source_target_pairs={{0,24},{12,36},{24,48},{36,60},{48,72},{60,84},{72,96},{84,108},{9... | collective-permute-start | bytes 491528 | tf_op jit(solution)/shard_map/ppermute | solution.py:210
  6.3 15.9 %collective-permute-start.1 = (f32[5,2,32,128]{3,2,1,0:T(8,128)S(1)}, f32[5,2,32,128]{3,2,1,0:T(8,128)S(1)}, u32[]{:S(2)}, u32[]{:S(2)}) collective-permute-start(f32[5,2,32,128]{3,2,1,0:T(8,128)S(1)} %pad_maximum_fusion.3), channel_id=1, source_target_pairs={{0,12},{12,24},{24,36},{36,48},{48,60},{60,72},{72,84},{84,96},{96... | collective-permute-start | bytes 491528 | tf_op jit(solution)/shard_map/ppermute | solution.py:210
  8.2 14.1 %collective-permute-start.2 = (f32[5,2,32,128]{3,2,1,0:T(8,128)S(1)}, f32[5,2,32,128]{3,2,1,0:T(8,128)S(1)}, u32[]{:S(2)}, u32[]{:S(2)}) collective-permute-start(f32[5,2,32,128]{3,2,1,0:T(8,128)S(1)} %pad_maximum_fusion.3), channel_id=1, source_target_pairs={{12,0},{24,12},{36,24},{48,36},{60,48},{72,60},{84,72},{96,84},{10... | collective-permute-start | bytes 491528 | tf_op jit(solution)/shard_map/ppermute | solution.py:211
  11.8 11.6 %collective-permute-start.3 = (f32[5,2,32,128]{3,2,1,0:T(8,128)S(1)}, f32[5,2,32,128]{3,2,1,0:T(8,128)S(1)}, u32[]{:S(2)}, u32[]{:S(2)}) collective-permute-start(f32[5,2,32,128]{3,2,1,0:T(8,128)S(1)} %pad_maximum_fusion.3), channel_id=1, source_target_pairs={{24,0},{36,12},{48,24},{60,36},{72,48},{84,60},{96,72},{108,84},{1... | collective-permute-start | bytes 491528 | tf_op jit(solution)/shard_map/ppermute | solution.py:211
  23.5 6.9 %collective-permute-start.5 = (f32[5,10,4,128]{3,2,1,0:T(4,128)S(1)}, f32[5,10,4,128]{3,2,1,0:T(4,128)S(1)}, u32[]{:S(2)}, u32[]{:S(2)}) collective-permute-start(f32[5,10,4,128]{3,2,1,0:T(4,128)S(1)} %get-tuple-element.80), channel_id=1, source_target_pairs={{1,0},{2,1},{3,2},{4,3},{5,4},{6,5},{7,6},{8,7},{9,8},{10,9},{11,1... | collective-permute-start | bytes 307208 | tf_op jit(solution)/shard_map/ppermute | solution.py:220
  24.8 7.1 %collective-permute-start.4 = (f32[5,10,4,128]{3,2,1,0:T(4,128)S(1)}, f32[5,10,4,128]{3,2,1,0:T(4,128)S(1)}, u32[]{:S(2)}, u32[]{:S(2)}) collective-permute-start(f32[5,10,4,128]{3,2,1,0:T(4,128)S(1)} %get-tuple-element.79), channel_id=1, source_target_pairs={{0,1},{1,2},{2,3},{3,4},{4,5},{5,6},{6,7},{7,8},{8,9},{9,10},{10,1... | collective-permute-start | bytes 307208 | tf_op jit(solution)/shard_map/ppermute | solution.py:219
  32.1 2.5 %copy-start.17 = (f32[6,36,127]{2,1,0:T(8,128)}, f32[6,36,127]{2,1,0:T(8,128)S(1)}, u32[]{:S(2)}) copy-start(f32[6,36,127]{2,1,0:T(8,128)S(1)} %slice.2166) | copy-start | bytes 329188
  32.3 3.4 %copy-start.19 = (f32[4,34,127]{2,1,0:T(8,128)}, f32[4,34,127]{2,1,0:T(8,128)S(1)}, u32[]{:S(2)}) copy-start(f32[4,34,127]{2,1,0:T(8,128)S(1)} %slice.2211) | copy-start | bytes 207268
  32.4 4.4 %copy-start.24 = (f32[2,32,127]{2,1,0:T(8,128)}, f32[2,32,127]{2,1,0:T(8,128)S(1)}, u32[]{:S(2)}) copy-start(f32[2,32,127]{2,1,0:T(8,128)S(1)} %slice.2254) | copy-start | bytes 97540
  36.5 1.5 %copy-start.11 = (f32[2,32,128]{2,1,0:T(8,128)}, f32[2,32,128]{2,1,0:T(8,128)S(1)}, u32[]{:S(2)}) copy-start(f32[2,32,128]{2,1,0:T(8,128)S(1)} %get-tuple-element.40) | copy-start | bytes 98308
  36.5 1.5 %copy-start.13 = (f32[2,32,128]{2,1,0:T(8,128)}, f32[2,32,128]{2,1,0:T(8,128)S(1)}, u32[]{:S(2)}) copy-start(f32[2,32,128]{2,1,0:T(8,128)S(1)} %get-tuple-element.42) | copy-start | bytes 98308
  36.5 1.5 %copy-start.15 = (f32[2,32,128]{2,1,0:T(8,128)}, f32[2,32,128]{2,1,0:T(8,128)S(1)}, u32[]{:S(2)}) copy-start(f32[2,32,128]{2,1,0:T(8,128)S(1)} %get-tuple-element.43) | copy-start | bytes 98308
  40.9 50.8 %collective-permute-start.7 = (f32[5,1,16,64]{3,2,0,1:T(8,128)}, f32[5,1,16,64]{3,2,0,1:T(8,128)}, u32[]{:S(2)}, u32[]{:S(2)}) collective-permute-start(f32[5,1,16,64]{3,2,0,1:T(8,128)} %get-tuple-element.201), channel_id=1, source_target_pairs={{1,0},{2,1},{3,2},{4,3},{5,4},{6,5},{7,6},{8,7},{9,8},{10,9},{11,1... | collective-permute-start | bytes 61448 | tf_op jit(solution)/shard_map/ppermute | solution.py:318
  42.1 48.7 %collective-permute-start.6 = (f32[5,1,16,64]{3,2,0,1:T(8,128)}, f32[5,1,16,64]{3,2,0,1:T(8,128)}, u32[]{:S(2)}, u32[]{:S(2)}) collective-permute-start(f32[5,1,16,64]{3,2,0,1:T(8,128)} %get-tuple-element.201), channel_id=1, source_target_pairs={{0,1},{1,2},{2,3},{3,4},{4,5},{5,6},{6,7},{7,8},{8,9},{9,10},{10,1... | collective-permute-start | bytes 61448 | tf_op jit(solution)/shard_map/ppermute | solution.py:317
  82.2 15.7 %collective-permute-start.9 = (f32[3,2,4,128]{3,2,1,0:T(4,128)}, f32[3,2,4,128]{3,2,1,0:T(4,128)}, u32[]{:S(2)}, u32[]{:S(2)}) collective-permute-start(f32[3,2,4,128]{3,2,1,0:T(4,128)} %get-tuple-element.173), channel_id=1, source_target_pairs={{1,0},{2,1},{3,2},{4,3},{5,4},{6,5},{7,6},{8,7},{9,8},{10,9},{11,1... | collective-permute-start | bytes 36872 | tf_op jit(solution)/shard_map/ppermute | solution.py:315
  83.5 14.4 %collective-permute-start.8 = (f32[3,2,4,128]{3,2,1,0:T(4,128)}, f32[3,2,4,128]{3,2,1,0:T(4,128)}, u32[]{:S(2)}, u32[]{:S(2)}) collective-permute-start(f32[3,2,4,128]{3,2,1,0:T(4,128)} %get-tuple-element.172), channel_id=1, source_target_pairs={{0,1},{1,2},{2,3},{3,4},{4,5},{5,6},{6,7},{7,8},{8,9},{9,10},{10,1... | collective-permute-start | bytes 36872 | tf_op jit(solution)/shard_map/ppermute | solution.py:314
  90.0 4.4 %copy-start.31 = (pred[3]{0:T(512)(128)(4,1)S(1)}, pred[3]{0:T(512)(128)(4,1)}, u32[]{:S(2)}) copy-start(pred[3]{0:T(512)(128)(4,1)} %compare_and_fusion.1) | copy-start | bytes 13
  92.5 2.1 %copy-start.27 = (f32[3]{0:T(128)S(1)}, f32[3]{0:T(128)}, u32[]{:S(2)}) copy-start(f32[3]{0:T(128)} %get-tuple-element.205) | copy-start | bytes 40
  92.5 2.2 %copy-start.26 = (f32[3]{0:T(128)S(1)}, f32[3]{0:T(128)}, u32[]{:S(2)}) copy-start(f32[3]{0:T(128)} %get-tuple-element.204) | copy-start | bytes 40
  98.7 13.8 %collective-permute-start.10 = (f32[6,2,40,128]{3,2,1,0:T(8,128)S(1)}, f32[6,2,40,128]{3,2,1,0:T(8,128)S(1)}, u32[]{:S(2)}, u32[]{:S(2)}) collective-permute-start(f32[6,2,40,128]{3,2,1,0:T(8,128)S(1)} %pad_maximum_fusion.2), channel_id=1, source_target_pairs={{0,24},{12,36},{24,48},{36,60},{48,72},{60,84},{72,96},{84,108},{9... | collective-permute-start | bytes 737288 | tf_op jit(solution)/shard_map/ppermute | solution.py:210
  104.8 7.7 %collective-permute-start.11 = (f32[6,2,40,128]{3,2,1,0:T(8,128)S(1)}, f32[6,2,40,128]{3,2,1,0:T(8,128)S(1)}, u32[]{:S(2)}, u32[]{:S(2)}) collective-permute-start(f32[6,2,40,128]{3,2,1,0:T(8,128)S(1)} %pad_maximum_fusion.2), channel_id=1, source_target_pairs={{0,12},{12,24},{24,36},{36,48},{48,60},{60,72},{72,84},{84,96},{96... | collective-permute-start | bytes 737288 | tf_op jit(solution)/shard_map/ppermute | solution.py:210
  106.7 8.6 %collective-permute-start.12 = (f32[6,2,40,128]{3,2,1,0:T(8,128)S(1)}, f32[6,2,40,128]{3,2,1,0:T(8,128)S(1)}, u32[]{:S(2)}, u32[]{:S(2)}) collective-permute-start(f32[6,2,40,128]{3,2,1,0:T(8,128)S(1)} %pad_maximum_fusion.2), channel_id=1, source_target_pairs={{12,0},{24,12},{36,24},{48,36},{60,48},{72,60},{84,72},{96,84},{10... | collective-permute-start | bytes 737288 | tf_op jit(solution)/shard_map/ppermute | solution.py:211
  110.4 14.2 %collective-permute-start.13 = (f32[6,2,40,128]{3,2,1,0:T(8,128)S(1)}, f32[6,2,40,128]{3,2,1,0:T(8,128)S(1)}, u32[]{:S(2)}, u32[]{:S(2)}) collective-permute-start(f32[6,2,40,128]{3,2,1,0:T(8,128)S(1)} %pad_maximum_fusion.2), channel_id=1, source_target_pairs={{24,0},{36,12},{48,24},{60,36},{72,48},{84,60},{96,72},{108,84},{1... | collective-permute-start | bytes 737288 | tf_op jit(solution)/shard_map/ppermute | solution.py:211
  131.3 2.0 %copy-start.6 = (f32[2,32,128]{2,1,0:T(8,128)S(1)}, f32[2,32,128]{2,1,0:T(8,128)}, u32[]{:S(2)}) copy-start(f32[2,32,128]{2,1,0:T(8,128)} %copy-done.5) | copy-start | bytes 98308
  131.3 2.0 %copy-start.8 = (f32[2,32,128]{2,1,0:T(8,128)S(1)}, f32[2,32,128]{2,1,0:T(8,128)}, u32[]{:S(2)}) copy-start(f32[2,32,128]{2,1,0:T(8,128)} %copy-done.7) | copy-start | bytes 98308
  131.3 1.9 %copy-start.10 = (f32[2,32,128]{2,1,0:T(8,128)S(1)}, f32[2,32,128]{2,1,0:T(8,128)}, u32[]{:S(2)}) copy-start(f32[2,32,128]{2,1,0:T(8,128)} %copy-done.9) | copy-start | bytes 98308
  131.3 1.9 %copy-start.12 = (f32[2,32,128]{2,1,0:T(8,128)S(1)}, f32[2,32,128]{2,1,0:T(8,128)}, u32[]{:S(2)}) copy-start(f32[2,32,128]{2,1,0:T(8,128)} %copy-done.11) | copy-start | bytes 98308
  131.3 1.9 %copy-start.14 = (f32[2,32,128]{2,1,0:T(8,128)S(1)}, f32[2,32,128]{2,1,0:T(8,128)}, u32[]{:S(2)}) copy-start(f32[2,32,128]{2,1,0:T(8,128)} %copy-done.13) | copy-start | bytes 98308
  131.3 1.9 %copy-start.16 = (f32[2,32,128]{2,1,0:T(8,128)S(1)}, f32[2,32,128]{2,1,0:T(8,128)}, u32[]{:S(2)}) copy-start(f32[2,32,128]{2,1,0:T(8,128)} %copy-done.15) | copy-start | bytes 98308
  (14 other events, 11.7 us)

commit v3 on v2

--- a/solution.py
+++ b/solution.py
@@ -305,8 +305,13 @@
     cells_dev = coarse_x * coarse_y * coarse_z
 
     sums = coarse_res.sum(axis=(1, 2, 3))
-    slots = jnp.where(jnp.arange(count_y)[:, None] == gy, sums[None, :], 0.0)
-    all_sums = lax.psum(slots, "gy")
+    gathered = sums[None, :]
+    while gathered.shape[0] < count_y:
+        have = gathered.shape[0]
+        take = min(have, count_y - have)
+        ring = [(i, (i + have) % count_y) for i in range(count_y)]
+        gathered = jnp.concatenate([gathered, lax.ppermute(gathered[:take], "gy", ring)], axis=0)
+    all_sums = jnp.take(gathered, (gy - jnp.arange(count_y)) % count_y, axis=0)
 
     forward = [(i, i + 1) for i in range(count_y - 1)]
     backward = [(i + 1, i) for i in range(count_y - 1)]

time: 136 us -> 148 us (1.088)
  blocking collectives: 31.7 us -> 0 us
  starting transfers between devices: 45.4 us -> 67.6 us
  waiting for transfers between devices: 14.1 us -> 29.4 us
  other arithmetic: 27.6 us -> 31.3 us
  local copies, waits for them, and re-layouts: 12 us -> 14.3 us
    psum x1 -> x0, blocking collectives: 31.7 us -> none  [shards(): all_sums = lax.psum(slots, 'gy')]
    ppermute x0 -> x4, starting transfers between devices: none -> 20.1 us  [shards(): lax.ppermute(gathered[:take], 'gy', ring)]
    ppermute x0 -> x4, waiting for transfers between devices: none -> 16.1 us  [shards(): lax.ppermute(gathered[:take], 'gy', ring)]
    ppermute x1, starting transfers between devices: 5.15 us -> 6.68 us  [shards(): below = lax.ppermute(residual[:, :, -fine_reach:, :], 'gy', forward)]
    unnamed x76 -> x82, local copies, waits for them, and re-layouts: 3.78 us -> 4.13 us
  transfers between devices with their start and end apart: 14 -> 18, of which waited for: 5 -> 9; matrix products, arithmetic and copies ran while one was open for 16% -> 18% of each run, Pallas kernels for 0% -> 0%
where the time goes in v3:
time: 148 us; the launch traced here: 147 us
  starting transfers between devices  67.6 us (46%)
  other arithmetic  31.3 us (21%)
  waiting for transfers between devices  29.4 us (20%)
  local copies, waits for them, and re-layouts  14.3 us (10%)
  matrix products  2.04 us (1%)
  between operations  1.91 us (1%)
    ppermute x4, starting transfers between devices, shards(): lax.ppermute(gathered[:take], 'gy', ring)  20.1 us
    ppermute x4, waiting for transfers between devices, shards(): lax.ppermute(gathered[:take], 'gy', ring)  16.1 us
    ppermute x4, starting transfers between devices, halo_x(): lows.append(lax.ppermute(array[..., width - need:, :, :], 'gx', forward))  15.3 us
    ppermute x4, waiting for transfers between devices, halo_x(): highs.append(lax.ppermute(array[..., :need, :, :], 'gx', backward))  11.7 us
    ppermute x4, starting transfers between devices, halo_x(): highs.append(lax.ppermute(array[..., :need, :, :], 'gx', backward))  11.3 us
    ppermute x1, starting transfers between devices, shards(): below = lax.ppermute(residual[:, :, -fine_reach:, :], 'gy', forward)  6.68 us
    ppermute x1, starting transfers between devices, shards(): pack_below = lax.ppermute(coarse_pack, 'gy', forward)  5.56 us
    ppermute x1, starting transfers between devices, halo_y(): low = lax.ppermute(array[..., -depth:, :], 'gy', forward)  4.91 us
  transfers between devices with their start and end apart: 18, of which 9 were waited for; matrix products, arithmetic and copies ran while one was open for 18% of the time, Pallas kernels for 0%

profile of v3, /device:TPU:30, one launch (start us, length us, event | category | flops | bytes accessed | tf_op | source)
XLA Modules:
  0.0 146.6 jit_solution(7060578034232160250)
XLA Ops:
  0.7 1.0 pad_maximum_fusion.3
  1.6 4.6 %collective-permute-start = (f32[5,2,32,128]{3,2,1,0:T(8,128)S(1)}, f32[5,2,32,128]{3,2,1,0:T(8,128)S(1)}, u32[]{:S(2)}, u32[]{:S(2)}) collective-permute-start(f32[5,2,32,128]{3,2,1,0:T(8,128)S(1)} %pad_maximum_fusion.3), channel_id=1, source_target_pairs={{0,24},{12,36},{24,48},{36,60},{48,72},{60,84},{72,96},{84,108},{9... | collective-permute-start | bytes 491528 | tf_op jit(solution)/shard_map/ppermute | solution.py:210
  6.3 1.9 %collective-permute-start.1 = (f32[5,2,32,128]{3,2,1,0:T(8,128)S(1)}, f32[5,2,32,128]{3,2,1,0:T(8,128)S(1)}, u32[]{:S(2)}, u32[]{:S(2)}) collective-permute-start(f32[5,2,32,128]{3,2,1,0:T(8,128)S(1)} %pad_maximum_fusion.3), channel_id=1, source_target_pairs={{0,12},{12,24},{24,36},{36,48},{48,60},{60,72},{72,84},{84,96},{96... | collective-permute-start | bytes 491528 | tf_op jit(solution)/shard_map/ppermute | solution.py:210
  8.2 3.6 %collective-permute-start.2 = (f32[5,2,32,128]{3,2,1,0:T(8,128)S(1)}, f32[5,2,32,128]{3,2,1,0:T(8,128)S(1)}, u32[]{:S(2)}, u32[]{:S(2)}) collective-permute-start(f32[5,2,32,128]{3,2,1,0:T(8,128)S(1)} %pad_maximum_fusion.3), channel_id=1, source_target_pairs={{12,0},{24,12},{36,24},{48,36},{60,48},{72,60},{84,72},{96,84},{10... | collective-permute-start | bytes 491528 | tf_op jit(solution)/shard_map/ppermute | solution.py:211
  11.8 1.9 %collective-permute-start.3 = (f32[5,2,32,128]{3,2,1,0:T(8,128)S(1)}, f32[5,2,32,128]{3,2,1,0:T(8,128)S(1)}, u32[]{:S(2)}, u32[]{:S(2)}) collective-permute-start(f32[5,2,32,128]{3,2,1,0:T(8,128)S(1)} %pad_maximum_fusion.3), channel_id=1, source_target_pairs={{24,0},{36,12},{48,24},{60,36},{72,48},{84,60},{96,72},{108,84},{1... | collective-permute-start | bytes 491528 | tf_op jit(solution)/shard_map/ppermute | solution.py:211
  18.4 1.3 constant_dynamic-slice_fusion.1
  19.7 1.4 compare_select_fusion.8
  23.5 1.3 collective-permute-start.5
  24.8 4.9 %collective-permute-start.4 = (f32[5,10,4,128]{3,2,1,0:T(4,128)S(1)}, f32[5,10,4,128]{3,2,1,0:T(4,128)S(1)}, u32[]{:S(2)}, u32[]{:S(2)}) collective-permute-start(f32[5,10,4,128]{3,2,1,0:T(4,128)S(1)} %get-tuple-element.79), channel_id=1, source_target_pairs={{0,1},{1,2},{2,3},{3,4},{4,5},{5,6},{6,7},{7,8},{8,9},{9,10},{10,1... | collective-permute-start | bytes 307208 | tf_op jit(solution)/shard_map/ppermute | solution.py:219
  30.5 1.4 collective-permute-done.4
  38.1 1.5 reduce_sum.63
  39.5 1.4 fusion.452
  40.9 1.3 collective-permute-start.7
  42.2 5.6 %collective-permute-start.6 = (f32[5,1,16,64]{3,2,0,1:T(8,128)}, f32[5,1,16,64]{3,2,0,1:T(8,128)}, u32[]{:S(2)}, u32[]{:S(2)}) collective-permute-start(f32[5,1,16,64]{3,2,0,1:T(8,128)} %get-tuple-element.201), channel_id=1, source_target_pairs={{0,1},{1,2},{2,3},{3,4},{4,5},{5,6},{6,7},{7,8},{8,9},{9,10},{10,1... | collective-permute-start | bytes 61448 | tf_op jit(solution)/shard_map/ppermute | solution.py:322
  49.0 3.7 %collective-permute-start.8 = (f32[1,3]{1,0:T(1,128)}, f32[1,3]{1,0:T(1,128)S(1)}, u32[]{:S(2)}, u32[]{:S(2)}) collective-permute-start(f32[1,3]{1,0:T(1,128)} %bitcast.344), channel_id=1, source_target_pairs={{0,1},{1,2},{2,3},{3,4},{4,5},{5,6},{6,7},{7,8},{8,9},{9,10},{10,1... | collective-permute-start | bytes 44 | tf_op jit(solution)/shard_map/ppermute | solution.py:313
  52.7 1.3 collective-permute-start.13
  54.0 6.7 %collective-permute-start.12 = (f32[3,2,4,128]{3,2,1,0:T(4,128)}, f32[3,2,4,128]{3,2,1,0:T(4,128)}, u32[]{:S(2)}, u32[]{:S(2)}) collective-permute-start(f32[3,2,4,128]{3,2,1,0:T(4,128)} %get-tuple-element.172), channel_id=1, source_target_pairs={{0,1},{1,2},{2,3},{3,4},{4,5},{5,6},{6,7},{7,8},{8,9},{9,10},{10,1... | collective-permute-start | bytes 36872 | tf_op jit(solution)/shard_map/ppermute | solution.py:319
  60.6 2.8 %collective-permute-done.8 = f32[1,3]{1,0:T(1,128)S(1)} collective-permute-done((f32[1,3]{1,0:T(1,128)}, f32[1,3]{1,0:T(1,128)S(1)}, u32[]{:S(2)}, u32[]{:S(2)}) %collective-permute-start.8) | collective-permute-done | bytes 44 | tf_op jit(solution)/shard_map/ppermute | solution.py:313
  64.0 3.6 %collective-permute-start.9 = (f32[2,3]{1,0:T(2,128)S(1)}, f32[2,3]{1,0:T(2,128)S(1)}, u32[]{:S(2)}, u32[]{:S(2)}) collective-permute-start(f32[2,3]{1,0:T(2,128)S(1)} %pad_maximum_fusion.13), channel_id=1, source_target_pairs={{0,2},{1,3},{2,4},{3,5},{4,6},{5,7},{6,8},{7,9},{8,10},{9,11},{10,... | collective-permute-start | bytes 80 | tf_op jit(solution)/shard_map/ppermute | solution.py:313
  67.6 6.6 %collective-permute-done.9 = f32[2,3]{1,0:T(2,128)S(1)} collective-permute-done((f32[2,3]{1,0:T(2,128)S(1)}, f32[2,3]{1,0:T(2,128)S(1)}, u32[]{:S(2)}, u32[]{:S(2)}) %collective-permute-start.9) | collective-permute-done | bytes 56 | tf_op jit(solution)/shard_map/ppermute | solution.py:313
  74.8 4.9 %collective-permute-start.10 = (f32[4,3]{1,0:T(4,128)S(1)}, f32[4,3]{1,0:T(4,128)S(1)}, u32[]{:S(2)}, u32[]{:S(2)}) collective-permute-start(f32[4,3]{1,0:T(4,128)S(1)} %pad_maximum_fusion.12), channel_id=1, source_target_pairs={{0,4},{1,5},{2,6},{3,7},{4,8},{5,9},{6,10},{7,11},{8,0},{9,1},{10,... | collective-permute-start | bytes 152 | tf_op jit(solution)/shard_map/ppermute | solution.py:313
  79.7 5.1 %collective-permute-done.10 = f32[4,3]{1,0:T(4,128)S(1)} collective-permute-done((f32[4,3]{1,0:T(4,128)S(1)}, f32[4,3]{1,0:T(4,128)S(1)}, u32[]{:S(2)}, u32[]{:S(2)}) %collective-permute-start.10) | collective-permute-done | bytes 80 | tf_op jit(solution)/shard_map/ppermute | solution.py:313
  84.8 7.8 %collective-permute-start.11 = (f32[4,3]{1,0:T(4,128)S(1)}, f32[4,3]{1,0:T(4,128)}, u32[]{:S(2)}, u32[]{:S(2)}) collective-permute-start(f32[4,3]{1,0:T(4,128)S(1)} %pad_maximum_fusion.12), channel_id=1, source_target_pairs={{0,8},{1,9},{2,10},{3,11},{4,0},{5,1},{6,2},{7,3},{8,4},{9,5},{10,... | collective-permute-start | bytes 152 | tf_op jit(solution)/shard_map/ppermute | solution.py:313
  92.7 1.7 %collective-permute-done.11 = f32[4,3]{1,0:T(4,128)} collective-permute-done((f32[4,3]{1,0:T(4,128)S(1)}, f32[4,3]{1,0:T(4,128)}, u32[]{:S(2)}, u32[]{:S(2)}) %collective-permute-start.11) | collective-permute-done | bytes 80 | tf_op jit(solution)/shard_map/ppermute | solution.py:313
  94.3 1.4 concatenate.448
  110.1 6.8 %collective-permute-start.14 = (f32[6,2,40,128]{3,2,1,0:T(8,128)S(1)}, f32[6,2,40,128]{3,2,1,0:T(8,128)S(1)}, u32[]{:S(2)}, u32[]{:S(2)}) collective-permute-start(f32[6,2,40,128]{3,2,1,0:T(8,128)S(1)} %pad_maximum_fusion.2), channel_id=1, source_target_pairs={{0,24},{12,36},{24,48},{36,60},{48,72},{60,84},{72,96},{84,108},{9... | collective-permute-start | bytes 737288 | tf_op jit(solution)/shard_map/ppermute | solution.py:210
  116.9 1.9 %collective-permute-start.15 = (f32[6,2,40,128]{3,2,1,0:T(8,128)S(1)}, f32[6,2,40,128]{3,2,1,0:T(8,128)S(1)}, u32[]{:S(2)}, u32[]{:S(2)}) collective-permute-start(f32[6,2,40,128]{3,2,1,0:T(8,128)S(1)} %pad_maximum_fusion.2), channel_id=1, source_target_pairs={{0,12},{12,24},{24,36},{36,48},{48,60},{60,72},{72,84},{84,96},{96... | collective-permute-start | bytes 737288 | tf_op jit(solution)/shard_map/ppermute | solution.py:210
  118.8 3.6 %collective-permute-start.16 = (f32[6,2,40,128]{3,2,1,0:T(8,128)S(1)}, f32[6,2,40,128]{3,2,1,0:T(8,128)S(1)}, u32[]{:S(2)}, u32[]{:S(2)}) collective-permute-start(f32[6,2,40,128]{3,2,1,0:T(8,128)S(1)} %pad_maximum_fusion.2), channel_id=1, source_target_pairs={{12,0},{24,12},{36,24},{48,36},{60,48},{72,60},{84,72},{96,84},{10... | collective-permute-start | bytes 737288 | tf_op jit(solution)/shard_map/ppermute | solution.py:211
  122.5 2.1 %collective-permute-start.17 = (f32[6,2,40,128]{3,2,1,0:T(8,128)S(1)}, f32[6,2,40,128]{3,2,1,0:T(8,128)S(1)}, u32[]{:S(2)}, u32[]{:S(2)}) collective-permute-start(f32[6,2,40,128]{3,2,1,0:T(8,128)S(1)} %pad_maximum_fusion.2), channel_id=1, source_target_pairs={{24,0},{36,12},{48,24},{60,36},{72,48},{84,60},{96,72},{108,84},{1... | collective-permute-start | bytes 737288 | tf_op jit(solution)/shard_map/ppermute | solution.py:211
  125.4 2.0 %collective-permute-done.16 = f32[6,2,40,128]{3,2,1,0:T(8,128)S(1)} collective-permute-done((f32[6,2,40,128]{3,2,1,0:T(8,128)S(1)}, f32[6,2,40,128]{3,2,1,0:T(8,128)S(1)}, u32[]{:S(2)}, u32[]{:S(2)}) %collective-permute-start.16) | collective-permute-done | bytes 245792 | tf_op jit(solution)/shard_map/ppermute | solution.py:211
  127.5 9.2 %collective-permute-done.17 = f32[6,2,40,128]{3,2,1,0:T(8,128)S(1)} collective-permute-done((f32[6,2,40,128]{3,2,1,0:T(8,128)S(1)}, f32[6,2,40,128]{3,2,1,0:T(8,128)S(1)}, u32[]{:S(2)}, u32[]{:S(2)}) %collective-permute-start.17) | collective-permute-done | bytes 245792 | tf_op jit(solution)/shard_map/ppermute | solution.py:211
  143.5 1.6 %slice_add_fusion.8 = f32[3,2,32,128]{3,2,1,0:T(8,128)} fusion(f32[3,4,34,128]{3,2,1,0:T(8,128)S(1)} %get-tuple-element.6, f32[3,6,36,128]{3,2,1,0:T(8,128)S(1)} %get-tuple-element.10, f32[3,8,38,128]{3,2,1,0:T(8,128)S(1)} %get-tuple-element.14, f32[3,4,34,128]{3,2,1,0:T(8,128)} %copy-done.5, f32[3,6,36,128]{3,2,1,0:T(8,128)S(1)} %get-tuple-element.54, ...), kind=kLoop, calls=%fused_computation.248 | loop fusion | flops 147456 | bytes 737280 | tf_op jit(solution)/shard_map/add | solution.py:252
  (250 shorter events, 38.8 us)
Async XLA Ops:
  0.6 22.3 %copy-start.24 = (f32[2,32,128]{2,1,0:T(8,128)S(1)}, f32[2,32,128]{2,1,0:T(8,128)}, u32[]{:S(2)}) copy-start(f32[2,32,128]{2,1,0:T(8,128)} %param.6) | copy-start | bytes 98308
  0.6 22.3 %copy-start.25 = (f32[2,32,128]{2,1,0:T(8,128)S(1)}, f32[2,32,128]{2,1,0:T(8,128)}, u32[]{:S(2)}) copy-start(f32[2,32,128]{2,1,0:T(8,128)} %param.5) | copy-start | bytes 98308
  0.7 22.3 %copy-start.22 = (f32[3,2,32,128]{3,2,1,0:T(8,128)S(1)}, f32[3,2,32,128]{3,2,1,0:T(8,128)}, u32[]{:S(2)}) copy-start(f32[3,2,32,128]{3,2,1,0:T(8,128)} %param.4) | copy-start | bytes 294916
  1.6 21.2 %collective-permute-start = (f32[5,2,32,128]{3,2,1,0:T(8,128)S(1)}, f32[5,2,32,128]{3,2,1,0:T(8,128)S(1)}, u32[]{:S(2)}, u32[]{:S(2)}) collective-permute-start(f32[5,2,32,128]{3,2,1,0:T(8,128)S(1)} %pad_maximum_fusion.3), channel_id=1, source_target_pairs={{0,24},{12,36},{24,48},{36,60},{48,72},{60,84},{72,96},{84,108},{9... | collective-permute-start | bytes 491528 | tf_op jit(solution)/shard_map/ppermute | solution.py:210
  6.3 16.6 %collective-permute-start.1 = (f32[5,2,32,128]{3,2,1,0:T(8,128)S(1)}, f32[5,2,32,128]{3,2,1,0:T(8,128)S(1)}, u32[]{:S(2)}, u32[]{:S(2)}) collective-permute-start(f32[5,2,32,128]{3,2,1,0:T(8,128)S(1)} %pad_maximum_fusion.3), channel_id=1, source_target_pairs={{0,12},{12,24},{24,36},{36,48},{48,60},{60,72},{72,84},{84,96},{96... | collective-permute-start | bytes 491528 | tf_op jit(solution)/shard_map/ppermute | solution.py:210
  8.2 14.8 %collective-permute-start.2 = (f32[5,2,32,128]{3,2,1,0:T(8,128)S(1)}, f32[5,2,32,128]{3,2,1,0:T(8,128)S(1)}, u32[]{:S(2)}, u32[]{:S(2)}) collective-permute-start(f32[5,2,32,128]{3,2,1,0:T(8,128)S(1)} %pad_maximum_fusion.3), channel_id=1, source_target_pairs={{12,0},{24,12},{36,24},{48,36},{60,48},{72,60},{84,72},{96,84},{10... | collective-permute-start | bytes 491528 | tf_op jit(solution)/shard_map/ppermute | solution.py:211
  11.8 11.6 %collective-permute-start.3 = (f32[5,2,32,128]{3,2,1,0:T(8,128)S(1)}, f32[5,2,32,128]{3,2,1,0:T(8,128)S(1)}, u32[]{:S(2)}, u32[]{:S(2)}) collective-permute-start(f32[5,2,32,128]{3,2,1,0:T(8,128)S(1)} %pad_maximum_fusion.3), channel_id=1, source_target_pairs={{24,0},{36,12},{48,24},{60,36},{72,48},{84,60},{96,72},{108,84},{1... | collective-permute-start | bytes 491528 | tf_op jit(solution)/shard_map/ppermute | solution.py:211
  13.8 18.2 %copy-start.30 = (s32[128]{0:T(128)}, s32[128]{0:T(128)S(1)}, u32[]{:S(2)}) copy-start(s32[128]{0:T(128)S(1)} %and_select_fusion.2) | copy-start | bytes 1540
  23.5 7.0 %collective-permute-start.5 = (f32[5,10,4,128]{3,2,1,0:T(4,128)S(1)}, f32[5,10,4,128]{3,2,1,0:T(4,128)S(1)}, u32[]{:S(2)}, u32[]{:S(2)}) collective-permute-start(f32[5,10,4,128]{3,2,1,0:T(4,128)S(1)} %get-tuple-element.80), channel_id=1, source_target_pairs={{1,0},{2,1},{3,2},{4,3},{5,4},{6,5},{7,6},{8,7},{9,8},{10,9},{11,1... | collective-permute-start | bytes 307208 | tf_op jit(solution)/shard_map/ppermute | solution.py:220
  24.8 7.1 %collective-permute-start.4 = (f32[5,10,4,128]{3,2,1,0:T(4,128)S(1)}, f32[5,10,4,128]{3,2,1,0:T(4,128)S(1)}, u32[]{:S(2)}, u32[]{:S(2)}) collective-permute-start(f32[5,10,4,128]{3,2,1,0:T(4,128)S(1)} %get-tuple-element.79), channel_id=1, source_target_pairs={{0,1},{1,2},{2,3},{3,4},{4,5},{5,6},{6,7},{7,8},{8,9},{9,10},{10,1... | collective-permute-start | bytes 307208 | tf_op jit(solution)/shard_map/ppermute | solution.py:219
  32.1 2.5 %copy-start.18 = (f32[6,36,127]{2,1,0:T(8,128)}, f32[6,36,127]{2,1,0:T(8,128)S(1)}, u32[]{:S(2)}) copy-start(f32[6,36,127]{2,1,0:T(8,128)S(1)} %slice.2168) | copy-start | bytes 329188
  32.3 3.4 %copy-start.20 = (f32[4,34,127]{2,1,0:T(8,128)}, f32[4,34,127]{2,1,0:T(8,128)S(1)}, u32[]{:S(2)}) copy-start(f32[4,34,127]{2,1,0:T(8,128)S(1)} %slice.2213) | copy-start | bytes 207268
  32.4 4.4 %copy-start.26 = (f32[2,32,127]{2,1,0:T(8,128)}, f32[2,32,127]{2,1,0:T(8,128)S(1)}, u32[]{:S(2)}) copy-start(f32[2,32,127]{2,1,0:T(8,128)S(1)} %slice.2256) | copy-start | bytes 97540
  40.9 51.8 %copy-start.23 = (f32[5,1,1,16,64]{4,3,1,2,0:T(8,128)}, f32[5,1,1,16,64]{4,3,1,2,0:T(8,128)S(1)}, u32[]{:S(2)}) copy-start(f32[5,1,1,16,64]{4,3,1,2,0:T(8,128)S(1)} %get-tuple-element.200) | copy-start | bytes 61444
  40.9 60.1 %collective-permute-start.7 = (f32[5,1,16,64]{3,2,0,1:T(8,128)}, f32[5,1,16,64]{3,2,0,1:T(8,128)}, u32[]{:S(2)}, u32[]{:S(2)}) collective-permute-start(f32[5,1,16,64]{3,2,0,1:T(8,128)} %get-tuple-element.201), channel_id=1, source_target_pairs={{1,0},{2,1},{3,2},{4,3},{5,4},{6,5},{7,6},{8,7},{9,8},{10,9},{11,1... | collective-permute-start | bytes 61448 | tf_op jit(solution)/shard_map/ppermute | solution.py:323
  42.2 58.0 %collective-permute-start.6 = (f32[5,1,16,64]{3,2,0,1:T(8,128)}, f32[5,1,16,64]{3,2,0,1:T(8,128)}, u32[]{:S(2)}, u32[]{:S(2)}) collective-permute-start(f32[5,1,16,64]{3,2,0,1:T(8,128)} %get-tuple-element.201), channel_id=1, source_target_pairs={{0,1},{1,2},{2,3},{3,4},{4,5},{5,6},{6,7},{7,8},{8,9},{9,10},{10,1... | collective-permute-start | bytes 61448 | tf_op jit(solution)/shard_map/ppermute | solution.py:322
  49.0 14.4 %collective-permute-start.8 = (f32[1,3]{1,0:T(1,128)}, f32[1,3]{1,0:T(1,128)S(1)}, u32[]{:S(2)}, u32[]{:S(2)}) collective-permute-start(f32[1,3]{1,0:T(1,128)} %bitcast.344), channel_id=1, source_target_pairs={{0,1},{1,2},{2,3},{3,4},{4,5},{5,6},{6,7},{7,8},{8,9},{9,10},{10,1... | collective-permute-start | bytes 44 | tf_op jit(solution)/shard_map/ppermute | solution.py:313
  52.7 56.6 %collective-permute-start.13 = (f32[3,2,4,128]{3,2,1,0:T(4,128)}, f32[3,2,4,128]{3,2,1,0:T(4,128)}, u32[]{:S(2)}, u32[]{:S(2)}) collective-permute-start(f32[3,2,4,128]{3,2,1,0:T(4,128)} %get-tuple-element.173), channel_id=1, source_target_pairs={{1,0},{2,1},{3,2},{4,3},{5,4},{6,5},{7,6},{8,7},{9,8},{10,9},{11,1... | collective-permute-start | bytes 36872 | tf_op jit(solution)/shard_map/ppermute | solution.py:320
  54.0 55.3 %collective-permute-start.12 = (f32[3,2,4,128]{3,2,1,0:T(4,128)}, f32[3,2,4,128]{3,2,1,0:T(4,128)}, u32[]{:S(2)}, u32[]{:S(2)}) collective-permute-start(f32[3,2,4,128]{3,2,1,0:T(4,128)} %get-tuple-element.172), channel_id=1, source_target_pairs={{0,1},{1,2},{2,3},{3,4},{4,5},{5,6},{6,7},{7,8},{8,9},{9,10},{10,1... | collective-permute-start | bytes 36872 | tf_op jit(solution)/shard_map/ppermute | solution.py:319
  64.0 10.2 %collective-permute-start.9 = (f32[2,3]{1,0:T(2,128)S(1)}, f32[2,3]{1,0:T(2,128)S(1)}, u32[]{:S(2)}, u32[]{:S(2)}) collective-permute-start(f32[2,3]{1,0:T(2,128)S(1)} %pad_maximum_fusion.13), channel_id=1, source_target_pairs={{0,2},{1,3},{2,4},{3,5},{4,6},{5,7},{6,8},{7,9},{8,10},{9,11},{10,... | collective-permute-start | bytes 80 | tf_op jit(solution)/shard_map/ppermute | solution.py:313
  74.8 10.0 %collective-permute-start.10 = (f32[4,3]{1,0:T(4,128)S(1)}, f32[4,3]{1,0:T(4,128)S(1)}, u32[]{:S(2)}, u32[]{:S(2)}) collective-permute-start(f32[4,3]{1,0:T(4,128)S(1)} %pad_maximum_fusion.12), channel_id=1, source_target_pairs={{0,4},{1,5},{2,6},{3,7},{4,8},{5,9},{6,10},{7,11},{8,0},{9,1},{10,... | collective-permute-start | bytes 152 | tf_op jit(solution)/shard_map/ppermute | solution.py:313
  84.8 7.8 %copy-start.34 = (f32[4,3]{1,0:T(4,128)}, f32[4,3]{1,0:T(4,128)S(1)}, u32[]{:S(2)}) copy-start(f32[4,3]{1,0:T(4,128)S(1)} %collective-permute-done.10) | copy-start | bytes 148
  84.8 9.5 %collective-permute-start.11 = (f32[4,3]{1,0:T(4,128)S(1)}, f32[4,3]{1,0:T(4,128)}, u32[]{:S(2)}, u32[]{:S(2)}) collective-permute-start(f32[4,3]{1,0:T(4,128)S(1)} %pad_maximum_fusion.12), channel_id=1, source_target_pairs={{0,8},{1,9},{2,10},{3,11},{4,0},{5,1},{6,2},{7,3},{8,4},{9,5},{10,... | collective-permute-start | bytes 152 | tf_op jit(solution)/shard_map/ppermute | solution.py:313
  97.1 8.4 %copy-start.33 = (pred[3]{0:T(512)(128)(4,1)S(1)}, pred[3]{0:T(512)(128)(4,1)}, u32[]{:S(2)}) copy-start(pred[3]{0:T(512)(128)(4,1)} %compare_and_fusion.2) | copy-start | bytes 13
  101.8 3.8 %copy-start.29 = (f32[3]{0:T(128)S(1)}, f32[3]{0:T(128)}, u32[]{:S(2)}) copy-start(f32[3]{0:T(128)} %get-tuple-element.205) | copy-start | bytes 40
  101.8 3.9 %copy-start.28 = (f32[3]{0:T(128)S(1)}, f32[3]{0:T(128)}, u32[]{:S(2)}) copy-start(f32[3]{0:T(128)} %get-tuple-element.204) | copy-start | bytes 40
  110.1 14.5 %collective-permute-start.14 = (f32[6,2,40,128]{3,2,1,0:T(8,128)S(1)}, f32[6,2,40,128]{3,2,1,0:T(8,128)S(1)}, u32[]{:S(2)}, u32[]{:S(2)}) collective-permute-start(f32[6,2,40,128]{3,2,1,0:T(8,128)S(1)} %pad_maximum_fusion.2), channel_id=1, source_target_pairs={{0,24},{12,36},{24,48},{36,60},{48,72},{60,84},{72,96},{84,108},{9... | collective-permute-start | bytes 737288 | tf_op jit(solution)/shard_map/ppermute | solution.py:210
  116.9 7.7 %collective-permute-start.15 = (f32[6,2,40,128]{3,2,1,0:T(8,128)S(1)}, f32[6,2,40,128]{3,2,1,0:T(8,128)S(1)}, u32[]{:S(2)}, u32[]{:S(2)}) collective-permute-start(f32[6,2,40,128]{3,2,1,0:T(8,128)S(1)} %pad_maximum_fusion.2), channel_id=1, source_target_pairs={{0,12},{12,24},{24,36},{36,48},{48,60},{60,72},{72,84},{84,96},{96... | collective-permute-start | bytes 737288 | tf_op jit(solution)/shard_map/ppermute | solution.py:210
  118.8 8.6 %collective-permute-start.16 = (f32[6,2,40,128]{3,2,1,0:T(8,128)S(1)}, f32[6,2,40,128]{3,2,1,0:T(8,128)S(1)}, u32[]{:S(2)}, u32[]{:S(2)}) collective-permute-start(f32[6,2,40,128]{3,2,1,0:T(8,128)S(1)} %pad_maximum_fusion.2), channel_id=1, source_target_pairs={{12,0},{24,12},{36,24},{48,36},{60,48},{72,60},{84,72},{96,84},{10... | collective-permute-start | bytes 737288 | tf_op jit(solution)/shard_map/ppermute | solution.py:211
  122.5 14.2 %collective-permute-start.17 = (f32[6,2,40,128]{3,2,1,0:T(8,128)S(1)}, f32[6,2,40,128]{3,2,1,0:T(8,128)S(1)}, u32[]{:S(2)}, u32[]{:S(2)}) collective-permute-start(f32[6,2,40,128]{3,2,1,0:T(8,128)S(1)} %pad_maximum_fusion.2), channel_id=1, source_target_pairs={{24,0},{36,12},{48,24},{60,36},{72,48},{84,60},{96,72},{108,84},{1... | collective-permute-start | bytes 737288 | tf_op jit(solution)/shard_map/ppermute | solution.py:211
  143.4 2.0 %copy-start.7 = (f32[2,32,128]{2,1,0:T(8,128)S(1)}, f32[2,32,128]{2,1,0:T(8,128)}, u32[]{:S(2)}) copy-start(f32[2,32,128]{2,1,0:T(8,128)} %copy-done.6) | copy-start | bytes 98308
  143.4 2.0 %copy-start.9 = (f32[2,32,128]{2,1,0:T(8,128)S(1)}, f32[2,32,128]{2,1,0:T(8,128)}, u32[]{:S(2)}) copy-start(f32[2,32,128]{2,1,0:T(8,128)} %copy-done.8) | copy-start | bytes 98308
  (21 other events, 24.0 us)

commit v4 on v2

--- a/solution.py
+++ b/solution.py
@@ -304,9 +304,20 @@
     members = same_group(starts)
     cells_dev = coarse_x * coarse_y * coarse_z
 
+    count_x = lax.axis_size("gx")
     sums = coarse_res.sum(axis=(1, 2, 3))
-    slots = jnp.where(jnp.arange(count_y)[:, None] == gy, sums[None, :], 0.0)
+    own_info = jnp.concatenate([sums, starts.astype(jnp.float32)])
+    side = (depth + 2) // 2
+    lows, highs = [], []
+    for dx in range(side, 0, -1):
+        lows.append(lax.ppermute(own_info, "gx", [(i, i + dx) for i in range(count_x - dx)]))
+        highs.append(lax.ppermute(own_info, "gx", [(i + dx, i) for i in range(count_x - dx)]))
+    column_info = jnp.stack(lows + [own_info] + highs[::-1])
+    slots = jnp.where(
+        jnp.arange(count_y)[None, :, None] == gy, column_info[:, None, :3], 0.0
+    )
     all_sums = lax.psum(slots, "gy")
+    column_starts = jnp.round(column_info[:, 3:]).astype(jnp.int32)
 
     forward = [(i, i + 1) for i in range(count_y - 1)]
     backward = [(i + 1, i) for i in range(count_y - 1)]
@@ -336,12 +347,7 @@
     smoothed, coarse_left = smooth(
         jnp.zeros_like(window_res), window_res, coarse_inverse, coarse_apply, COARSE_SWEEPS
     )
-    totals = jnp.sum(members[:, :, None] * all_sums[None, :, :], axis=1)
-    group_cells = jnp.sum(members, axis=1) * cells_dev
-    group_shift = totals / (SHIFT_SCALE * group_cells[:, None])
-    window_shift = jnp.take(group_shift, jnp.clip(owners, 0, count_y - 1), axis=0)
-    window_shift = jnp.where(valid[:, None], window_shift, 0.0)
-    correction = smoothed + window_shift.T[:, :, None, None, None]
+    correction = smoothed
     correction = jnp.moveaxis(correction, 1, 2).reshape(3, coarse_x, 3 * coarse_y, coarse_z)
     reach_c = (depth + 2) // 2
     corr_y = correction[:, :, coarse_y - reach_c : 2 * coarse_y + reach_c, :]
@@ -356,6 +362,22 @@
     joined = halo_x(jnp.concatenate([residual_y, fine_corr], axis=0), fine_reach)
     residual_ext = crop(joined[0:3], 1)
     fine_corr = joined[3:6]
+
+    column_members = same_group(column_starts)
+    totals = jnp.sum(column_members[:, :, :, None] * all_sums[:, None, :, :], axis=2)
+    group_cells = jnp.sum(column_members, axis=2) * cells_dev
+    group_shift = totals / (SHIFT_SCALE * group_cells[:, :, None])
+    columns = lax.axis_index("gx") + jnp.arange(-side, side + 1)
+    column_ok = (columns >= 0) & (columns < count_x)
+    owners = gy - 1 + jnp.arange(3)
+    owner_ok = (owners >= 0) & (owners < count_y)
+    block_shift = jnp.take(group_shift, jnp.clip(owners, 0, count_y - 1), axis=1)
+    block_shift = jnp.where(column_ok[:, None, None] & owner_ok[None, :, None], block_shift, 0.0)
+    block_shift = jnp.repeat(jnp.moveaxis(block_shift, 2, 0), 2, axis=1)
+    block_shift = block_shift[:, 2 * side - fine_reach : block_shift.shape[1] - (2 * side - fine_reach)]
+    rows = jnp.array([fine_reach, width_y, fine_reach])
+    block_shift = jnp.repeat(block_shift, rows, axis=2, total_repeat_length=width_y + 2 * fine_reach)
+    fine_corr = fine_corr + block_shift[:, :, :, None]
     solution = solution + crop(fine_corr, fine_reach)
     residual_ext = residual_ext - apply_ext(fine_corr, mu_ext, lam_ext, 1.0)
     solution, residual = smooth_ext(

time: 136 us -> 192 us (1.41)
  blocking collectives: 31.7 us -> 51.7 us
  starting transfers between devices: 45.4 us -> 60.6 us
  local copies, waits for them, and re-layouts: 12 us -> 25.7 us
  other arithmetic: 27.6 us -> 35.8 us
    psum x1, blocking collectives: 31.7 us -> 51.7 us  [shards(): all_sums = lax.psum(slots, 'gy')]
    ppermute x0 -> x4, starting transfers between devices: none -> 14.1 us  [the longest x2 8.51 us: shards(): lax.ppermute(own_info, 'gx', [(i, i + dx) for i in range(count_x - dx)])]
    gather x1 -> x3, local copies, waits for them, and re-layouts: 0.68 us -> 4.97 us  [the longest x2 2.95 us: shards(): jnp.repeat(block_shift, rows, axis=2, total_repeat_length=width_y + 2 * f...]
    unnamed x76 -> x104, local copies, waits for them, and re-layouts: 3.78 us -> 7.16 us
    ppermute x4, waiting for transfers between devices: 12.4 us -> 10.1 us  [halo_x(): highs.append(lax.ppermute(array[..., :need, :, :], 'gx', backward))]
  transfers between devices with their start and end apart: 14 -> 18, of which waited for: 5 -> 6; matrix products, arithmetic and copies ran while one was open for 16% -> 22% of each run, Pallas kernels for 0% -> 0%
where the time goes in v4:
time: 192 us; the launch traced here: 190 us
  starting transfers between devices  60.6 us (32%)
  blocking collectives  51.7 us (27%)
  other arithmetic  35.8 us (19%)
  local copies, waits for them, and re-layouts  25.7 us (13%)
  waiting for transfers between devices  12.2 us (6%)
  matrix products  2.04 us (1%)
  between operations  2.04 us (1%)
    psum x1, blocking collectives, shards(): all_sums = lax.psum(slots, 'gy')  51.7 us
    ppermute x4, starting transfers between devices, halo_x(): lows.append(lax.ppermute(array[..., width - need:, :, :], 'gx', forward))  15.7 us
    ppermute x4, starting transfers between devices, halo_x(): highs.append(lax.ppermute(array[..., :need, :, :], 'gx', backward))  11.4 us
    ppermute x4, waiting for transfers between devices, halo_x(): highs.append(lax.ppermute(array[..., :need, :, :], 'gx', backward))  10.1 us
    ppermute x2, starting transfers between devices, shards(): lax.ppermute(own_info, 'gx', [(i, i + dx) for i in range(count_x - dx)])  8.51 us
    unnamed x104, local copies, waits for them, and re-layouts  7.16 us
    ppermute x2, starting transfers between devices, shards(): lax.ppermute(own_info, 'gx', [(i + dx, i) for i in range(count_x - dx)])  5.55 us
    ppermute x1, starting transfers between devices, shards(): pack_below = lax.ppermute(coarse_pack, 'gy', forward)  5.55 us
  transfers between devices with their start and end apart: 18, of which 6 were waited for; matrix products, arithmetic and copies ran while one was open for 22% of the time, Pallas kernels for 0%

profile of v4, /device:TPU:30, one launch (start us, length us, event | category | flops | bytes accessed | tf_op | source)
XLA Modules:
  0.0 190.1 jit_solution(3036527177823521225)
XLA Ops:
  1.6 4.6 %collective-permute-start = (f32[5,2,32,128]{3,2,1,0:T(8,128)S(1)}, f32[5,2,32,128]{3,2,1,0:T(8,128)S(1)}, u32[]{:S(2)}, u32[]{:S(2)}) collective-permute-start(f32[5,2,32,128]{3,2,1,0:T(8,128)S(1)} %pad_maximum_fusion.3), channel_id=1, source_target_pairs={{0,24},{12,36},{24,48},{36,60},{48,72},{60,84},{72,96},{84,108},{9... | collective-permute-start | bytes 491528 | tf_op jit(solution)/shard_map/ppermute | solution.py:210
  6.3 1.9 %collective-permute-start.1 = (f32[5,2,32,128]{3,2,1,0:T(8,128)S(1)}, f32[5,2,32,128]{3,2,1,0:T(8,128)S(1)}, u32[]{:S(2)}, u32[]{:S(2)}) collective-permute-start(f32[5,2,32,128]{3,2,1,0:T(8,128)S(1)} %pad_maximum_fusion.3), channel_id=1, source_target_pairs={{0,12},{12,24},{24,36},{36,48},{48,60},{60,72},{72,84},{84,96},{96... | collective-permute-start | bytes 491528 | tf_op jit(solution)/shard_map/ppermute | solution.py:210
  8.2 3.6 %collective-permute-start.2 = (f32[5,2,32,128]{3,2,1,0:T(8,128)S(1)}, f32[5,2,32,128]{3,2,1,0:T(8,128)S(1)}, u32[]{:S(2)}, u32[]{:S(2)}) collective-permute-start(f32[5,2,32,128]{3,2,1,0:T(8,128)S(1)} %pad_maximum_fusion.3), channel_id=1, source_target_pairs={{12,0},{24,12},{36,24},{48,36},{60,48},{72,60},{84,72},{96,84},{10... | collective-permute-start | bytes 491528 | tf_op jit(solution)/shard_map/ppermute | solution.py:211
  11.8 1.9 %collective-permute-start.3 = (f32[5,2,32,128]{3,2,1,0:T(8,128)S(1)}, f32[5,2,32,128]{3,2,1,0:T(8,128)S(1)}, u32[]{:S(2)}, u32[]{:S(2)}) collective-permute-start(f32[5,2,32,128]{3,2,1,0:T(8,128)S(1)} %pad_maximum_fusion.3), channel_id=1, source_target_pairs={{24,0},{36,12},{48,24},{60,36},{72,48},{84,60},{96,72},{108,84},{1... | collective-permute-start | bytes 491528 | tf_op jit(solution)/shard_map/ppermute | solution.py:211
  17.6 1.4 compare_select_fusion.5
  24.8 4.9 %collective-permute-start.4 = (f32[5,10,4,128]{3,2,1,0:T(4,128)S(1)}, f32[5,10,4,128]{3,2,1,0:T(4,128)S(1)}, u32[]{:S(2)}, u32[]{:S(2)}) collective-permute-start(f32[5,10,4,128]{3,2,1,0:T(4,128)S(1)} %get-tuple-element.88), channel_id=1, source_target_pairs={{0,1},{1,2},{2,3},{3,4},{4,5},{5,6},{6,7},{7,8},{8,9},{9,10},{10,1... | collective-permute-start | bytes 307208 | tf_op jit(solution)/shard_map/ppermute | solution.py:219
  30.4 1.5 collective-permute-done.4
  38.1 1.5 reduce_sum.63
  39.5 1.4 fusion.450
  42.2 5.5 %collective-permute-start.8 = (f32[5,1,16,64]{3,2,0,1:T(8,128)}, f32[5,1,16,64]{3,2,0,1:T(8,128)}, u32[]{:S(2)}, u32[]{:S(2)}) collective-permute-start(f32[5,1,16,64]{3,2,0,1:T(8,128)} %get-tuple-element.213), channel_id=1, source_target_pairs={{0,1},{1,2},{2,3},{3,4},{4,5},{5,6},{6,7},{7,8},{8,9},{9,10},{10,1... | collective-permute-start | bytes 61448 | tf_op jit(solution)/shard_map/ppermute | solution.py:328
  49.1 6.6 %collective-permute-start.14 = (f32[15]{0:T(128)S(1)}, f32[15]{0:T(128)S(1)}, u32[]{:S(2)}, u32[]{:S(2)}) collective-permute-start(f32[15]{0:T(128)S(1)} %pad_maximum_fusion.14), channel_id=1, source_target_pairs={{0,24},{12,36},{24,48},{36,60},{48,72},{60,84},{72,96},{84,108},{9... | collective-permute-start | bytes 188 | tf_op jit(solution)/shard_map/ppermute | solution.py:313
  55.7 1.9 %collective-permute-start.15 = (f32[15]{0:T(128)S(1)}, f32[15]{0:T(128)S(1)}, u32[]{:S(2)}, u32[]{:S(2)}) collective-permute-start(f32[15]{0:T(128)S(1)} %pad_maximum_fusion.14), channel_id=1, source_target_pairs={{0,12},{12,24},{24,36},{36,48},{48,60},{60,72},{72,84},{84,96},{96... | collective-permute-start | bytes 188 | tf_op jit(solution)/shard_map/ppermute | solution.py:313
  57.6 3.6 %collective-permute-start.16 = (f32[15]{0:T(128)S(1)}, f32[15]{0:T(128)S(1)}, u32[]{:S(2)}, u32[]{:S(2)}) collective-permute-start(f32[15]{0:T(128)S(1)} %pad_maximum_fusion.14), channel_id=1, source_target_pairs={{12,0},{24,12},{36,24},{48,36},{60,48},{72,60},{84,72},{96,84},{10... | collective-permute-start | bytes 188 | tf_op jit(solution)/shard_map/ppermute | solution.py:314
  61.9 1.9 %collective-permute-start.17 = (f32[15]{0:T(128)S(1)}, f32[15]{0:T(128)S(1)}, u32[]{:S(2)}, u32[]{:S(2)}) collective-permute-start(f32[15]{0:T(128)S(1)} %pad_maximum_fusion.14), channel_id=1, source_target_pairs={{24,0},{36,12},{48,24},{60,36},{72,48},{84,60},{96,72},{108,84},{1... | collective-permute-start | bytes 188 | tf_op jit(solution)/shard_map/ppermute | solution.py:314
  65.2 5.1 %collective-permute-start.6 = (f32[3,2,4,128]{3,2,1,0:T(4,128)}, f32[3,2,4,128]{3,2,1,0:T(4,128)}, u32[]{:S(2)}, u32[]{:S(2)}) collective-permute-start(f32[3,2,4,128]{3,2,1,0:T(4,128)} %get-tuple-element.184), channel_id=1, source_target_pairs={{0,1},{1,2},{2,3},{3,4},{4,5},{5,6},{6,7},{7,8},{8,9},{9,10},{10,1... | collective-permute-start | bytes 36872 | tf_op jit(solution)/shard_map/ppermute | solution.py:325
  71.9 1.4 broadcast_select_fusion
  73.3 51.7 %psum.7 = f32[5,12,3]{1,2,0:T(4,128)} all-reduce(f32[5,12,3]{1,2,0:T(4,128)} %broadcast_select_fusion), channel_id=1, replica_groups=mesh['gx'=64,'gy'=12] {'gy'}, use_global_device_ids=true, to_apply=%region_9.10 | all-reduce | flops 180 | bytes 1440 | tf_op jit(solution)/shard_map/psum | solution.py:319
  125.0 1.3 convert_select_fusion
  127.4 1.4 multiply_reduce_fusion
  128.8 1.4 copy.148
  140.7 1.4 pad_maximum_fusion.2
  142.1 7.2 %collective-permute-start.10 = (f32[6,2,40,128]{3,2,1,0:T(8,128)}, f32[6,2,40,128]{3,2,1,0:T(8,128)}, u32[]{:S(2)}, u32[]{:S(2)}) collective-permute-start(f32[6,2,40,128]{3,2,1,0:T(8,128)} %pad_maximum_fusion.2), channel_id=1, source_target_pairs={{0,24},{12,36},{24,48},{36,60},{48,72},{60,84},{72,96},{84,108},{9... | collective-permute-start | bytes 737288 | tf_op jit(solution)/shard_map/ppermute | solution.py:210
  150.0 2.0 %gather_fusion = f32[3,5,3]{1,2,0:T(4,128)} fusion(f32[5,12,3]{0,2,1:T(4,128)} %broadcast_divide_fusion, s32[1024]{0:T(1024)} %get-tuple-element.228), kind=kCustom, calls=%fused_computation | custom fusion | bytes 372 | tf_op jit(solution)/shard_map/jit(_take)/gather | solution.py:374
  152.0 1.9 %collective-permute-start.11 = (f32[6,2,40,128]{3,2,1,0:T(8,128)}, f32[6,2,40,128]{3,2,1,0:T(8,128)}, u32[]{:S(2)}, u32[]{:S(2)}) collective-permute-start(f32[6,2,40,128]{3,2,1,0:T(8,128)} %pad_maximum_fusion.2), channel_id=1, source_target_pairs={{0,12},{12,24},{24,36},{36,48},{48,60},{60,72},{72,84},{84,96},{96... | collective-permute-start | bytes 737288 | tf_op jit(solution)/shard_map/ppermute | solution.py:210
  153.9 1.4 fusion.444
  155.3 1.4 copy.149
  158.8 1.4 gather_fusion.1
  160.2 1.6 copy.151
  161.8 3.8 %collective-permute-start.12 = (f32[6,2,40,128]{3,2,1,0:T(8,128)}, f32[6,2,40,128]{3,2,1,0:T(8,128)S(1)}, u32[]{:S(2)}, u32[]{:S(2)}) collective-permute-start(f32[6,2,40,128]{3,2,1,0:T(8,128)} %pad_maximum_fusion.2), channel_id=1, source_target_pairs={{12,0},{24,12},{36,24},{48,36},{60,48},{72,60},{84,72},{96,84},{10... | collective-permute-start | bytes 737288 | tf_op jit(solution)/shard_map/ppermute | solution.py:211
  165.6 2.1 %collective-permute-start.13 = (f32[6,2,40,128]{3,2,1,0:T(8,128)}, f32[6,2,40,128]{3,2,1,0:T(8,128)S(1)}, u32[]{:S(2)}, u32[]{:S(2)}) collective-permute-start(f32[6,2,40,128]{3,2,1,0:T(8,128)} %pad_maximum_fusion.2), channel_id=1, source_target_pairs={{24,0},{36,12},{48,24},{60,36},{72,48},{84,60},{96,72},{108,84},{1... | collective-permute-start | bytes 737288 | tf_op jit(solution)/shard_map/ppermute | solution.py:211
  170.9 9.1 %collective-permute-done.13 = f32[6,2,40,128]{3,2,1,0:T(8,128)S(1)} collective-permute-done((f32[6,2,40,128]{3,2,1,0:T(8,128)}, f32[6,2,40,128]{3,2,1,0:T(8,128)S(1)}, u32[]{:S(2)}, u32[]{:S(2)}) %collective-permute-start.13) | collective-permute-done | bytes 245792 | tf_op jit(solution)/shard_map/ppermute | solution.py:211
  186.9 1.7 slice_add_fusion.9
  (279 shorter events, 48.4 us)
Async XLA Ops:
  0.6 22.1 %copy-start.25 = (f32[2,32,128]{2,1,0:T(8,128)S(1)}, f32[2,32,128]{2,1,0:T(8,128)}, u32[]{:S(2)}) copy-start(f32[2,32,128]{2,1,0:T(8,128)} %param.9) | copy-start | bytes 98308
  0.6 22.1 %copy-start.26 = (f32[2,32,128]{2,1,0:T(8,128)S(1)}, f32[2,32,128]{2,1,0:T(8,128)}, u32[]{:S(2)}) copy-start(f32[2,32,128]{2,1,0:T(8,128)} %param.8) | copy-start | bytes 98308
  0.7 22.1 %copy-start.23 = (f32[3,2,32,128]{3,2,1,0:T(8,128)S(1)}, f32[3,2,32,128]{3,2,1,0:T(8,128)}, u32[]{:S(2)}) copy-start(f32[3,2,32,128]{3,2,1,0:T(8,128)} %param.7) | copy-start | bytes 294916
  1.6 21.0 %collective-permute-start = (f32[5,2,32,128]{3,2,1,0:T(8,128)S(1)}, f32[5,2,32,128]{3,2,1,0:T(8,128)S(1)}, u32[]{:S(2)}, u32[]{:S(2)}) collective-permute-start(f32[5,2,32,128]{3,2,1,0:T(8,128)S(1)} %pad_maximum_fusion.3), channel_id=1, source_target_pairs={{0,24},{12,36},{24,48},{36,60},{48,72},{60,84},{72,96},{84,108},{9... | collective-permute-start | bytes 491528 | tf_op jit(solution)/shard_map/ppermute | solution.py:210
  6.3 16.4 %collective-permute-start.1 = (f32[5,2,32,128]{3,2,1,0:T(8,128)S(1)}, f32[5,2,32,128]{3,2,1,0:T(8,128)S(1)}, u32[]{:S(2)}, u32[]{:S(2)}) collective-permute-start(f32[5,2,32,128]{3,2,1,0:T(8,128)S(1)} %pad_maximum_fusion.3), channel_id=1, source_target_pairs={{0,12},{12,24},{24,36},{36,48},{48,60},{60,72},{72,84},{84,96},{96... | collective-permute-start | bytes 491528 | tf_op jit(solution)/shard_map/ppermute | solution.py:210
  8.2 14.6 %collective-permute-start.2 = (f32[5,2,32,128]{3,2,1,0:T(8,128)S(1)}, f32[5,2,32,128]{3,2,1,0:T(8,128)S(1)}, u32[]{:S(2)}, u32[]{:S(2)}) collective-permute-start(f32[5,2,32,128]{3,2,1,0:T(8,128)S(1)} %pad_maximum_fusion.3), channel_id=1, source_target_pairs={{12,0},{24,12},{36,24},{48,36},{60,48},{72,60},{84,72},{96,84},{10... | collective-permute-start | bytes 491528 | tf_op jit(solution)/shard_map/ppermute | solution.py:211
  11.8 11.6 %collective-permute-start.3 = (f32[5,2,32,128]{3,2,1,0:T(8,128)S(1)}, f32[5,2,32,128]{3,2,1,0:T(8,128)S(1)}, u32[]{:S(2)}, u32[]{:S(2)}) collective-permute-start(f32[5,2,32,128]{3,2,1,0:T(8,128)S(1)} %pad_maximum_fusion.3), channel_id=1, source_target_pairs={{24,0},{36,12},{48,24},{60,36},{72,48},{84,60},{96,72},{108,84},{1... | collective-permute-start | bytes 491528 | tf_op jit(solution)/shard_map/ppermute | solution.py:211
  13.8 18.2 %copy-start.35 = (s32[128]{0:T(128)}, s32[128]{0:T(128)S(1)}, u32[]{:S(2)}) copy-start(s32[128]{0:T(128)S(1)} %and_select_fusion) | copy-start | bytes 1540
  13.8 18.2 %copy-start.38 = (pred[3]{0:T(512)(128)(4,1)}, pred[3]{0:T(512)(128)(4,1)S(1)}, u32[]{:S(2)}) copy-start(pred[3]{0:T(512)(128)(4,1)S(1)} %compare_and_fusion.2) | copy-start | bytes 13
  23.5 6.9 %collective-permute-start.5 = (f32[5,10,4,128]{3,2,1,0:T(4,128)S(1)}, f32[5,10,4,128]{3,2,1,0:T(4,128)S(1)}, u32[]{:S(2)}, u32[]{:S(2)}) collective-permute-start(f32[5,10,4,128]{3,2,1,0:T(4,128)S(1)} %get-tuple-element.89), channel_id=1, source_target_pairs={{1,0},{2,1},{3,2},{4,3},{5,4},{6,5},{7,6},{8,7},{9,8},{10,9},{11,1... | collective-permute-start | bytes 307208 | tf_op jit(solution)/shard_map/ppermute | solution.py:220
  24.8 7.1 %collective-permute-start.4 = (f32[5,10,4,128]{3,2,1,0:T(4,128)S(1)}, f32[5,10,4,128]{3,2,1,0:T(4,128)S(1)}, u32[]{:S(2)}, u32[]{:S(2)}) collective-permute-start(f32[5,10,4,128]{3,2,1,0:T(4,128)S(1)} %get-tuple-element.88), channel_id=1, source_target_pairs={{0,1},{1,2},{2,3},{3,4},{4,5},{5,6},{6,7},{7,8},{8,9},{9,10},{10,1... | collective-permute-start | bytes 307208 | tf_op jit(solution)/shard_map/ppermute | solution.py:219
  40.9 20.4 %copy-start.24 = (f32[5,1,1,16,64]{4,3,1,2,0:T(8,128)}, f32[5,1,1,16,64]{4,3,1,2,0:T(8,128)S(1)}, u32[]{:S(2)}) copy-start(f32[5,1,1,16,64]{4,3,1,2,0:T(8,128)S(1)} %get-tuple-element.212) | copy-start | bytes 61444
  40.9 90.8 %collective-permute-start.9 = (f32[5,1,16,64]{3,2,0,1:T(8,128)}, f32[5,1,16,64]{3,2,0,1:T(8,128)}, u32[]{:S(2)}, u32[]{:S(2)}) collective-permute-start(f32[5,1,16,64]{3,2,0,1:T(8,128)} %get-tuple-element.213), channel_id=1, source_target_pairs={{1,0},{2,1},{3,2},{4,3},{5,4},{6,5},{7,6},{8,7},{9,8},{10,9},{11,1... | collective-permute-start | bytes 61448 | tf_op jit(solution)/shard_map/ppermute | solution.py:329
  42.2 88.7 %collective-permute-start.8 = (f32[5,1,16,64]{3,2,0,1:T(8,128)}, f32[5,1,16,64]{3,2,0,1:T(8,128)}, u32[]{:S(2)}, u32[]{:S(2)}) collective-permute-start(f32[5,1,16,64]{3,2,0,1:T(8,128)} %get-tuple-element.213), channel_id=1, source_target_pairs={{0,1},{1,2},{2,3},{3,4},{4,5},{5,6},{6,7},{7,8},{8,9},{9,10},{10,1... | collective-permute-start | bytes 61448 | tf_op jit(solution)/shard_map/ppermute | solution.py:328
  49.1 21.6 %copy-start.40 = (f32[15]{0:T(128)}, f32[15]{0:T(128)S(1)}, u32[]{:S(2)}) copy-start(f32[15]{0:T(128)S(1)} %pad_maximum_fusion.14) | copy-start | bytes 184
  49.1 12.8 %collective-permute-start.14 = (f32[15]{0:T(128)S(1)}, f32[15]{0:T(128)S(1)}, u32[]{:S(2)}, u32[]{:S(2)}) collective-permute-start(f32[15]{0:T(128)S(1)} %pad_maximum_fusion.14), channel_id=1, source_target_pairs={{0,24},{12,36},{24,48},{36,60},{48,72},{60,84},{72,96},{84,108},{9... | collective-permute-start | bytes 188 | tf_op jit(solution)/shard_map/ppermute | solution.py:313
  55.7 8.2 %collective-permute-start.15 = (f32[15]{0:T(128)S(1)}, f32[15]{0:T(128)S(1)}, u32[]{:S(2)}, u32[]{:S(2)}) collective-permute-start(f32[15]{0:T(128)S(1)} %pad_maximum_fusion.14), channel_id=1, source_target_pairs={{0,12},{12,24},{24,36},{36,48},{48,60},{60,72},{72,84},{84,96},{96... | collective-permute-start | bytes 188 | tf_op jit(solution)/shard_map/ppermute | solution.py:313
  57.6 7.6 %collective-permute-start.16 = (f32[15]{0:T(128)S(1)}, f32[15]{0:T(128)S(1)}, u32[]{:S(2)}, u32[]{:S(2)}) collective-permute-start(f32[15]{0:T(128)S(1)} %pad_maximum_fusion.14), channel_id=1, source_target_pairs={{12,0},{24,12},{36,24},{48,36},{60,48},{72,60},{84,72},{96,84},{10... | collective-permute-start | bytes 188 | tf_op jit(solution)/shard_map/ppermute | solution.py:314
  61.9 8.8 %copy-start.41 = (f32[15]{0:T(128)}, f32[15]{0:T(128)S(1)}, u32[]{:S(2)}) copy-start(f32[15]{0:T(128)S(1)} %collective-permute-done.14) | copy-start | bytes 184
  61.9 8.8 %collective-permute-start.17 = (f32[15]{0:T(128)S(1)}, f32[15]{0:T(128)S(1)}, u32[]{:S(2)}, u32[]{:S(2)}) collective-permute-start(f32[15]{0:T(128)S(1)} %pad_maximum_fusion.14), channel_id=1, source_target_pairs={{24,0},{36,12},{48,24},{60,36},{72,48},{84,60},{96,72},{108,84},{1... | collective-permute-start | bytes 188 | tf_op jit(solution)/shard_map/ppermute | solution.py:314
  63.8 6.9 %copy-start.42 = (f32[15]{0:T(128)}, f32[15]{0:T(128)S(1)}, u32[]{:S(2)}) copy-start(f32[15]{0:T(128)S(1)} %collective-permute-done.15) | copy-start | bytes 184
  63.9 76.1 %collective-permute-start.7 = (f32[3,2,4,128]{3,2,1,0:T(4,128)}, f32[3,2,4,128]{3,2,1,0:T(4,128)S(1)}, u32[]{:S(2)}, u32[]{:S(2)}) collective-permute-start(f32[3,2,4,128]{3,2,1,0:T(4,128)} %get-tuple-element.185), channel_id=1, source_target_pairs={{1,0},{2,1},{3,2},{4,3},{5,4},{6,5},{7,6},{8,7},{9,8},{10,9},{11,1... | collective-permute-start | bytes 36872 | tf_op jit(solution)/shard_map/ppermute | solution.py:326
  65.2 74.8 %collective-permute-start.6 = (f32[3,2,4,128]{3,2,1,0:T(4,128)}, f32[3,2,4,128]{3,2,1,0:T(4,128)}, u32[]{:S(2)}, u32[]{:S(2)}) collective-permute-start(f32[3,2,4,128]{3,2,1,0:T(4,128)} %get-tuple-element.184), channel_id=1, source_target_pairs={{0,1},{1,2},{2,3},{3,4},{4,5},{5,6},{6,7},{7,8},{8,9},{9,10},{10,1... | collective-permute-start | bytes 36872 | tf_op jit(solution)/shard_map/ppermute | solution.py:325
  139.3 10.1 %copy-start.29 = (f32[5,12,3]{0,2,1:T(4,128)S(1)}, f32[5,12,3]{0,2,1:T(4,128)}, u32[]{:S(2)}) copy-start(f32[5,12,3]{0,2,1:T(4,128)} %copy.148) | copy-start | bytes 2164
  139.3 10.1 %copy-start.32 = (f32[5,12]{0,1:T(8,128)S(1)}, f32[5,12]{0,1:T(8,128)}, u32[]{:S(2)}) copy-start(f32[5,12]{0,1:T(8,128)} %copy.147) | copy-start | bytes 724
  139.3 14.6 %copy-start.45 = (pred[5,3]{0,1:T(4,128)(4,1)S(1)}, pred[5,3]{0,1:T(4,128)(4,1)}, u32[]{:S(2)}) copy-start(pred[5,3]{0,1:T(4,128)(4,1)} %broadcast_and_fusion.1) | copy-start | bytes 49
  139.9 15.3 %copy-start.31 = (f32[3,2,4,128]{3,2,1,0:T(4,128)}, f32[3,2,4,128]{3,2,1,0:T(4,128)S(1)}, u32[]{:S(2)}) copy-start(f32[3,2,4,128]{3,2,1,0:T(4,128)S(1)} %collective-permute-done.7) | copy-start | bytes 36868
  142.1 25.6 %collective-permute-start.10 = (f32[6,2,40,128]{3,2,1,0:T(8,128)}, f32[6,2,40,128]{3,2,1,0:T(8,128)}, u32[]{:S(2)}, u32[]{:S(2)}) collective-permute-start(f32[6,2,40,128]{3,2,1,0:T(8,128)} %pad_maximum_fusion.2), channel_id=1, source_target_pairs={{0,24},{12,36},{24,48},{36,60},{48,72},{60,84},{72,96},{84,108},{9... | collective-permute-start | bytes 737288 | tf_op jit(solution)/shard_map/ppermute | solution.py:210
  152.0 16.7 %collective-permute-start.11 = (f32[6,2,40,128]{3,2,1,0:T(8,128)}, f32[6,2,40,128]{3,2,1,0:T(8,128)}, u32[]{:S(2)}, u32[]{:S(2)}) collective-permute-start(f32[6,2,40,128]{3,2,1,0:T(8,128)} %pad_maximum_fusion.2), channel_id=1, source_target_pairs={{0,12},{12,24},{24,36},{36,48},{48,60},{60,72},{72,84},{84,96},{96... | collective-permute-start | bytes 737288 | tf_op jit(solution)/shard_map/ppermute | solution.py:210
  161.8 18.2 %copy-start.30 = (f32[3,10,40]{2,1,0:T(8,128)S(1)}, f32[3,10,40]{2,1,0:T(8,128)}, u32[]{:S(2)}) copy-start(f32[3,10,40]{2,1,0:T(8,128)} %copy.151) | copy-start | bytes 14404
  161.8 9.1 %collective-permute-start.12 = (f32[6,2,40,128]{3,2,1,0:T(8,128)}, f32[6,2,40,128]{3,2,1,0:T(8,128)S(1)}, u32[]{:S(2)}, u32[]{:S(2)}) collective-permute-start(f32[6,2,40,128]{3,2,1,0:T(8,128)} %pad_maximum_fusion.2), channel_id=1, source_target_pairs={{12,0},{24,12},{36,24},{48,36},{60,48},{72,60},{84,72},{96,84},{10... | collective-permute-start | bytes 737288 | tf_op jit(solution)/shard_map/ppermute | solution.py:211
  165.6 14.4 %collective-permute-start.13 = (f32[6,2,40,128]{3,2,1,0:T(8,128)}, f32[6,2,40,128]{3,2,1,0:T(8,128)S(1)}, u32[]{:S(2)}, u32[]{:S(2)}) collective-permute-start(f32[6,2,40,128]{3,2,1,0:T(8,128)} %pad_maximum_fusion.2), channel_id=1, source_target_pairs={{24,0},{36,12},{48,24},{60,36},{72,48},{84,60},{96,72},{108,84},{1... | collective-permute-start | bytes 737288 | tf_op jit(solution)/shard_map/ppermute | solution.py:211
  (32 other events, 58.0 us)

commit v5 on v2

--- a/solution.py
+++ b/solution.py
@@ -126,6 +126,12 @@
     return jnp.where(labels[..., :, None] == labels[..., None, :], 1.0, 0.0).astype(jnp.float32)
 
 
+def crop_xy(array, cut_x, cut_y):
+    size_x = array.shape[-3]
+    size_y = array.shape[-2]
+    return array[..., cut_x : size_x - cut_x, cut_y : size_y - cut_y, :]
+
+
 def crop(array, cut):
     if cut == 0:
         return array
@@ -221,38 +227,49 @@
     return jnp.concatenate([low, array, high], axis=-2)
 
 
-def inside_mask(width_x, width_y, depth):
+def inside_mask(width_x, width_y, depth_x, depth_y):
     gx = lax.axis_index("gx")
     gy = lax.axis_index("gy")
     total_x = width_x * lax.axis_size("gx")
     total_y = width_y * lax.axis_size("gy")
-    xs = gx * width_x + jnp.arange(width_x + 2 * depth) - depth
-    ys = gy * width_y + jnp.arange(width_y + 2 * depth) - depth
+    xs = gx * width_x + jnp.arange(width_x + 2 * depth_x) - depth_x
+    ys = gy * width_y + jnp.arange(width_y + 2 * depth_y) - depth_y
     ok_x = (xs >= 0) & (xs < total_x)
     ok_y = (ys >= 0) & (ys < total_y)
     return (ok_x[:, None] & ok_y[None, :])[:, :, None]
 
 
-def smooth_ext(solution, residual, inverse_diag, mu, lam, depth, steps):
+def smooth_ext(solution, residual, inverse_diag, mu, lam, steps):
     midpoint = 0.5 * (HIGH_BOUND + LOW_BOUND)
     halfwidth = 0.5 * (HIGH_BOUND - LOW_BOUND)
     sharpness = midpoint / halfwidth
     weight_old = 1.0 / sharpness
-    level = depth
-    direction = inverse_diag * residual / midpoint
-    solution = solution + crop(direction, level)
-    cut = depth + 1 - level
-    residual = crop(residual, 1) - apply_ext(direction, crop(mu, cut), crop(lam, cut), 1.0)
-    level -= 1
+
+    def extent(array):
+        return (
+            (array.shape[-3] - solution.shape[-3]) // 2,
+            (array.shape[-2] - solution.shape[-2]) // 2,
+        )
+
+    def fit(array, like):
+        ax, ay = extent(array)
+        bx, by = extent(like)
+        return crop_xy(array, ax - bx, ay - by)
+
+    direction = fit(inverse_diag, residual) * residual / midpoint
+    solution = solution + fit(direction, solution)
+    coef_like = jnp.zeros(residual.shape[-3:], residual.dtype)
+    residual = crop(residual, 1) - apply_ext(direction, fit(mu, coef_like), fit(lam, coef_like), 1.0)
     for step_id in range(steps - 1):
         weight_new = 1.0 / (2.0 * sharpness - weight_old)
         direction = weight_new * weight_old * crop(direction, 1) + 2.0 * weight_new / halfwidth * (
-            crop(inverse_diag, depth - level) * residual
-        )
-        solution = solution + crop(direction, level)
-        cut = depth + 1 - level
-        residual = crop(residual, 1) - apply_ext(direction, crop(mu, cut), crop(lam, cut), 1.0)
-        level -= 1
+            fit(inverse_diag, residual) * residual
+        )
+        solution = solution + fit(direction, solution)
+        coef_like = jnp.zeros(residual.shape[-3:], residual.dtype)
+        residual = crop(residual, 1) - apply_ext(
+            direction, fit(mu, coef_like), fit(lam, coef_like), 1.0
+        )
         weight_old = weight_new
     return (solution, residual)
 
@@ -278,28 +295,36 @@
     gy = lax.axis_index("gy")
     count_y = lax.axis_size("gy")
 
+    coarse_x = width_x // 2
+    coarse_y = width_y // 2
+    coarse_z = width_z // 2
+    fine_reach = depth + 1
+    res_rows = COARSE_SWEEPS + (depth + 2) // 2
+    coef_rows = res_rows + 2
+    deep_y = 2 * coef_rows
+
     stacked = jnp.concatenate([rhs_field, shear_modulus[None], lame_lambda[None]], axis=0)
     stacked = halo_x(stacked, depth + 1)
-    stacked = halo_y(stacked, depth + 1)
+    stacked = halo_y(stacked, deep_y)
     mu_ext = stacked[3]
     lam_ext = stacked[4]
     rhs_ext = crop(stacked[0:3], 1)
-    inside = inside_mask(width_x, width_y, depth)
+    inside = inside_mask(width_x, width_y, depth, deep_y - 1)
     inverse_diag = jnp.where(inside[None], 1.0 / diagonal_ext(mu_ext, lam_ext, 1.0), 0.0)
 
-    solution, residual = smooth_ext(
-        jnp.zeros_like(rhs_field), rhs_ext, inverse_diag, mu_ext, lam_ext, depth, SWEEPS
-    )
-    coarse_x = width_x // 2
-    coarse_y = width_y // 2
-    coarse_z = width_z // 2
+    solution, residual_deep = smooth_ext(
+        jnp.zeros_like(rhs_field), rhs_ext, inverse_diag, mu_ext, lam_ext, SWEEPS
+    )
+    deep_r = (residual_deep.shape[2] - width_y) // 2
+    residual_y = crop_xy(residual_deep, 0, deep_r - fine_reach)
     pairs = pair_matrix(coarse_z)
-    coarse_res = restrict_z(residual, pairs).reshape(3, coarse_x, 2, coarse_y, 2, coarse_z)
-    coarse_res = coarse_res.sum(axis=(2, 4))
-    coarse_coef = restrict_z(jnp.stack([shear_modulus, lame_lambda]), pairs)
-    coarse_coef = coarse_coef.reshape(2, coarse_x, 2, coarse_y, 2, coarse_z).sum(axis=(2, 4)) / 8.0
-    coarse_mu = coarse_coef[0]
-    coarse_lam = coarse_coef[1]
+    res_win = restrict_z(crop_xy(residual_deep, 0, deep_r - 2 * res_rows), pairs)
+    res_win = res_win.reshape(3, coarse_x, 2, coarse_y + 2 * res_rows, 2, coarse_z).sum(axis=(2, 4))
+    fine_coef = crop_xy(jnp.stack([mu_ext, lam_ext]), depth + 1, deep_y - 2 * coef_rows)
+    coef_win = restrict_z(fine_coef, pairs)
+    coef_win = coef_win.reshape(2, coarse_x, 2, coarse_y + 2 * coef_rows, 2, coarse_z)
+    coef_win = coef_win.sum(axis=(2, 4)) / 8.0
+    coarse_res = res_win[:, :, res_rows : res_rows + coarse_y]
     starts = group_start[0]
     members = same_group(starts)
     cells_dev = coarse_x * coarse_y * coarse_z
@@ -308,17 +333,14 @@
     slots = jnp.where(jnp.arange(count_y)[:, None] == gy, sums[None, :], 0.0)
     all_sums = lax.psum(slots, "gy")
 
-    forward = [(i, i + 1) for i in range(count_y - 1)]
-    backward = [(i + 1, i) for i in range(count_y - 1)]
-    fine_reach = depth + 1
-    below = lax.ppermute(residual[:, :, -fine_reach:, :], "gy", forward)
-    above = lax.ppermute(residual[:, :, :fine_reach, :], "gy", backward)
-    coarse_pack = jnp.concatenate([coarse_res, coarse_mu[None], coarse_lam[None]], axis=0)
-    pack_below = lax.ppermute(coarse_pack, "gy", forward)
-    pack_above = lax.ppermute(coarse_pack, "gy", backward)
-    residual_y = jnp.concatenate([below, residual, above], axis=2)
-
-    window = jnp.stack([pack_below, coarse_pack, pack_above], axis=1)
+    def blocks(array, rows):
+        gap = jnp.zeros(array.shape[:2] + (coarse_y - rows,) + array.shape[3:], array.dtype)
+        low = jnp.concatenate([gap, array[:, :, :rows]], axis=2)
+        own = array[:, :, rows : rows + coarse_y]
+        high = jnp.concatenate([array[:, :, rows + coarse_y :], gap], axis=2)
+        return jnp.stack([low, own, high], axis=1)
+
+    window = jnp.concatenate([blocks(res_win, res_rows), blocks(coef_win, coef_rows)], axis=0)
     next_start = lax.dynamic_index_in_dim(starts, jnp.minimum(gy + 1, count_y - 1), 0, keepdims=False)
     own_start = lax.dynamic_index_in_dim(starts, gy, 0, keepdims=False)
     window_starts = jnp.stack([jnp.zeros_like(own_start), own_start, next_start])
@@ -357,9 +379,12 @@
     residual_ext = crop(joined[0:3], 1)
     fine_corr = joined[3:6]
     solution = solution + crop(fine_corr, fine_reach)
-    residual_ext = residual_ext - apply_ext(fine_corr, mu_ext, lam_ext, 1.0)
+    coef_cut = (mu_ext.shape[-2] - fine_corr.shape[-2]) // 2
+    residual_ext = residual_ext - apply_ext(
+        fine_corr, crop_xy(mu_ext, 0, coef_cut), crop_xy(lam_ext, 0, coef_cut), 1.0
+    )
     solution, residual = smooth_ext(
-        solution, residual_ext, inverse_diag, mu_ext, lam_ext, depth, SWEEPS
+        solution, residual_ext, inverse_diag, mu_ext, lam_ext, SWEEPS
     )
     return (solution, residual)
 

time: 136 us -> 122 us (0.90)
  starting transfers between devices: 45.4 us -> 31.5 us
  waiting for transfers between devices: 14.1 us -> 19.6 us
  other arithmetic: 27.6 us -> 23.2 us
  local copies, waits for them, and re-layouts: 12 us -> 8.73 us
  blocking collectives: 31.7 us -> 33.6 us
    ppermute x4 -> x0, starting transfers between devices: 13.3 us -> none  [the longest x1 5.55 us: shards(): pack_below = lax.ppermute(coarse_pack, 'gy', forward)]
    ppermute x1, waiting for transfers between devices: 0.14 us -> 6.5 us  [halo_y(): high = lax.ppermute(array[..., :depth, :], 'gy', backward)]
    unnamed x76 -> x41, local copies, waits for them, and re-layouts: 3.78 us -> 1.17 us
    psum x1, blocking collectives: 31.7 us -> 33.6 us  [shards(): all_sums = lax.psum(slots, 'gy')]
    another operation x21, other arithmetic: 3.99 us -> 5.73 us  [apply_ext(): return jnp.stack(results)]
    another operation x5 -> x1, other arithmetic: 1.79 us -> 0.19 us  [the longest x2 1.4 us: shards(): window = jnp.stack([pack_below, coarse_pack, pack_above], axis=1)]
    another operation x2 -> x4, local copies, waits for them, and re-layouts: 1.6 us -> 0.02 us  [blocks(): return jnp.stack([low, own, high], axis=1)]
    mul x2 -> x12, other arithmetic: 0.02 us -> 1.55 us  [the longest x9 1.31 us: operate(): results.append(scale * (-laplace[comp_id] - grad_term))]
  transfers between devices with their start and end apart: 14 -> 10, of which waited for: 5 -> 5; matrix products, arithmetic and copies ran while one was open for 16% -> 7% of each run, Pallas kernels for 0% -> 0%
where the time goes in v5:
time: 122 us; the launch traced here: 121 us
  blocking collectives  33.6 us (28%)
  starting transfers between devices  31.5 us (26%)
  other arithmetic  23.2 us (19%)
  waiting for transfers between devices  19.6 us (16%)
  local copies, waits for them, and re-layouts  8.73 us (7%)
  matrix products  2.55 us (2%)
  between operations  1.63 us (1%)
    psum x1, blocking collectives, shards(): all_sums = lax.psum(slots, 'gy')  33.6 us
    ppermute x4, starting transfers between devices, halo_x(): lows.append(lax.ppermute(array[..., width - need:, :, :], 'gx', forward))  14 us
    ppermute x4, waiting for transfers between devices, halo_x(): highs.append(lax.ppermute(array[..., :need, :, :], 'gx', backward))  11.9 us
    ppermute x4, starting transfers between devices, halo_x(): highs.append(lax.ppermute(array[..., :need, :, :], 'gx', backward))  11.3 us
    ppermute x1, waiting for transfers between devices, halo_y(): high = lax.ppermute(array[..., :depth, :], 'gy', backward)  6.5 us
    another operation x21, other arithmetic, apply_ext(): return jnp.stack(results)  5.73 us
    ppermute x1, starting transfers between devices, halo_y(): low = lax.ppermute(array[..., -depth:, :], 'gy', forward)  4.93 us
  transfers between devices with their start and end apart: 10, of which 5 were waited for; matrix products, arithmetic and copies ran while one was open for 7% of the time, Pallas kernels for 0%

profile of v5, /device:TPU:30, one launch (start us, length us, event | category | flops | bytes accessed | tf_op | source)
XLA Modules:
  0.0 120.9 jit_solution(15640411056904345828)
XLA Ops:
  0.6 0.9 pad_maximum_fusion.1
  1.6 4.6 %collective-permute-start = (f32[5,2,32,128]{3,2,1,0:T(8,128)S(1)}, f32[5,2,32,128]{3,2,1,0:T(8,128)S(1)}, u32[]{:S(2)}, u32[]{:S(2)}) collective-permute-start(f32[5,2,32,128]{3,2,1,0:T(8,128)S(1)} %pad_maximum_fusion.1), channel_id=1, source_target_pairs={{0,24},{12,36},{24,48},{36,60},{48,72},{60,84},{72,96},{84,108},{9... | collective-permute-start | bytes 491528 | tf_op jit(solution)/shard_map/ppermute | solution.py:216
  6.2 1.9 %collective-permute-start.1 = (f32[5,2,32,128]{3,2,1,0:T(8,128)S(1)}, f32[5,2,32,128]{3,2,1,0:T(8,128)S(1)}, u32[]{:S(2)}, u32[]{:S(2)}) collective-permute-start(f32[5,2,32,128]{3,2,1,0:T(8,128)S(1)} %pad_maximum_fusion.1), channel_id=1, source_target_pairs={{0,12},{12,24},{24,36},{36,48},{48,60},{60,72},{72,84},{84,96},{96... | collective-permute-start | bytes 491528 | tf_op jit(solution)/shard_map/ppermute | solution.py:216
  8.1 3.6 %collective-permute-start.2 = (f32[5,2,32,128]{3,2,1,0:T(8,128)S(1)}, f32[5,2,32,128]{3,2,1,0:T(8,128)S(1)}, u32[]{:S(2)}, u32[]{:S(2)}) collective-permute-start(f32[5,2,32,128]{3,2,1,0:T(8,128)S(1)} %pad_maximum_fusion.1), channel_id=1, source_target_pairs={{12,0},{24,12},{36,24},{48,36},{60,48},{72,60},{84,72},{96,84},{10... | collective-permute-start | bytes 491528 | tf_op jit(solution)/shard_map/ppermute | solution.py:217
  11.8 1.9 %collective-permute-start.3 = (f32[5,2,32,128]{3,2,1,0:T(8,128)S(1)}, f32[5,2,32,128]{3,2,1,0:T(8,128)S(1)}, u32[]{:S(2)}, u32[]{:S(2)}) collective-permute-start(f32[5,2,32,128]{3,2,1,0:T(8,128)S(1)} %pad_maximum_fusion.1), channel_id=1, source_target_pairs={{24,0},{36,12},{48,24},{60,36},{72,48},{84,60},{96,72},{108,84},{1... | collective-permute-start | bytes 491528 | tf_op jit(solution)/shard_map/ppermute | solution.py:217
  14.8 0.7 compare_select_fusion.7
  16.4 1.3 %constant_dynamic-slice_fusion.1 = (s32[1,1]{1,0:T(1,128)}, s32[1,1]{1,0:T(1,128)}) fusion(s32[1,12]{1,0:T(1,128)} %param.7, s32[]{:T(128)S(6)} %select_n.116, s32[]{:T(128)S(6)} %select_n.117), kind=kLoop, calls=%fused_computation.870 | loop fusion | bytes 24 | tf_op jit(solution)/shard_map/jit(dynamic_index_in_dim)/dynamic_slice | solution.py:345
  17.7 1.4 %compare_select_fusion.8 = f32[2]{0:T(128)S(1)} fusion(s32[1]{0:T(128)} %bitcast.26, s32[1]{0:T(128)} %bitcast.25), kind=kLoop, calls=%fused_computation.853 | loop fusion | flops 6 | bytes 16 | tf_op jit(solution)/shard_map/jit(_where)/select_n | solution.py:101
  19.8 0.7 and.114
  20.5 0.9 constant_dynamic-update-slice_fusion.2
  21.5 1.9 %collective-permute-done.3 = f32[5,2,32,128]{3,2,1,0:T(8,128)S(1)} collective-permute-done((f32[5,2,32,128]{3,2,1,0:T(8,128)S(1)}, f32[5,2,32,128]{3,2,1,0:T(8,128)S(1)}, u32[]{:S(2)}, u32[]{:S(2)}) %collective-permute-start.3) | collective-permute-done | bytes 163872 | tf_op jit(solution)/shard_map/ppermute | solution.py:217
  23.5 1.3 %collective-permute-start.5 = (f32[5,10,16,128]{3,2,1,0:T(8,128)S(1)}, f32[5,10,16,128]{3,2,1,0:T(8,128)S(1)}, u32[]{:S(2)}, u32[]{:S(2)}) collective-permute-start(f32[5,10,16,128]{3,2,1,0:T(8,128)S(1)} %get-tuple-element.55), channel_id=1, source_target_pairs={{1,0},{2,1},{3,2},{4,3},{5,4},{6,5},{7,6},{8,7},{9,8},{10,9},{11,1... | collective-permute-start | bytes 1228808 | tf_op jit(solution)/shard_map/ppermute | solution.py:226
  24.8 4.9 %collective-permute-start.4 = (f32[5,10,16,128]{3,2,1,0:T(8,128)S(1)}, f32[5,10,16,128]{3,2,1,0:T(8,128)S(1)}, u32[]{:S(2)}, u32[]{:S(2)}) collective-permute-start(f32[5,10,16,128]{3,2,1,0:T(8,128)S(1)} %get-tuple-element.54), channel_id=1, source_target_pairs={{0,1},{1,2},{2,3},{3,4},{4,5},{5,6},{6,7},{7,8},{8,9},{9,10},{10,1... | collective-permute-start | bytes 1228808 | tf_op jit(solution)/shard_map/ppermute | solution.py:225
  30.3 6.5 %collective-permute-done.5 = f32[5,10,16,128]{3,2,1,0:T(8,128)S(1)} collective-permute-done((f32[5,10,16,128]{3,2,1,0:T(8,128)S(1)}, f32[5,10,16,128]{3,2,1,0:T(8,128)S(1)}, u32[]{:S(2)}, u32[]{:S(2)}) %collective-permute-start.5) | collective-permute-done | bytes 409632 | tf_op jit(solution)/shard_map/ppermute | solution.py:226
  36.8 1.2 collective-permute-done.4
  43.8 0.6 copy-done.2
  44.4 0.9 convolution_reduce_fusion
  45.3 1.0 reduce_sum.66
  46.9 0.6 slice_reduce_fusion
  47.6 1.5 %fusion.6 = f32[2,64,64]{2,1,0:T(8,128)} fusion(f32[5,10,16,128]{3,2,1,0:T(8,128)S(1)} %collective-permute-done.5, f32[5,10,32,128]{3,2,1,0:T(8,128)S(1)} %constant_dynamic-update-slice_fusion, f32[5,10,16,128]{3,2,1,0:T(8,128)S(1)} %collective-permute-done.4, s32[128]{0:T(128)} %copy-done.10), kind=kOutput, calls=%fused_computation.8 | convolution fusion | flops 26001408 | bytes 1671680 | tf_op jit(solution)/shard_map/...j,kj->...k/dot_general | solution.py:287
  49.0 0.9 reduce_sum.63
  50.0 0.7 fusion.495
  54.3 33.6 %psum.7 = f32[12,3]{0,1:T(4,128)S(1)} all-reduce(f32[12,3]{0,1:T(4,128)S(1)} %broadcast_select_fusion), channel_id=1, replica_groups=mesh['gx'=64,'gy'=12] {'gy'}, use_global_device_ids=true, to_apply=%region_6.7 | all-reduce | flops 36 | bytes 288 | tf_op jit(solution)/shard_map/psum | solution.py:334
  88.1 0.7 gather_fusion
  89.7 5.5 %collective-permute-start.6 = (f32[6,2,40,128]{3,2,1,0:T(8,128)S(1)}, f32[6,2,40,128]{3,2,1,0:T(8,128)S(1)}, u32[]{:S(2)}, u32[]{:S(2)}) collective-permute-start(f32[6,2,40,128]{3,2,1,0:T(8,128)S(1)} %pad_maximum_fusion), channel_id=1, source_target_pairs={{0,24},{12,36},{24,48},{36,60},{48,72},{60,84},{72,96},{84,108},{9... | collective-permute-start | bytes 737288 | tf_op jit(solution)/shard_map/ppermute | solution.py:216
  95.2 1.9 %collective-permute-start.7 = (f32[6,2,40,128]{3,2,1,0:T(8,128)S(1)}, f32[6,2,40,128]{3,2,1,0:T(8,128)S(1)}, u32[]{:S(2)}, u32[]{:S(2)}) collective-permute-start(f32[6,2,40,128]{3,2,1,0:T(8,128)S(1)} %pad_maximum_fusion), channel_id=1, source_target_pairs={{0,12},{12,24},{24,36},{36,48},{48,60},{60,72},{72,84},{84,96},{96... | collective-permute-start | bytes 737288 | tf_op jit(solution)/shard_map/ppermute | solution.py:216
  97.2 3.6 %collective-permute-start.8 = (f32[6,2,40,128]{3,2,1,0:T(8,128)S(1)}, f32[6,2,40,128]{3,2,1,0:T(8,128)S(1)}, u32[]{:S(2)}, u32[]{:S(2)}) collective-permute-start(f32[6,2,40,128]{3,2,1,0:T(8,128)S(1)} %pad_maximum_fusion), channel_id=1, source_target_pairs={{12,0},{24,12},{36,24},{48,36},{60,48},{72,60},{84,72},{96,84},{10... | collective-permute-start | bytes 737288 | tf_op jit(solution)/shard_map/ppermute | solution.py:217
  100.8 2.1 %collective-permute-start.9 = (f32[6,2,40,128]{3,2,1,0:T(8,128)S(1)}, f32[6,2,40,128]{3,2,1,0:T(8,128)S(1)}, u32[]{:S(2)}, u32[]{:S(2)}) collective-permute-start(f32[6,2,40,128]{3,2,1,0:T(8,128)S(1)} %pad_maximum_fusion), channel_id=1, source_target_pairs={{24,0},{36,12},{48,24},{60,36},{72,48},{84,60},{96,72},{108,84},{1... | collective-permute-start | bytes 737288 | tf_op jit(solution)/shard_map/ppermute | solution.py:217
  103.5 2.3 %collective-permute-done.8 = f32[6,2,40,128]{3,2,1,0:T(8,128)S(1)} collective-permute-done((f32[6,2,40,128]{3,2,1,0:T(8,128)S(1)}, f32[6,2,40,128]{3,2,1,0:T(8,128)S(1)}, u32[]{:S(2)}, u32[]{:S(2)}) %collective-permute-start.8) | collective-permute-done | bytes 245792 | tf_op jit(solution)/shard_map/ppermute | solution.py:217
  105.8 7.8 %collective-permute-done.9 = f32[6,2,40,128]{3,2,1,0:T(8,128)S(1)} collective-permute-done((f32[6,2,40,128]{3,2,1,0:T(8,128)S(1)}, f32[6,2,40,128]{3,2,1,0:T(8,128)S(1)}, u32[]{:S(2)}, u32[]{:S(2)}) %collective-permute-start.9) | collective-permute-done | bytes 245792 | tf_op jit(solution)/shard_map/ppermute | solution.py:217
  118.0 1.7 %slice_add_fusion.23 = f32[3,2,32,128]{3,2,1,0:T(8,128)} fusion(f32[3,4,34,128]{3,2,1,0:T(8,128)S(1)} %get-tuple-element.4, f32[3,6,36,128]{3,2,1,0:T(8,128)S(1)} %get-tuple-element.8, f32[3,8,38,128]{3,2,1,0:T(8,128)S(1)} %get-tuple-element.12, f32[3,4,58,128]{3,2,1,0:T(8,128)S(1)} %get-tuple-element.29, f32[3,6,60,128]{3,2,1,0:T(8,128)} %copy-done.1, ...), kind=kLoop, calls=%fused_computation.347 | loop fusion | flops 147456 | bytes 737280 | tf_op jit(solution)/shard_map/add | solution.py:268
  120.3 0.7 slice_subtract_fusion.45
  (191 shorter events, 19.3 us)
Async XLA Ops:
  1.6 18.9 %collective-permute-start = (f32[5,2,32,128]{3,2,1,0:T(8,128)S(1)}, f32[5,2,32,128]{3,2,1,0:T(8,128)S(1)}, u32[]{:S(2)}, u32[]{:S(2)}) collective-permute-start(f32[5,2,32,128]{3,2,1,0:T(8,128)S(1)} %pad_maximum_fusion.1), channel_id=1, source_target_pairs={{0,24},{12,36},{24,48},{36,60},{48,72},{60,84},{72,96},{84,108},{9... | collective-permute-start | bytes 491528 | tf_op jit(solution)/shard_map/ppermute | solution.py:216
  6.2 14.3 %collective-permute-start.1 = (f32[5,2,32,128]{3,2,1,0:T(8,128)S(1)}, f32[5,2,32,128]{3,2,1,0:T(8,128)S(1)}, u32[]{:S(2)}, u32[]{:S(2)}) collective-permute-start(f32[5,2,32,128]{3,2,1,0:T(8,128)S(1)} %pad_maximum_fusion.1), channel_id=1, source_target_pairs={{0,12},{12,24},{24,36},{36,48},{48,60},{60,72},{72,84},{84,96},{96... | collective-permute-start | bytes 491528 | tf_op jit(solution)/shard_map/ppermute | solution.py:216
  8.1 13.3 %collective-permute-start.2 = (f32[5,2,32,128]{3,2,1,0:T(8,128)S(1)}, f32[5,2,32,128]{3,2,1,0:T(8,128)S(1)}, u32[]{:S(2)}, u32[]{:S(2)}) collective-permute-start(f32[5,2,32,128]{3,2,1,0:T(8,128)S(1)} %pad_maximum_fusion.1), channel_id=1, source_target_pairs={{12,0},{24,12},{36,24},{48,36},{60,48},{72,60},{84,72},{96,84},{10... | collective-permute-start | bytes 491528 | tf_op jit(solution)/shard_map/ppermute | solution.py:217
  11.8 11.6 %collective-permute-start.3 = (f32[5,2,32,128]{3,2,1,0:T(8,128)S(1)}, f32[5,2,32,128]{3,2,1,0:T(8,128)S(1)}, u32[]{:S(2)}, u32[]{:S(2)}) collective-permute-start(f32[5,2,32,128]{3,2,1,0:T(8,128)S(1)} %pad_maximum_fusion.1), channel_id=1, source_target_pairs={{24,0},{36,12},{48,24},{60,36},{72,48},{84,60},{96,72},{108,84},{1... | collective-permute-start | bytes 491528 | tf_op jit(solution)/shard_map/ppermute | solution.py:217
  13.7 30.0 %copy-start.10 = (s32[128]{0:T(128)}, s32[128]{0:T(128)S(1)}, u32[]{:S(2)}) copy-start(s32[128]{0:T(128)S(1)} %and_select_fusion) | copy-start | bytes 1540
  14.8 8.7 %copy-start.8 = (pred[3]{0:T(512)(128)(4,1)}, pred[3]{0:T(512)(128)(4,1)S(1)}, u32[]{:S(2)}) copy-start(pred[3]{0:T(512)(128)(4,1)S(1)} %get-tuple-element.198) | copy-start | bytes 13
  23.5 13.3 %collective-permute-start.5 = (f32[5,10,16,128]{3,2,1,0:T(8,128)S(1)}, f32[5,10,16,128]{3,2,1,0:T(8,128)S(1)}, u32[]{:S(2)}, u32[]{:S(2)}) collective-permute-start(f32[5,10,16,128]{3,2,1,0:T(8,128)S(1)} %get-tuple-element.55), channel_id=1, source_target_pairs={{1,0},{2,1},{3,2},{4,3},{5,4},{6,5},{7,6},{8,7},{9,8},{10,9},{11,1... | collective-permute-start | bytes 1228808 | tf_op jit(solution)/shard_map/ppermute | solution.py:226
  24.8 13.2 %collective-permute-start.4 = (f32[5,10,16,128]{3,2,1,0:T(8,128)S(1)}, f32[5,10,16,128]{3,2,1,0:T(8,128)S(1)}, u32[]{:S(2)}, u32[]{:S(2)}) collective-permute-start(f32[5,10,16,128]{3,2,1,0:T(8,128)S(1)} %get-tuple-element.54), channel_id=1, source_target_pairs={{0,1},{1,2},{2,3},{3,4},{4,5},{5,6},{6,7},{7,8},{8,9},{9,10},{10,1... | collective-permute-start | bytes 1228808 | tf_op jit(solution)/shard_map/ppermute | solution.py:225
  39.2 1.9 %copy-start = (f32[3,8,62,128]{3,2,1,0:T(8,128)}, f32[3,8,62,128]{3,2,1,0:T(8,128)S(1)}, u32[]{:S(2)}) copy-start(f32[3,8,62,128]{3,2,1,0:T(8,128)S(1)} %get-tuple-element.37) | copy-start | bytes 2285572
  41.3 1.4 %copy-start.1 = (f32[3,6,60,128]{3,2,1,0:T(8,128)}, f32[3,6,60,128]{3,2,1,0:T(8,128)S(1)}, u32[]{:S(2)}) copy-start(f32[3,6,60,128]{3,2,1,0:T(8,128)S(1)} %get-tuple-element.33) | copy-start | bytes 1658884
  43.8 0.7 copy-start.2
  47.5 2.4 %copy-start.5 = (f32[3,1,6,64]{3,2,0,1:T(8,128)S(1)}, f32[3,1,6,64]{3,2,0,1:T(8,128)}, u32[]{:S(2)}) copy-start(f32[3,1,6,64]{3,2,0,1:T(8,128)} %get-tuple-element.186) | copy-start | bytes 13828
  47.6 2.5 %copy-start.4 = (f32[3,1,6,64]{3,2,0,1:T(8,128)S(1)}, f32[3,1,6,64]{3,2,0,1:T(8,128)}, u32[]{:S(2)}) copy-start(f32[3,1,6,64]{3,2,0,1:T(8,128)} %get-tuple-element.185) | copy-start | bytes 13828
  49.0 2.1 %copy-start.9 = (pred[3]{0:T(512)(128)(4,1)S(1)}, pred[3]{0:T(512)(128)(4,1)}, u32[]{:S(2)}) copy-start(pred[3]{0:T(512)(128)(4,1)} %copy-done.8) | copy-start | bytes 13
  49.0 2.2 %copy-start.7 = (f32[3]{0:T(128)S(1)}, f32[3]{0:T(128)}, u32[]{:S(2)}) copy-start(f32[3]{0:T(128)} %get-tuple-element.194) | copy-start | bytes 40
  49.0 2.3 %copy-start.6 = (f32[3]{0:T(128)S(1)}, f32[3]{0:T(128)}, u32[]{:S(2)}) copy-start(f32[3]{0:T(128)} %get-tuple-element.193) | copy-start | bytes 40
  53.3 0.9 copy-start.3
  53.3 0.9 copy-start.12
  53.3 0.9 copy-start.15
  53.3 34.7 %copy-start.14 = (f32[12]{0:T(128)S(1)}, f32[12]{0:T(128)}, u32[]{:S(2)}) copy-start(f32[12]{0:T(128)} %broadcast_multiply_fusion.1) | copy-start | bytes 148
  53.3 35.5 %copy-start.13 = (pred[3]{0:T(512)(128)(4,1)S(1)}, pred[3]{0:T(512)(128)(4,1)}, u32[]{:S(2)}) copy-start(pred[3]{0:T(512)(128)(4,1)} %get-tuple-element.197) | copy-start | bytes 13
  53.3 35.9 %copy-start.16 = (pred[48]{0:T(512)(128)(4,1)S(1)}, pred[48]{0:T(512)(128)(4,1)}, u32[]{:S(2)}) copy-start(pred[48]{0:T(512)(128)(4,1)} %and.114) | copy-start | bytes 148
  53.5 35.8 %copy-start.11 = (s32[128]{0:T(128)S(1)}, s32[128]{0:T(128)}, u32[]{:S(2)}) copy-start(s32[128]{0:T(128)} %copy-done.10) | copy-start | bytes 1540
  89.7 13.7 %collective-permute-start.6 = (f32[6,2,40,128]{3,2,1,0:T(8,128)S(1)}, f32[6,2,40,128]{3,2,1,0:T(8,128)S(1)}, u32[]{:S(2)}, u32[]{:S(2)}) collective-permute-start(f32[6,2,40,128]{3,2,1,0:T(8,128)S(1)} %pad_maximum_fusion), channel_id=1, source_target_pairs={{0,24},{12,36},{24,48},{36,60},{48,72},{60,84},{72,96},{84,108},{9... | collective-permute-start | bytes 737288 | tf_op jit(solution)/shard_map/ppermute | solution.py:216
  95.2 8.2 %collective-permute-start.7 = (f32[6,2,40,128]{3,2,1,0:T(8,128)S(1)}, f32[6,2,40,128]{3,2,1,0:T(8,128)S(1)}, u32[]{:S(2)}, u32[]{:S(2)}) collective-permute-start(f32[6,2,40,128]{3,2,1,0:T(8,128)S(1)} %pad_maximum_fusion), channel_id=1, source_target_pairs={{0,12},{12,24},{24,36},{36,48},{48,60},{60,72},{72,84},{84,96},{96... | collective-permute-start | bytes 737288 | tf_op jit(solution)/shard_map/ppermute | solution.py:216
  97.2 8.6 %collective-permute-start.8 = (f32[6,2,40,128]{3,2,1,0:T(8,128)S(1)}, f32[6,2,40,128]{3,2,1,0:T(8,128)S(1)}, u32[]{:S(2)}, u32[]{:S(2)}) collective-permute-start(f32[6,2,40,128]{3,2,1,0:T(8,128)S(1)} %pad_maximum_fusion), channel_id=1, source_target_pairs={{12,0},{24,12},{36,24},{48,36},{60,48},{72,60},{84,72},{96,84},{10... | collective-permute-start | bytes 737288 | tf_op jit(solution)/shard_map/ppermute | solution.py:217
  100.8 12.7 %collective-permute-start.9 = (f32[6,2,40,128]{3,2,1,0:T(8,128)S(1)}, f32[6,2,40,128]{3,2,1,0:T(8,128)S(1)}, u32[]{:S(2)}, u32[]{:S(2)}) collective-permute-start(f32[6,2,40,128]{3,2,1,0:T(8,128)S(1)} %pad_maximum_fusion), channel_id=1, source_target_pairs={{24,0},{36,12},{48,24},{60,36},{72,48},{84,60},{96,72},{108,84},{1... | collective-permute-start | bytes 737288 | tf_op jit(solution)/shard_map/ppermute | solution.py:217

commit v6 on v5

--- a/solution.py
+++ b/solution.py
@@ -86,7 +86,7 @@
     direction = inverse_diag * residual / midpoint
     solution = solution + direction
     residual = residual - apply_fn(direction)
-    for step_id in range(steps - 1):
+    for _ in range(steps - 1):
         weight_new = 1.0 / (2.0 * sharpness - weight_old)
         direction = weight_new * weight_old * direction + 2.0 * weight_new / halfwidth * (
             inverse_diag * residual
@@ -260,7 +260,7 @@
     solution = solution + fit(direction, solution)
     coef_like = jnp.zeros(residual.shape[-3:], residual.dtype)
     residual = crop(residual, 1) - apply_ext(direction, fit(mu, coef_like), fit(lam, coef_like), 1.0)
-    for step_id in range(steps - 1):
+    for _ in range(steps - 1):
         weight_new = 1.0 / (2.0 * sharpness - weight_old)
         direction = weight_new * weight_old * crop(direction, 1) + 2.0 * weight_new / halfwidth * (
             fit(inverse_diag, residual) * residual
@@ -287,7 +287,7 @@
     return jnp.einsum("...j,kj->...k", array, pairs, precision=lax.Precision.HIGHEST)
 
 
-def shards(rhs_field, shear_modulus, lame_lambda, group_start):
+def shards_body(rhs_field, shear_modulus, lame_lambda, group_start):
     width_x = rhs_field.shape[1]
     width_y = rhs_field.shape[2]
     width_z = rhs_field.shape[3]
@@ -355,16 +355,10 @@
         return operate(pad_groups(field, window_starts), coef_pad[0], coef_pad[1], 4.0)
 
     window_res = window[0:3]
-    smoothed, coarse_left = smooth(
+    smoothed, _ = smooth(
         jnp.zeros_like(window_res), window_res, coarse_inverse, coarse_apply, COARSE_SWEEPS
     )
-    totals = jnp.sum(members[:, :, None] * all_sums[None, :, :], axis=1)
-    group_cells = jnp.sum(members, axis=1) * cells_dev
-    group_shift = totals / (SHIFT_SCALE * group_cells[:, None])
-    window_shift = jnp.take(group_shift, jnp.clip(owners, 0, count_y - 1), axis=0)
-    window_shift = jnp.where(valid[:, None], window_shift, 0.0)
-    correction = smoothed + window_shift.T[:, :, None, None, None]
-    correction = jnp.moveaxis(correction, 1, 2).reshape(3, coarse_x, 3 * coarse_y, coarse_z)
+    correction = jnp.moveaxis(smoothed, 1, 2).reshape(3, coarse_x, 3 * coarse_y, coarse_z)
     reach_c = (depth + 2) // 2
     corr_y = correction[:, :, coarse_y - reach_c : 2 * coarse_y + reach_c, :]
     corr_z = upsample_z(corr_y, pairs)
@@ -374,10 +368,27 @@
     ).reshape(3, width_x, 2 * corr_y.shape[2], width_z)
     fine_depth = 2 * reach_c
     fine_corr = fine_corr[:, :, fine_depth - fine_reach : fine_corr.shape[2] - (fine_depth - fine_reach), :]
-
-    joined = halo_x(jnp.concatenate([residual_y, fine_corr], axis=0), fine_reach)
-    residual_ext = crop(joined[0:3], 1)
-    fine_corr = joined[3:6]
+    fine_corr = halo_x(fine_corr, fine_reach)
+    residual_ext = crop_xy(halo_x(residual_y, depth), 0, 1)
+
+    totals = jnp.sum(members[:, :, None] * all_sums[None, :, :], axis=1)
+    group_cells = jnp.sum(members, axis=1) * cells_dev
+    group_shift = totals / (SHIFT_SCALE * group_cells[:, None])
+    window_shift = jnp.take(group_shift, jnp.clip(owners, 0, count_y - 1), axis=0)
+    window_shift = jnp.where(valid[:, None], window_shift, 0.0)
+    count_x = lax.axis_size("gx")
+    side = reach_c
+    lows, highs = [], []
+    for dx in range(side, 0, -1):
+        lows.append(lax.ppermute(window_shift, "gx", [(i, i + dx) for i in range(count_x - dx)]))
+        highs.append(lax.ppermute(window_shift, "gx", [(i + dx, i) for i in range(count_x - dx)]))
+    block_shift = jnp.stack(lows + [window_shift] + highs[::-1])
+    block_shift = jnp.repeat(jnp.moveaxis(block_shift, 2, 0), 2, axis=1)
+    block_shift = block_shift[:, 2 * side - fine_reach : block_shift.shape[1] - (2 * side - fine_reach)]
+    rows = jnp.array([fine_reach, width_y, fine_reach])
+    block_shift = jnp.repeat(block_shift, rows, axis=2, total_repeat_length=width_y + 2 * fine_reach)
+    fine_corr = fine_corr + block_shift[:, :, :, None]
+
     solution = solution + crop(fine_corr, fine_reach)
     coef_cut = (mu_ext.shape[-2] - fine_corr.shape[-2]) // 2
     residual_ext = residual_ext - apply_ext(
@@ -391,7 +402,7 @@
 
 def solution(mesh):
     return jax.shard_map(
-        shards,
+        shards_body,
         mesh=mesh,
         in_specs=(
             P(None, "gx", "gy", None),

time: 122 us -> 153 us (1.25)
  starting transfers between devices: 31.5 us -> 56.1 us
  local copies, waits for them, and re-layouts: 8.73 us -> 17.2 us
  waiting for transfers between devices: 19.6 us -> 24.1 us
  blocking collectives: 33.6 us -> 29.9 us
    ppermute x0 -> x4, starting transfers between devices: none -> 15.4 us  [the longest x2 9.81 us: shards_body(): lax.ppermute(window_shift, 'gx', [(i, i + dx) for i in range(count_x - dx)])]
    ppermute x4 -> x6, starting transfers between devices: 14 us -> 19.5 us  [halo_x(): lows.append(lax.ppermute(array[..., width - need:, :, :], 'gx', forward))]
    ppermute x1, waiting for transfers between devices: 1.18 us -> 6.39 us  [halo_y(): low = lax.ppermute(array[..., -depth:, :], 'gy', forward)]
    unnamed x41 -> x43, local copies, waits for them, and re-layouts: 1.17 us -> 6.35 us
    ppermute x4 -> x6, starting transfers between devices: 11.3 us -> 15.6 us  [halo_x(): highs.append(lax.ppermute(array[..., :need, :, :], 'gx', backward))]
    psum x1, blocking collectives: 33.6 us -> 29.9 us  [shards_body(): all_sums = lax.psum(slots, 'gy')]
    ppermute x4 -> x6, waiting for transfers between devices: 0.01 us -> 3.16 us  [halo_x(): lows.append(lax.ppermute(array[..., width - need:, :, :], 'gx', forward))]
    slice x21, local copies, waits for them, and re-layouts: 1.4 us -> 3.9 us  [shifted_ext(): return jnp.concatenate([zero, inner[..., :-1]], axis=-1)]
  transfers between devices with their start and end apart: 10 -> 18, of which waited for: 5 -> 5; matrix products, arithmetic and copies ran while one was open for 7% -> 17% of each run, Pallas kernels for 0% -> 0%
where the time goes in v6:
time: 153 us; the launch traced here: 152 us
  starting transfers between devices  56.1 us (37%)
  blocking collectives  29.9 us (20%)
  waiting for transfers between devices  24.1 us (16%)
  other arithmetic  22.1 us (14%)
  local copies, waits for them, and re-layouts  17.2 us (11%)
  between operations  1.73 us (1%)
    psum x1, blocking collectives, shards_body(): all_sums = lax.psum(slots, 'gy')  29.9 us
    ppermute x6, starting transfers between devices, halo_x(): lows.append(lax.ppermute(array[..., width - need:, :, :], 'gx', forward))  19.5 us
    ppermute x6, starting transfers between devices, halo_x(): highs.append(lax.ppermute(array[..., :need, :, :], 'gx', backward))  15.6 us
    ppermute x2, starting transfers between devices, shards_body(): lax.ppermute(window_shift, 'gx', [(i, i + dx) for i in range(count_x - dx)])  9.81 us
    ppermute x6, waiting for transfers between devices, halo_x(): highs.append(lax.ppermute(array[..., :need, :, :], 'gx', backward))  9.75 us
    ppermute x1, waiting for transfers between devices, halo_y(): low = lax.ppermute(array[..., -depth:, :], 'gy', forward)  6.39 us
    unnamed x43, local copies, waits for them, and re-layouts  6.35 us
    another operation x21, other arithmetic, apply_ext(): return jnp.stack(results)  5.63 us
  transfers between devices with their start and end apart: 18, of which 5 were waited for; matrix products, arithmetic and copies ran while one was open for 17% of the time, Pallas kernels for 0%

profile of v6, /device:TPU:30, one launch (start us, length us, event | category | flops | bytes accessed | tf_op | source)
XLA Modules:
  0.0 152.3 jit_solution(4298129462301752478)
XLA Ops:
  0.7 1.0 pad_maximum_fusion
  1.6 4.6 %collective-permute-start = (f32[5,2,32,128]{3,2,1,0:T(8,128)S(1)}, f32[5,2,32,128]{3,2,1,0:T(8,128)S(1)}, u32[]{:S(2)}, u32[]{:S(2)}) collective-permute-start(f32[5,2,32,128]{3,2,1,0:T(8,128)S(1)} %pad_maximum_fusion), channel_id=1, source_target_pairs={{0,24},{12,36},{24,48},{36,60},{48,72},{60,84},{72,96},{84,108},{9... | collective-permute-start | bytes 491528 | tf_op jit(solution)/shard_map/ppermute | solution.py:216
  6.3 1.9 %collective-permute-start.1 = (f32[5,2,32,128]{3,2,1,0:T(8,128)S(1)}, f32[5,2,32,128]{3,2,1,0:T(8,128)S(1)}, u32[]{:S(2)}, u32[]{:S(2)}) collective-permute-start(f32[5,2,32,128]{3,2,1,0:T(8,128)S(1)} %pad_maximum_fusion), channel_id=1, source_target_pairs={{0,12},{12,24},{24,36},{36,48},{48,60},{60,72},{72,84},{84,96},{96... | collective-permute-start | bytes 491528 | tf_op jit(solution)/shard_map/ppermute | solution.py:216
  8.2 3.6 %collective-permute-start.2 = (f32[5,2,32,128]{3,2,1,0:T(8,128)S(1)}, f32[5,2,32,128]{3,2,1,0:T(8,128)S(1)}, u32[]{:S(2)}, u32[]{:S(2)}) collective-permute-start(f32[5,2,32,128]{3,2,1,0:T(8,128)S(1)} %pad_maximum_fusion), channel_id=1, source_target_pairs={{12,0},{24,12},{36,24},{48,36},{60,48},{72,60},{84,72},{96,84},{10... | collective-permute-start | bytes 491528 | tf_op jit(solution)/shard_map/ppermute | solution.py:217
  11.8 1.9 %collective-permute-start.3 = (f32[5,2,32,128]{3,2,1,0:T(8,128)S(1)}, f32[5,2,32,128]{3,2,1,0:T(8,128)S(1)}, u32[]{:S(2)}, u32[]{:S(2)}) collective-permute-start(f32[5,2,32,128]{3,2,1,0:T(8,128)S(1)} %pad_maximum_fusion), channel_id=1, source_target_pairs={{24,0},{36,12},{48,24},{60,36},{72,48},{84,60},{96,72},{108,84},{1... | collective-permute-start | bytes 491528 | tf_op jit(solution)/shard_map/ppermute | solution.py:217
  15.9 1.3 pad_clamp_fusion
  17.2 1.3 constant_dynamic-slice_fusion.1
  18.5 1.2 compare_select_fusion.8
  20.6 2.9 %collective-permute-done.3 = f32[5,2,32,128]{3,2,1,0:T(8,128)S(1)} collective-permute-done((f32[5,2,32,128]{3,2,1,0:T(8,128)S(1)}, f32[5,2,32,128]{3,2,1,0:T(8,128)S(1)}, u32[]{:S(2)}, u32[]{:S(2)}) %collective-permute-start.3) | collective-permute-done | bytes 163872 | tf_op jit(solution)/shard_map/ppermute | solution.py:217
  23.5 4.3 %collective-permute-start.4 = (f32[5,10,16,128]{3,2,1,0:T(8,128)S(1)}, f32[5,10,16,128]{3,2,1,0:T(8,128)S(1)}, u32[]{:S(2)}, u32[]{:S(2)}) collective-permute-start(f32[5,10,16,128]{3,2,1,0:T(8,128)S(1)} %get-tuple-element.61), channel_id=1, source_target_pairs={{0,1},{1,2},{2,3},{3,4},{4,5},{5,6},{6,7},{7,8},{8,9},{9,10},{10,1... | collective-permute-start | bytes 1228808 | tf_op jit(solution)/shard_map/ppermute | solution.py:225
  27.8 1.3 collective-permute-start.5
  29.7 6.4 %collective-permute-done.4 = f32[5,10,16,128]{3,2,1,0:T(8,128)S(1)} collective-permute-done((f32[5,10,16,128]{3,2,1,0:T(8,128)S(1)}, f32[5,10,16,128]{3,2,1,0:T(8,128)S(1)}, u32[]{:S(2)}, u32[]{:S(2)}) %collective-permute-start.4) | collective-permute-done | bytes 409632 | tf_op jit(solution)/shard_map/ppermute | solution.py:225
  36.1 4.8 %collective-permute-done.5 = f32[5,10,16,128]{3,2,1,0:T(8,128)S(1)} collective-permute-done((f32[5,10,16,128]{3,2,1,0:T(8,128)S(1)}, f32[5,10,16,128]{3,2,1,0:T(8,128)S(1)}, u32[]{:S(2)}, u32[]{:S(2)}) %collective-permute-start.5) | collective-permute-done | bytes 409632 | tf_op jit(solution)/shard_map/ppermute | solution.py:226
  47.7 1.9 %collective-permute-start.15 = (f32[3,2,40,128]{3,2,1,0:T(8,128)}, f32[3,2,40,128]{3,2,1,0:T(8,128)}, u32[]{:S(2)}, u32[]{:S(2)}) collective-permute-start(f32[3,2,40,128]{3,2,1,0:T(8,128)} %slice.2606), channel_id=1, source_target_pairs={{0,12},{12,24},{24,36},{36,48},{48,60},{60,72},{72,84},{84,96},{96... | collective-permute-start | bytes 368648 | tf_op jit(solution)/shard_map/ppermute | solution.py:216
  49.7 3.6 %collective-permute-start.16 = (f32[3,2,40,128]{3,2,1,0:T(8,128)}, f32[3,2,40,128]{3,2,1,0:T(8,128)}, u32[]{:S(2)}, u32[]{:S(2)}) collective-permute-start(f32[3,2,40,128]{3,2,1,0:T(8,128)} %slice.2606), channel_id=1, source_target_pairs={{12,0},{24,12},{36,24},{48,36},{60,48},{72,60},{84,72},{96,84},{10... | collective-permute-start | bytes 368648 | tf_op jit(solution)/shard_map/ppermute | solution.py:217
  54.5 29.9 %psum.7 = f32[12,3]{0,1:T(4,128)S(1)} all-reduce(f32[12,3]{0,1:T(4,128)S(1)} %broadcast_select_fusion), channel_id=1, replica_groups=mesh['gx'=64,'gy'=12] {'gy'}, use_global_device_ids=true, to_apply=%region_9.10 | all-reduce | flops 36 | bytes 288 | tf_op jit(solution)/shard_map/psum | solution.py:334
  85.8 1.2 select_select_fusion
  87.0 7.9 %collective-permute-start.10 = (f32[3,3]{1,0:T(4,128)}, f32[3,3]{1,0:T(4,128)}, u32[]{:S(2)}, u32[]{:S(2)}) collective-permute-start(f32[3,3]{1,0:T(4,128)} %select_select_fusion), channel_id=1, source_target_pairs={{0,24},{12,36},{24,48},{36,60},{48,72},{60,84},{72,96},{84,108},{9... | collective-permute-start | bytes 116 | tf_op jit(solution)/shard_map/ppermute | solution.py:383
  94.9 1.9 %collective-permute-start.11 = (f32[3,3]{1,0:T(4,128)}, f32[3,3]{1,0:T(4,128)}, u32[]{:S(2)}, u32[]{:S(2)}) collective-permute-start(f32[3,3]{1,0:T(4,128)} %select_select_fusion), channel_id=1, source_target_pairs={{0,12},{12,24},{24,36},{36,48},{48,60},{60,72},{72,84},{84,96},{96... | collective-permute-start | bytes 116 | tf_op jit(solution)/shard_map/ppermute | solution.py:383
  96.9 3.6 %collective-permute-start.12 = (f32[3,3]{1,0:T(4,128)}, f32[3,3]{1,0:T(4,128)}, u32[]{:S(2)}, u32[]{:S(2)}) collective-permute-start(f32[3,3]{1,0:T(4,128)} %select_select_fusion), channel_id=1, source_target_pairs={{12,0},{24,12},{36,24},{48,36},{60,48},{72,60},{84,72},{96,84},{10... | collective-permute-start | bytes 116 | tf_op jit(solution)/shard_map/ppermute | solution.py:384
  107.9 1.9 %collective-permute-start.13 = (f32[3,3]{1,0:T(4,128)}, f32[3,3]{1,0:T(4,128)S(1)}, u32[]{:S(2)}, u32[]{:S(2)}) collective-permute-start(f32[3,3]{1,0:T(4,128)} %select_select_fusion), channel_id=1, source_target_pairs={{24,0},{36,12},{48,24},{60,36},{72,48},{84,60},{96,72},{108,84},{1... | collective-permute-start | bytes 116 | tf_op jit(solution)/shard_map/ppermute | solution.py:384
  110.6 7.2 %collective-permute-start.6 = (f32[3,2,40,128]{3,2,1,0:T(8,128)S(1)}, f32[3,2,40,128]{3,2,1,0:T(8,128)S(1)}, u32[]{:S(2)}, u32[]{:S(2)}) collective-permute-start(f32[3,2,40,128]{3,2,1,0:T(8,128)S(1)} %broadcast_in_dim.141), channel_id=1, source_target_pairs={{0,24},{12,36},{24,48},{36,60},{48,72},{60,84},{72,96},{84,108},{9... | collective-permute-start | bytes 368648 | tf_op jit(solution)/shard_map/ppermute | solution.py:216
  118.6 1.9 %collective-permute-start.7 = (f32[3,2,40,128]{3,2,1,0:T(8,128)S(1)}, f32[3,2,40,128]{3,2,1,0:T(8,128)S(1)}, u32[]{:S(2)}, u32[]{:S(2)}) collective-permute-start(f32[3,2,40,128]{3,2,1,0:T(8,128)S(1)} %broadcast_in_dim.141), channel_id=1, source_target_pairs={{0,12},{12,24},{24,36},{36,48},{48,60},{60,72},{72,84},{84,96},{96... | collective-permute-start | bytes 368648 | tf_op jit(solution)/shard_map/ppermute | solution.py:216
  121.2 1.9 %collective-permute-start.14 = (f32[3,1,40,128]{3,2,1,0:T(8,128)S(1)}, f32[3,1,40,128]{3,2,1,0:T(8,128)S(1)}, u32[]{:S(2)}, u32[]{:S(2)}) collective-permute-start(f32[3,1,40,128]{3,2,1,0:T(8,128)S(1)} %get-tuple-element.144), channel_id=1, source_target_pairs={{0,24},{12,36},{24,48},{36,60},{48,72},{60,84},{72,96},{84,108},{9... | collective-permute-start | bytes 184328 | tf_op jit(solution)/shard_map/ppermute | solution.py:216
  124.2 3.1 %collective-permute-done.14 = f32[3,1,40,128]{3,2,1,0:T(8,128)S(1)} collective-permute-done((f32[3,1,40,128]{3,2,1,0:T(8,128)S(1)}, f32[3,1,40,128]{3,2,1,0:T(8,128)S(1)}, u32[]{:S(2)}, u32[]{:S(2)}) %collective-permute-start.14) | collective-permute-done | bytes 61472 | tf_op jit(solution)/shard_map/ppermute | solution.py:216
  127.4 2.4 %collective-permute-start.8 = (f32[3,2,40,128]{3,2,1,0:T(8,128)S(1)}, f32[3,2,40,128]{3,2,1,0:T(8,128)S(1)}, u32[]{:S(2)}, u32[]{:S(2)}) collective-permute-start(f32[3,2,40,128]{3,2,1,0:T(8,128)S(1)} %broadcast_in_dim.141), channel_id=1, source_target_pairs={{12,0},{24,12},{36,24},{48,36},{60,48},{72,60},{84,72},{96,84},{10... | collective-permute-start | bytes 368648 | tf_op jit(solution)/shard_map/ppermute | solution.py:217
  129.8 1.9 %collective-permute-start.9 = (f32[3,2,40,128]{3,2,1,0:T(8,128)S(1)}, f32[3,2,40,128]{3,2,1,0:T(8,128)S(1)}, u32[]{:S(2)}, u32[]{:S(2)}) collective-permute-start(f32[3,2,40,128]{3,2,1,0:T(8,128)S(1)} %broadcast_in_dim.141), channel_id=1, source_target_pairs={{24,0},{36,12},{48,24},{60,36},{72,48},{84,60},{96,72},{108,84},{1... | collective-permute-start | bytes 368648 | tf_op jit(solution)/shard_map/ppermute | solution.py:217
  131.8 2.1 %collective-permute-start.17 = (f32[3,1,40,128]{3,2,1,0:T(8,128)S(1)}, f32[3,1,40,128]{3,2,1,0:T(8,128)S(1)}, u32[]{:S(2)}, u32[]{:S(2)}) collective-permute-start(f32[3,1,40,128]{3,2,1,0:T(8,128)S(1)} %get-tuple-element.143), channel_id=1, source_target_pairs={{24,0},{36,12},{48,24},{60,36},{72,48},{84,60},{96,72},{108,84},{1... | collective-permute-start | bytes 184328 | tf_op jit(solution)/shard_map/ppermute | solution.py:217
  134.0 6.9 %collective-permute-done.9 = f32[3,2,40,128]{3,2,1,0:T(8,128)S(1)} collective-permute-done((f32[3,2,40,128]{3,2,1,0:T(8,128)S(1)}, f32[3,2,40,128]{3,2,1,0:T(8,128)S(1)}, u32[]{:S(2)}, u32[]{:S(2)}) %collective-permute-start.9) | collective-permute-done | bytes 122912 | tf_op jit(solution)/shard_map/ppermute | solution.py:217
  142.7 0.9 constant_dynamic-update-slice_fusion.17
  143.7 0.9 constant_dynamic-update-slice_fusion.15
  148.7 1.8 %slice_add_fusion.23 = f32[3,2,32,128]{3,2,1,0:T(8,128)} fusion(f32[3,4,34,128]{3,2,1,0:T(8,128)S(1)} %get-tuple-element.16, f32[3,6,36,128]{3,2,1,0:T(8,128)S(1)} %get-tuple-element.20, f32[3,8,38,128]{3,2,1,0:T(8,128)S(1)} %get-tuple-element.24, f32[3,10,40,128]{3,2,1,0:T(8,128)S(1)} %broadcast_add_fusion, f32[3,4,58,128]{3,2,1,0:T(8,128)} %copy-done.2, ...), kind=kLoop, calls=%fused_computation.348 | loop fusion | flops 147456 | bytes 786432 | tf_op jit(solution)/shard_map/add | solution.py:268
  (212 shorter events, 31.0 us)
Async XLA Ops:
  0.6 19.9 %copy-start.8 = (f32[2,32,128]{2,1,0:T(8,128)S(1)}, f32[2,32,128]{2,1,0:T(8,128)}, u32[]{:S(2)}) copy-start(f32[2,32,128]{2,1,0:T(8,128)} %param.8) | copy-start | bytes 98308
  0.6 19.9 %copy-start.7 = (f32[2,32,128]{2,1,0:T(8,128)S(1)}, f32[2,32,128]{2,1,0:T(8,128)}, u32[]{:S(2)}) copy-start(f32[2,32,128]{2,1,0:T(8,128)} %param.9) | copy-start | bytes 98308
  0.7 19.9 %copy-start.5 = (f32[3,2,32,128]{3,2,1,0:T(8,128)S(1)}, f32[3,2,32,128]{3,2,1,0:T(8,128)}, u32[]{:S(2)}) copy-start(f32[3,2,32,128]{3,2,1,0:T(8,128)} %param.7) | copy-start | bytes 294916
  1.6 18.8 %collective-permute-start = (f32[5,2,32,128]{3,2,1,0:T(8,128)S(1)}, f32[5,2,32,128]{3,2,1,0:T(8,128)S(1)}, u32[]{:S(2)}, u32[]{:S(2)}) collective-permute-start(f32[5,2,32,128]{3,2,1,0:T(8,128)S(1)} %pad_maximum_fusion), channel_id=1, source_target_pairs={{0,24},{12,36},{24,48},{36,60},{48,72},{60,84},{72,96},{84,108},{9... | collective-permute-start | bytes 491528 | tf_op jit(solution)/shard_map/ppermute | solution.py:216
  6.3 14.2 %collective-permute-start.1 = (f32[5,2,32,128]{3,2,1,0:T(8,128)S(1)}, f32[5,2,32,128]{3,2,1,0:T(8,128)S(1)}, u32[]{:S(2)}, u32[]{:S(2)}) collective-permute-start(f32[5,2,32,128]{3,2,1,0:T(8,128)S(1)} %pad_maximum_fusion), channel_id=1, source_target_pairs={{0,12},{12,24},{24,36},{36,48},{48,60},{60,72},{72,84},{84,96},{96... | collective-permute-start | bytes 491528 | tf_op jit(solution)/shard_map/ppermute | solution.py:216
  8.2 12.4 %collective-permute-start.2 = (f32[5,2,32,128]{3,2,1,0:T(8,128)S(1)}, f32[5,2,32,128]{3,2,1,0:T(8,128)S(1)}, u32[]{:S(2)}, u32[]{:S(2)}) collective-permute-start(f32[5,2,32,128]{3,2,1,0:T(8,128)S(1)} %pad_maximum_fusion), channel_id=1, source_target_pairs={{12,0},{24,12},{36,24},{48,36},{60,48},{72,60},{84,72},{96,84},{10... | collective-permute-start | bytes 491528 | tf_op jit(solution)/shard_map/ppermute | solution.py:217
  11.8 11.6 %collective-permute-start.3 = (f32[5,2,32,128]{3,2,1,0:T(8,128)S(1)}, f32[5,2,32,128]{3,2,1,0:T(8,128)S(1)}, u32[]{:S(2)}, u32[]{:S(2)}) collective-permute-start(f32[5,2,32,128]{3,2,1,0:T(8,128)S(1)} %pad_maximum_fusion), channel_id=1, source_target_pairs={{24,0},{36,12},{48,24},{60,36},{72,48},{84,60},{96,72},{108,84},{1... | collective-permute-start | bytes 491528 | tf_op jit(solution)/shard_map/ppermute | solution.py:217
  13.8 39.5 %copy-start.10 = (s32[128]{0:T(128)}, s32[128]{0:T(128)S(1)}, u32[]{:S(2)}) copy-start(s32[128]{0:T(128)S(1)} %and_select_fusion) | copy-start | bytes 1540
  23.5 12.6 %collective-permute-start.4 = (f32[5,10,16,128]{3,2,1,0:T(8,128)S(1)}, f32[5,10,16,128]{3,2,1,0:T(8,128)S(1)}, u32[]{:S(2)}, u32[]{:S(2)}) collective-permute-start(f32[5,10,16,128]{3,2,1,0:T(8,128)S(1)} %get-tuple-element.61), channel_id=1, source_target_pairs={{0,1},{1,2},{2,3},{3,4},{4,5},{5,6},{6,7},{7,8},{8,9},{9,10},{10,1... | collective-permute-start | bytes 1228808 | tf_op jit(solution)/shard_map/ppermute | solution.py:225
  27.8 13.0 %collective-permute-start.5 = (f32[5,10,16,128]{3,2,1,0:T(8,128)S(1)}, f32[5,10,16,128]{3,2,1,0:T(8,128)S(1)}, u32[]{:S(2)}, u32[]{:S(2)}) collective-permute-start(f32[5,10,16,128]{3,2,1,0:T(8,128)S(1)} %get-tuple-element.62), channel_id=1, source_target_pairs={{1,0},{2,1},{3,2},{4,3},{5,4},{6,5},{7,6},{8,7},{9,8},{10,9},{11,1... | collective-permute-start | bytes 1228808 | tf_op jit(solution)/shard_map/ppermute | solution.py:226
  42.1 1.9 %copy-start = (f32[3,8,62,128]{3,2,1,0:T(8,128)}, f32[3,8,62,128]{3,2,1,0:T(8,128)S(1)}, u32[]{:S(2)}) copy-start(f32[3,8,62,128]{3,2,1,0:T(8,128)S(1)} %get-tuple-element.55) | copy-start | bytes 2285572
  44.2 1.4 copy-start.1
  45.8 0.8 copy-start.2
  47.7 95.0 %collective-permute-start.15 = (f32[3,2,40,128]{3,2,1,0:T(8,128)}, f32[3,2,40,128]{3,2,1,0:T(8,128)}, u32[]{:S(2)}, u32[]{:S(2)}) collective-permute-start(f32[3,2,40,128]{3,2,1,0:T(8,128)} %slice.2606), channel_id=1, source_target_pairs={{0,12},{12,24},{24,36},{36,48},{48,60},{60,72},{72,84},{84,96},{96... | collective-permute-start | bytes 368648 | tf_op jit(solution)/shard_map/ppermute | solution.py:216
  49.7 94.0 %collective-permute-start.16 = (f32[3,2,40,128]{3,2,1,0:T(8,128)}, f32[3,2,40,128]{3,2,1,0:T(8,128)}, u32[]{:S(2)}, u32[]{:S(2)}) collective-permute-start(f32[3,2,40,128]{3,2,1,0:T(8,128)} %slice.2606), channel_id=1, source_target_pairs={{12,0},{24,12},{36,24},{48,36},{60,48},{72,60},{84,72},{96,84},{10... | collective-permute-start | bytes 368648 | tf_op jit(solution)/shard_map/ppermute | solution.py:217
  87.0 20.9 %collective-permute-start.10 = (f32[3,3]{1,0:T(4,128)}, f32[3,3]{1,0:T(4,128)}, u32[]{:S(2)}, u32[]{:S(2)}) collective-permute-start(f32[3,3]{1,0:T(4,128)} %select_select_fusion), channel_id=1, source_target_pairs={{0,24},{12,36},{24,48},{36,60},{48,72},{60,84},{72,96},{84,108},{9... | collective-permute-start | bytes 116 | tf_op jit(solution)/shard_map/ppermute | solution.py:383
  94.9 15.6 %collective-permute-start.11 = (f32[3,3]{1,0:T(4,128)}, f32[3,3]{1,0:T(4,128)}, u32[]{:S(2)}, u32[]{:S(2)}) collective-permute-start(f32[3,3]{1,0:T(4,128)} %select_select_fusion), channel_id=1, source_target_pairs={{0,12},{12,24},{24,36},{36,48},{48,60},{60,72},{72,84},{84,96},{96... | collective-permute-start | bytes 116 | tf_op jit(solution)/shard_map/ppermute | solution.py:383
  96.9 21.7 %collective-permute-start.12 = (f32[3,3]{1,0:T(4,128)}, f32[3,3]{1,0:T(4,128)}, u32[]{:S(2)}, u32[]{:S(2)}) collective-permute-start(f32[3,3]{1,0:T(4,128)} %select_select_fusion), channel_id=1, source_target_pairs={{12,0},{24,12},{36,24},{48,36},{60,48},{72,60},{84,72},{96,84},{10... | collective-permute-start | bytes 116 | tf_op jit(solution)/shard_map/ppermute | solution.py:384
  104.8 2.8 %copy-start.13 = (pred[48]{0:T(512)(128)(4,1)S(1)}, pred[48]{0:T(512)(128)(4,1)}, u32[]{:S(2)}) copy-start(pred[48]{0:T(512)(128)(4,1)} %and.124) | copy-start | bytes 148
  105.5 2.2 %copy-start.11 = (s32[128]{0:T(128)S(1)}, s32[128]{0:T(128)}, u32[]{:S(2)}) copy-start(s32[128]{0:T(128)} %copy-done.10) | copy-start | bytes 1540
  107.6 10.9 %copy-start.12 = (pred[3]{0:T(512)(128)(4,1)S(1)}, pred[3]{0:T(512)(128)(4,1)}, u32[]{:S(2)}) copy-start(pred[3]{0:T(512)(128)(4,1)} %get-tuple-element.211) | copy-start | bytes 13
  107.9 13.3 %collective-permute-start.13 = (f32[3,3]{1,0:T(4,128)}, f32[3,3]{1,0:T(4,128)S(1)}, u32[]{:S(2)}, u32[]{:S(2)}) collective-permute-start(f32[3,3]{1,0:T(4,128)} %select_select_fusion), channel_id=1, source_target_pairs={{24,0},{36,12},{48,24},{60,36},{72,48},{84,60},{96,72},{108,84},{1... | collective-permute-start | bytes 116 | tf_op jit(solution)/shard_map/ppermute | solution.py:384
  110.6 19.2 %collective-permute-start.6 = (f32[3,2,40,128]{3,2,1,0:T(8,128)S(1)}, f32[3,2,40,128]{3,2,1,0:T(8,128)S(1)}, u32[]{:S(2)}, u32[]{:S(2)}) collective-permute-start(f32[3,2,40,128]{3,2,1,0:T(8,128)S(1)} %broadcast_in_dim.141), channel_id=1, source_target_pairs={{0,24},{12,36},{24,48},{36,60},{48,72},{60,84},{72,96},{84,108},{9... | collective-permute-start | bytes 368648 | tf_op jit(solution)/shard_map/ppermute | solution.py:216
  118.6 13.2 %collective-permute-start.7 = (f32[3,2,40,128]{3,2,1,0:T(8,128)S(1)}, f32[3,2,40,128]{3,2,1,0:T(8,128)S(1)}, u32[]{:S(2)}, u32[]{:S(2)}) collective-permute-start(f32[3,2,40,128]{3,2,1,0:T(8,128)S(1)} %broadcast_in_dim.141), channel_id=1, source_target_pairs={{0,12},{12,24},{24,36},{36,48},{48,60},{60,72},{72,84},{84,96},{96... | collective-permute-start | bytes 368648 | tf_op jit(solution)/shard_map/ppermute | solution.py:216
  121.2 6.2 %collective-permute-start.14 = (f32[3,1,40,128]{3,2,1,0:T(8,128)S(1)}, f32[3,1,40,128]{3,2,1,0:T(8,128)S(1)}, u32[]{:S(2)}, u32[]{:S(2)}) collective-permute-start(f32[3,1,40,128]{3,2,1,0:T(8,128)S(1)} %get-tuple-element.144), channel_id=1, source_target_pairs={{0,24},{12,36},{24,48},{36,60},{48,72},{60,84},{72,96},{84,108},{9... | collective-permute-start | bytes 184328 | tf_op jit(solution)/shard_map/ppermute | solution.py:216
  127.4 6.5 %collective-permute-start.8 = (f32[3,2,40,128]{3,2,1,0:T(8,128)S(1)}, f32[3,2,40,128]{3,2,1,0:T(8,128)S(1)}, u32[]{:S(2)}, u32[]{:S(2)}) collective-permute-start(f32[3,2,40,128]{3,2,1,0:T(8,128)S(1)} %broadcast_in_dim.141), channel_id=1, source_target_pairs={{12,0},{24,12},{36,24},{48,36},{60,48},{72,60},{84,72},{96,84},{10... | collective-permute-start | bytes 368648 | tf_op jit(solution)/shard_map/ppermute | solution.py:217
  129.8 11.0 %collective-permute-start.9 = (f32[3,2,40,128]{3,2,1,0:T(8,128)S(1)}, f32[3,2,40,128]{3,2,1,0:T(8,128)S(1)}, u32[]{:S(2)}, u32[]{:S(2)}) collective-permute-start(f32[3,2,40,128]{3,2,1,0:T(8,128)S(1)} %broadcast_in_dim.141), channel_id=1, source_target_pairs={{24,0},{36,12},{48,24},{60,36},{72,48},{84,60},{96,72},{108,84},{1... | collective-permute-start | bytes 368648 | tf_op jit(solution)/shard_map/ppermute | solution.py:217
  131.8 12.8 %collective-permute-start.17 = (f32[3,1,40,128]{3,2,1,0:T(8,128)S(1)}, f32[3,1,40,128]{3,2,1,0:T(8,128)S(1)}, u32[]{:S(2)}, u32[]{:S(2)}) collective-permute-start(f32[3,1,40,128]{3,2,1,0:T(8,128)S(1)} %get-tuple-element.143), channel_id=1, source_target_pairs={{24,0},{36,12},{48,24},{60,36},{72,48},{84,60},{96,72},{108,84},{1... | collective-permute-start | bytes 184328 | tf_op jit(solution)/shard_map/ppermute | solution.py:217
  145.5 0.9 copy-start.4
  147.4 0.9 copy-start.6
  148.7 2.0 %copy-start.3 = (f32[2,32,127]{2,1,0:T(8,128)S(1)}, f32[2,32,127]{2,1,0:T(8,128)}, u32[]{:S(2)}) copy-start(f32[2,32,127]{2,1,0:T(8,128)} %get-tuple-element.91) | copy-start | bytes 97540
  150.7 0.8 copy-start.9

commit v7 on v5

--- a/solution.py
+++ b/solution.py
@@ -368,16 +368,36 @@
     reach_c = (depth + 2) // 2
     corr_y = correction[:, :, coarse_y - reach_c : 2 * coarse_y + reach_c, :]
     corr_z = upsample_z(corr_y, pairs)
+    corr_rows = corr_z.shape[2]
+    slab = 8 * ((corr_rows + 15) // 16)
+    corr_pad = jnp.pad(corr_z, ((0, 0), (0, 0), (0, 2 * slab - corr_rows), (0, 0)))
+    count_x = lax.axis_size("gx")
+    edge_rows = residual_y.shape[2]
+    lows_r, highs_r, lows_c, highs_c = [], [], [], []
+    for dx in range(reach_c, 0, -1):
+        forward = [(i, i + dx) for i in range(count_x - dx)]
+        backward = [(i + dx, i) for i in range(count_x - dx)]
+        need = min(width_x, depth - (dx - 1) * width_x)
+        if need == width_x:
+            corr_part = corr_pad.reshape(3, width_x, slab, width_z)
+        else:
+            corr_part = corr_pad
+        send_low = jnp.concatenate([residual_y[:, width_x - need :], corr_part[:, : need]], axis=2)
+        send_high = jnp.concatenate([residual_y[:, :need], corr_part[:, :need]], axis=2)
+        got_low = lax.ppermute(send_low, "gx", forward)
+        got_high = lax.ppermute(send_high, "gx", backward)
+        lows_r.append(got_low[:, :, :edge_rows])
+        highs_r.append(got_high[:, :, :edge_rows])
+        lows_c.append(got_low[:, :, edge_rows:].reshape(3, 1, -1, width_z)[:, :, :corr_rows])
+        highs_c.append(got_high[:, :, edge_rows:].reshape(3, 1, -1, width_z)[:, :, :corr_rows])
+    residual_ext = crop_xy(jnp.concatenate(lows_r + [residual_y] + highs_r[::-1], axis=1), 0, 1)
+    corr_cols = jnp.concatenate(lows_c + [corr_z] + highs_c[::-1], axis=1)
     fine_corr = jnp.broadcast_to(
-        corr_z[:, :, None, :, None, :],
-        (3, coarse_x, 2, corr_y.shape[2], 2, width_z),
-    ).reshape(3, width_x, 2 * corr_y.shape[2], width_z)
+        corr_cols[:, :, None, :, None, :],
+        (3, corr_cols.shape[1], 2, corr_rows, 2, width_z),
+    ).reshape(3, 2 * corr_cols.shape[1], 2 * corr_rows, width_z)
     fine_depth = 2 * reach_c
-    fine_corr = fine_corr[:, :, fine_depth - fine_reach : fine_corr.shape[2] - (fine_depth - fine_reach), :]
-
-    joined = halo_x(jnp.concatenate([residual_y, fine_corr], axis=0), fine_reach)
-    residual_ext = crop(joined[0:3], 1)
-    fine_corr = joined[3:6]
+    fine_corr = crop(fine_corr, fine_depth - fine_reach)
     solution = solution + crop(fine_corr, fine_reach)
     coef_cut = (mu_ext.shape[-2] - fine_corr.shape[-2]) // 2
     residual_ext = residual_ext - apply_ext(

time: 122 us -> 114 us (0.934)
  other arithmetic: 23.2 us -> 16.9 us
  matrix products: 2.55 us -> 0.66 us
  waiting for transfers between devices: 19.6 us -> 21.4 us
    ppermute x0 -> x4, starting transfers between devices: none -> 13 us  [the longest x2 7.23 us: shards(): got_low = lax.ppermute(send_low, 'gx', forward)]
    ppermute x0 -> x4, waiting for transfers between devices: none -> 7.76 us  [the longest x2 7.71 us: shards(): got_high = lax.ppermute(send_high, 'gx', backward)]
    ppermute x4 -> x2, starting transfers between devices: 14 us -> 6.53 us  [halo_x(): lows.append(lax.ppermute(array[..., width - need:, :, :], 'gx', forward))]
    ppermute x4 -> x2, waiting for transfers between devices: 11.9 us -> 5.45 us  [halo_x(): highs.append(lax.ppermute(array[..., :need, :, :], 'gx', backward))]
    ppermute x4 -> x2, starting transfers between devices: 11.3 us -> 5.56 us  [halo_x(): highs.append(lax.ppermute(array[..., :need, :, :], 'gx', backward))]
    dot_general x2, matrix products: 2.32 us -> 0.43 us  [restrict_z(): jnp.einsum('...j,kj->...k', array, pairs, precision=lax.Precision.HIGHEST)]
  transfers between devices with their start and end apart: 10 -> 10, of which waited for: 5 -> 4; matrix products, arithmetic and copies ran while one was open for 7% -> 4% of each run, Pallas kernels for 0% -> 0%
where the time goes in v7:
time: 114 us
  blocking collectives  33.6 us (29%)
  starting transfers between devices  31.3 us (27%)
  waiting for transfers between devices  21.4 us (19%)
  other arithmetic  16.9 us (15%)
  local copies, waits for them, and re-layouts  8.3 us (7%)
  between operations  1.69 us (1%)
    psum x1, blocking collectives, shards(): all_sums = lax.psum(slots, 'gy')  33.6 us
    ppermute x2, waiting for transfers between devices, shards(): got_high = lax.ppermute(send_high, 'gx', backward)  7.71 us
    ppermute x2, starting transfers between devices, shards(): got_low = lax.ppermute(send_low, 'gx', forward)  7.23 us
    ppermute x1, waiting for transfers between devices, halo_y(): high = lax.ppermute(array[..., :depth, :], 'gy', backward)  7 us
    ppermute x2, starting transfers between devices, halo_x(): lows.append(lax.ppermute(array[..., width - need:, :, :], 'gx', forward))  6.53 us
    ppermute x2, starting transfers between devices, shards(): got_high = lax.ppermute(send_high, 'gx', backward)  5.74 us
    another operation x21, other arithmetic, apply_ext(): return jnp.stack(results)  5.7 us
    ppermute x2, starting transfers between devices, halo_x(): highs.append(lax.ppermute(array[..., :need, :, :], 'gx', backward))  5.56 us
  transfers between devices with their start and end apart: 10, of which 4 were waited for; matrix products, arithmetic and copies ran while one was open for 4% of the time, Pallas kernels for 0%

profile of v7, /device:TPU:30, one launch (start us, length us, event | category | flops | bytes accessed | tf_op | source)
XLA Modules:
  0.0 113.8 jit_solution(9760801474400713012)
XLA Ops:
  0.7 1.0 pad_maximum_fusion.1
  1.6 4.6 %collective-permute-start = (f32[5,2,32,128]{3,2,1,0:T(8,128)S(1)}, f32[5,2,32,128]{3,2,1,0:T(8,128)S(1)}, u32[]{:S(2)}, u32[]{:S(2)}) collective-permute-start(f32[5,2,32,128]{3,2,1,0:T(8,128)S(1)} %pad_maximum_fusion.1), channel_id=1, source_target_pairs={{0,24},{12,36},{24,48},{36,60},{48,72},{60,84},{72,96},{84,108},{9... | collective-permute-start | bytes 491528 | tf_op jit(solution)/shard_map/ppermute | solution.py:216
  6.3 1.9 %collective-permute-start.1 = (f32[5,2,32,128]{3,2,1,0:T(8,128)S(1)}, f32[5,2,32,128]{3,2,1,0:T(8,128)S(1)}, u32[]{:S(2)}, u32[]{:S(2)}) collective-permute-start(f32[5,2,32,128]{3,2,1,0:T(8,128)S(1)} %pad_maximum_fusion.1), channel_id=1, source_target_pairs={{0,12},{12,24},{24,36},{36,48},{48,60},{60,72},{72,84},{84,96},{96... | collective-permute-start | bytes 491528 | tf_op jit(solution)/shard_map/ppermute | solution.py:216
  8.2 3.6 %collective-permute-start.2 = (f32[5,2,32,128]{3,2,1,0:T(8,128)S(1)}, f32[5,2,32,128]{3,2,1,0:T(8,128)S(1)}, u32[]{:S(2)}, u32[]{:S(2)}) collective-permute-start(f32[5,2,32,128]{3,2,1,0:T(8,128)S(1)} %pad_maximum_fusion.1), channel_id=1, source_target_pairs={{12,0},{24,12},{36,24},{48,36},{60,48},{72,60},{84,72},{96,84},{10... | collective-permute-start | bytes 491528 | tf_op jit(solution)/shard_map/ppermute | solution.py:217
  11.8 1.9 %collective-permute-start.3 = (f32[5,2,32,128]{3,2,1,0:T(8,128)S(1)}, f32[5,2,32,128]{3,2,1,0:T(8,128)S(1)}, u32[]{:S(2)}, u32[]{:S(2)}) collective-permute-start(f32[5,2,32,128]{3,2,1,0:T(8,128)S(1)} %pad_maximum_fusion.1), channel_id=1, source_target_pairs={{24,0},{36,12},{48,24},{60,36},{72,48},{84,60},{96,72},{108,84},{1... | collective-permute-start | bytes 491528 | tf_op jit(solution)/shard_map/ppermute | solution.py:217
  13.8 0.7 compare_select_fusion.7
  14.9 1.3 %constant_dynamic-slice_fusion.1 = (s32[1,1]{1,0:T(1,128)}, s32[1,1]{1,0:T(1,128)}) fusion(s32[1,12]{1,0:T(1,128)} %param.7, s32[]{:T(128)S(6)} %select_n.116, s32[]{:T(128)S(6)} %select_n.117), kind=kLoop, calls=%fused_computation.877 | loop fusion | bytes 24 | tf_op jit(solution)/shard_map/jit(dynamic_index_in_dim)/dynamic_slice | solution.py:345
  16.2 1.4 %compare_select_fusion.8 = f32[2]{0:T(128)S(1)} fusion(s32[1]{0:T(128)} %bitcast.32, s32[1]{0:T(128)} %bitcast.31), kind=kLoop, calls=%fused_computation.860 | loop fusion | flops 6 | bytes 16 | tf_op jit(solution)/shard_map/jit(_where)/select_n | solution.py:101
  18.0 5.4 %collective-permute-done.3 = f32[5,2,32,128]{3,2,1,0:T(8,128)S(1)} collective-permute-done((f32[5,2,32,128]{3,2,1,0:T(8,128)S(1)}, f32[5,2,32,128]{3,2,1,0:T(8,128)S(1)}, u32[]{:S(2)}, u32[]{:S(2)}) %collective-permute-start.3) | collective-permute-done | bytes 163872 | tf_op jit(solution)/shard_map/ppermute | solution.py:217
  23.5 1.3 %collective-permute-start.5 = (f32[5,10,16,128]{3,2,1,0:T(8,128)S(1)}, f32[5,10,16,128]{3,2,1,0:T(8,128)S(1)}, u32[]{:S(2)}, u32[]{:S(2)}) collective-permute-start(f32[5,10,16,128]{3,2,1,0:T(8,128)S(1)} %get-tuple-element.52), channel_id=1, source_target_pairs={{1,0},{2,1},{3,2},{4,3},{5,4},{6,5},{7,6},{8,7},{9,8},{10,9},{11,1... | collective-permute-start | bytes 1228808 | tf_op jit(solution)/shard_map/ppermute | solution.py:226
  24.8 4.9 %collective-permute-start.4 = (f32[5,10,16,128]{3,2,1,0:T(8,128)S(1)}, f32[5,10,16,128]{3,2,1,0:T(8,128)S(1)}, u32[]{:S(2)}, u32[]{:S(2)}) collective-permute-start(f32[5,10,16,128]{3,2,1,0:T(8,128)S(1)} %get-tuple-element.51), channel_id=1, source_target_pairs={{0,1},{1,2},{2,3},{3,4},{4,5},{5,6},{6,7},{7,8},{8,9},{9,10},{10,1... | collective-permute-start | bytes 1228808 | tf_op jit(solution)/shard_map/ppermute | solution.py:225
  29.9 7.0 %collective-permute-done.5 = f32[5,10,16,128]{3,2,1,0:T(8,128)S(1)} collective-permute-done((f32[5,10,16,128]{3,2,1,0:T(8,128)S(1)}, f32[5,10,16,128]{3,2,1,0:T(8,128)S(1)}, u32[]{:S(2)}, u32[]{:S(2)}) %collective-permute-start.5) | collective-permute-done | bytes 409632 | tf_op jit(solution)/shard_map/ppermute | solution.py:226
  36.9 1.2 %collective-permute-done.4 = f32[5,10,16,128]{3,2,1,0:T(8,128)S(1)} collective-permute-done((f32[5,10,16,128]{3,2,1,0:T(8,128)S(1)}, f32[5,10,16,128]{3,2,1,0:T(8,128)S(1)}, u32[]{:S(2)}, u32[]{:S(2)}) %collective-permute-start.4) | collective-permute-done | bytes 409632 | tf_op jit(solution)/shard_map/ppermute | solution.py:225
  39.8 0.5 fusion.62
  40.3 0.4 fusion.49
  40.6 0.5 fusion.41
  42.4 0.3 fusion.119
  43.3 0.4 copy-done.4
  48.3 33.6 %psum.7 = f32[12,3]{0,1:T(4,128)S(1)} all-reduce(f32[12,3]{0,1:T(4,128)S(1)} %broadcast_select_fusion), channel_id=1, replica_groups=mesh['gx'=64,'gy'=12] {'gy'}, use_global_device_ids=true, to_apply=%region_6.7 | all-reduce | flops 36 | bytes 288 | tf_op jit(solution)/shard_map/psum | solution.py:334
  82.1 0.6 gather_fusion
  83.5 0.5 slice-done
  84.0 1.9 %collective-permute-start.7 = (f32[3,2,56,128]{3,2,1,0:T(8,128)S(1)}, f32[3,2,56,128]{3,2,1,0:T(8,128)S(1)}, u32[]{:S(2)}, u32[]{:S(2)}) collective-permute-start(f32[3,2,56,128]{3,2,1,0:T(8,128)S(1)} %pad_maximum_fusion), channel_id=1, source_target_pairs={{0,12},{12,24},{24,36},{36,48},{48,60},{60,72},{72,84},{84,96},{96... | collective-permute-start | bytes 516104 | tf_op jit(solution)/shard_map/ppermute | solution.py:387
  85.9 3.6 %collective-permute-start.8 = (f32[3,2,56,128]{3,2,1,0:T(8,128)S(1)}, f32[3,2,56,128]{3,2,1,0:T(8,128)S(1)}, u32[]{:S(2)}, u32[]{:S(2)}) collective-permute-start(f32[3,2,56,128]{3,2,1,0:T(8,128)S(1)} %pad_maximum_fusion), channel_id=1, source_target_pairs={{12,0},{24,12},{36,24},{48,36},{60,48},{72,60},{84,72},{96,84},{10... | collective-permute-start | bytes 516104 | tf_op jit(solution)/shard_map/ppermute | solution.py:388
  89.9 5.3 %collective-permute-start.6 = (f32[3,1,72,128]{3,2,1,0:T(8,128)S(1)}, f32[3,1,72,128]{3,2,1,0:T(8,128)S(1)}, u32[]{:S(2)}, u32[]{:S(2)}) collective-permute-start(f32[3,1,72,128]{3,2,1,0:T(8,128)S(1)} %get-tuple-element.186), channel_id=1, source_target_pairs={{0,24},{12,36},{24,48},{36,60},{48,72},{60,84},{72,96},{84,108},{9... | collective-permute-start | bytes 331784 | tf_op jit(solution)/shard_map/ppermute | solution.py:387
  95.4 2.1 %collective-permute-start.9 = (f32[3,1,72,128]{3,2,1,0:T(8,128)S(1)}, f32[3,1,72,128]{3,2,1,0:T(8,128)S(1)}, u32[]{:S(2)}, u32[]{:S(2)}) collective-permute-start(f32[3,1,72,128]{3,2,1,0:T(8,128)S(1)} %get-tuple-element.185), channel_id=1, source_target_pairs={{24,0},{36,12},{48,24},{60,36},{72,48},{84,60},{96,72},{108,84},{1... | collective-permute-start | bytes 331784 | tf_op jit(solution)/shard_map/ppermute | solution.py:388
  97.6 7.7 %collective-permute-done.9 = f32[3,1,72,128]{3,2,1,0:T(8,128)S(1)} collective-permute-done((f32[3,1,72,128]{3,2,1,0:T(8,128)S(1)}, f32[3,1,72,128]{3,2,1,0:T(8,128)S(1)}, u32[]{:S(2)}, u32[]{:S(2)}) %collective-permute-start.9) | collective-permute-done | bytes 110624 | tf_op jit(solution)/shard_map/ppermute | solution.py:388
  106.0 0.7 copy-done.3
  106.7 0.4 fusion.101
  107.1 0.3 fusion.88
  107.5 0.4 fusion.80
  110.8 1.8 %slice_add_fusion.23 = f32[3,2,32,128]{3,2,1,0:T(8,128)} fusion(f32[3,4,34,128]{3,2,1,0:T(8,128)S(1)} %get-tuple-element.4, f32[3,6,36,128]{3,2,1,0:T(8,128)S(1)} %get-tuple-element.8, f32[3,8,38,128]{3,2,1,0:T(8,128)S(1)} %get-tuple-element.12, f32[3,10,40,128]{3,2,1,0:T(8,128)S(1)} %bitcast.594, f32[3,4,58,128]{3,2,1,0:T(8,128)} %copy-done.4, ...), kind=kLoop, calls=%fused_computation.349 | loop fusion | flops 147456 | bytes 786432 | tf_op jit(solution)/shard_map/add | solution.py:268
  113.2 0.7 slice_subtract_fusion.45
  (185 shorter events, 14.1 us)
Async XLA Ops:
  0.6 17.3 %copy-start.6 = (f32[2,32,128]{2,1,0:T(8,128)S(1)}, f32[2,32,128]{2,1,0:T(8,128)}, u32[]{:S(2)}) copy-start(f32[2,32,128]{2,1,0:T(8,128)} %param.6) | copy-start | bytes 98308
  0.6 17.3 %copy-start.7 = (f32[2,32,128]{2,1,0:T(8,128)S(1)}, f32[2,32,128]{2,1,0:T(8,128)}, u32[]{:S(2)}) copy-start(f32[2,32,128]{2,1,0:T(8,128)} %param.5) | copy-start | bytes 98308
  0.6 17.3 %copy-start.5 = (f32[3,2,32,128]{3,2,1,0:T(8,128)S(1)}, f32[3,2,32,128]{3,2,1,0:T(8,128)}, u32[]{:S(2)}) copy-start(f32[3,2,32,128]{3,2,1,0:T(8,128)} %param.4) | copy-start | bytes 294916
  1.6 16.2 %collective-permute-start = (f32[5,2,32,128]{3,2,1,0:T(8,128)S(1)}, f32[5,2,32,128]{3,2,1,0:T(8,128)S(1)}, u32[]{:S(2)}, u32[]{:S(2)}) collective-permute-start(f32[5,2,32,128]{3,2,1,0:T(8,128)S(1)} %pad_maximum_fusion.1), channel_id=1, source_target_pairs={{0,24},{12,36},{24,48},{36,60},{48,72},{60,84},{72,96},{84,108},{9... | collective-permute-start | bytes 491528 | tf_op jit(solution)/shard_map/ppermute | solution.py:216
  6.3 11.6 %collective-permute-start.1 = (f32[5,2,32,128]{3,2,1,0:T(8,128)S(1)}, f32[5,2,32,128]{3,2,1,0:T(8,128)S(1)}, u32[]{:S(2)}, u32[]{:S(2)}) collective-permute-start(f32[5,2,32,128]{3,2,1,0:T(8,128)S(1)} %pad_maximum_fusion.1), channel_id=1, source_target_pairs={{0,12},{12,24},{24,36},{36,48},{48,60},{60,72},{72,84},{84,96},{96... | collective-permute-start | bytes 491528 | tf_op jit(solution)/shard_map/ppermute | solution.py:216
  8.2 9.8 %collective-permute-start.2 = (f32[5,2,32,128]{3,2,1,0:T(8,128)S(1)}, f32[5,2,32,128]{3,2,1,0:T(8,128)S(1)}, u32[]{:S(2)}, u32[]{:S(2)}) collective-permute-start(f32[5,2,32,128]{3,2,1,0:T(8,128)S(1)} %pad_maximum_fusion.1), channel_id=1, source_target_pairs={{12,0},{24,12},{36,24},{48,36},{60,48},{72,60},{84,72},{96,84},{10... | collective-permute-start | bytes 491528 | tf_op jit(solution)/shard_map/ppermute | solution.py:217
  11.8 11.6 %collective-permute-start.3 = (f32[5,2,32,128]{3,2,1,0:T(8,128)S(1)}, f32[5,2,32,128]{3,2,1,0:T(8,128)S(1)}, u32[]{:S(2)}, u32[]{:S(2)}) collective-permute-start(f32[5,2,32,128]{3,2,1,0:T(8,128)S(1)} %pad_maximum_fusion.1), channel_id=1, source_target_pairs={{24,0},{36,12},{48,24},{60,36},{72,48},{84,60},{96,72},{108,84},{1... | collective-permute-start | bytes 491528 | tf_op jit(solution)/shard_map/ppermute | solution.py:217
  23.5 13.3 %collective-permute-start.5 = (f32[5,10,16,128]{3,2,1,0:T(8,128)S(1)}, f32[5,10,16,128]{3,2,1,0:T(8,128)S(1)}, u32[]{:S(2)}, u32[]{:S(2)}) collective-permute-start(f32[5,10,16,128]{3,2,1,0:T(8,128)S(1)} %get-tuple-element.52), channel_id=1, source_target_pairs={{1,0},{2,1},{3,2},{4,3},{5,4},{6,5},{7,6},{8,7},{9,8},{10,9},{11,1... | collective-permute-start | bytes 1228808 | tf_op jit(solution)/shard_map/ppermute | solution.py:226
  24.8 13.2 %collective-permute-start.4 = (f32[5,10,16,128]{3,2,1,0:T(8,128)S(1)}, f32[5,10,16,128]{3,2,1,0:T(8,128)S(1)}, u32[]{:S(2)}, u32[]{:S(2)}) collective-permute-start(f32[5,10,16,128]{3,2,1,0:T(8,128)S(1)} %get-tuple-element.51), channel_id=1, source_target_pairs={{0,1},{1,2},{2,3},{3,4},{4,5},{5,6},{6,7},{7,8},{8,9},{9,10},{10,1... | collective-permute-start | bytes 1228808 | tf_op jit(solution)/shard_map/ppermute | solution.py:225
  39.2 1.9 %copy-start = (f32[3,8,62,128]{3,2,1,0:T(8,128)}, f32[3,8,62,128]{3,2,1,0:T(8,128)S(1)}, u32[]{:S(2)}) copy-start(f32[3,8,62,128]{3,2,1,0:T(8,128)S(1)} %get-tuple-element.37) | copy-start | bytes 2285572
  41.4 1.4 %copy-start.1 = (f32[3,6,60,128]{3,2,1,0:T(8,128)}, f32[3,6,60,128]{3,2,1,0:T(8,128)S(1)}, u32[]{:S(2)}) copy-start(f32[3,6,60,128]{3,2,1,0:T(8,128)S(1)} %get-tuple-element.33) | copy-start | bytes 1658884
  43.0 0.7 copy-start.4
  44.2 4.0 %copy-start.2 = (f32[3,2,56,128]{3,2,1,0:T(8,128)}, f32[3,2,56,128]{3,2,1,0:T(8,128)S(1)}, u32[]{:S(2)}) copy-start(f32[3,2,56,128]{3,2,1,0:T(8,128)S(1)} %slice_subtract_fusion.14) | copy-start | bytes 516100
  83.1 0.9 slice-start
  84.0 13.5 %collective-permute-start.7 = (f32[3,2,56,128]{3,2,1,0:T(8,128)S(1)}, f32[3,2,56,128]{3,2,1,0:T(8,128)S(1)}, u32[]{:S(2)}, u32[]{:S(2)}) collective-permute-start(f32[3,2,56,128]{3,2,1,0:T(8,128)S(1)} %pad_maximum_fusion), channel_id=1, source_target_pairs={{0,12},{12,24},{24,36},{36,48},{48,60},{60,72},{72,84},{84,96},{96... | collective-permute-start | bytes 516104 | tf_op jit(solution)/shard_map/ppermute | solution.py:387
  85.9 11.7 %collective-permute-start.8 = (f32[3,2,56,128]{3,2,1,0:T(8,128)S(1)}, f32[3,2,56,128]{3,2,1,0:T(8,128)S(1)}, u32[]{:S(2)}, u32[]{:S(2)}) collective-permute-start(f32[3,2,56,128]{3,2,1,0:T(8,128)S(1)} %pad_maximum_fusion), channel_id=1, source_target_pairs={{12,0},{24,12},{36,24},{48,36},{60,48},{72,60},{84,72},{96,84},{10... | collective-permute-start | bytes 516104 | tf_op jit(solution)/shard_map/ppermute | solution.py:388
  89.9 7.6 %collective-permute-start.6 = (f32[3,1,72,128]{3,2,1,0:T(8,128)S(1)}, f32[3,1,72,128]{3,2,1,0:T(8,128)S(1)}, u32[]{:S(2)}, u32[]{:S(2)}) collective-permute-start(f32[3,1,72,128]{3,2,1,0:T(8,128)S(1)} %get-tuple-element.186), channel_id=1, source_target_pairs={{0,24},{12,36},{24,48},{36,60},{48,72},{60,84},{72,96},{84,108},{9... | collective-permute-start | bytes 331784 | tf_op jit(solution)/shard_map/ppermute | solution.py:387
  95.4 10.0 %collective-permute-start.9 = (f32[3,1,72,128]{3,2,1,0:T(8,128)S(1)}, f32[3,1,72,128]{3,2,1,0:T(8,128)S(1)}, u32[]{:S(2)}, u32[]{:S(2)}) collective-permute-start(f32[3,1,72,128]{3,2,1,0:T(8,128)S(1)} %get-tuple-element.185), channel_id=1, source_target_pairs={{24,0},{36,12},{48,24},{60,36},{72,48},{84,60},{96,72},{108,84},{1... | collective-permute-start | bytes 331784 | tf_op jit(solution)/shard_map/ppermute | solution.py:388
  105.8 0.9 copy-start.3

commit v8 on v7

--- a/solution.py
+++ b/solution.py
@@ -299,9 +299,9 @@
     coarse_y = width_y // 2
     coarse_z = width_z // 2
     fine_reach = depth + 1
-    res_rows = COARSE_SWEEPS + (depth + 2) // 2
-    coef_rows = res_rows + 2
-    deep_y = 2 * coef_rows
+    res_rows = COARSE_SWEEPS + (depth + 2) // 2 - 1
+    coef_rows = res_rows + 1
+    deep_y = 2 * res_rows + depth + 1
 
     stacked = jnp.concatenate([rhs_field, shear_modulus[None], lame_lambda[None]], axis=0)
     stacked = halo_x(stacked, depth + 1)

time: 114 us -> 122 us (1.070)
  other arithmetic: 16.9 us -> 24.8 us
  blocking collectives: 33.6 us -> 30.4 us
  starting transfers between devices: 31.3 us -> 33 us
    ppermute x1, waiting for transfers between devices: 1.18 us -> 5.59 us  [halo_y(): low = lax.ppermute(array[..., -depth:, :], 'gy', forward)]
    psum x1, blocking collectives: 33.6 us -> 30.4 us  [shards(): all_sums = lax.psum(slots, 'gy')]
    ppermute x2, waiting for transfers between devices: 5.45 us -> 3.09 us  [halo_x(): highs.append(lax.ppermute(array[..., :need, :, :], 'gx', backward))]
    ppermute x2, starting transfers between devices: 7.23 us -> 9.59 us  [shards(): got_low = lax.ppermute(send_low, 'gx', forward)]
    ppermute x1, waiting for transfers between devices: 7 us -> 4.76 us  [halo_y(): high = lax.ppermute(array[..., :depth, :], 'gy', backward)]
    mul x9, other arithmetic: 1.31 us -> 3.15 us  [operate(): results.append(scale * (-laplace[comp_id] - grad_term))]
  transfers between devices with their start and end apart: 10 -> 10, of which waited for: 4 -> 4; matrix products, arithmetic and copies ran while one was open for 4% -> 7% of each run, Pallas kernels for 0% -> 0%
where the time goes in v8:
time: 122 us; the launch traced here: 121 us
  starting transfers between devices  33 us (27%)
  blocking collectives  30.4 us (25%)
  other arithmetic  24.8 us (20%)
  waiting for transfers between devices  21.2 us (17%)
  local copies, waits for them, and re-layouts  8.92 us (7%)
  between operations  1.61 us (1%)
  matrix products  1.33 us (1%)
    psum x1, blocking collectives, shards(): all_sums = lax.psum(slots, 'gy')  30.4 us
    ppermute x2, starting transfers between devices, shards(): got_low = lax.ppermute(send_low, 'gx', forward)  9.59 us
    ppermute x2, waiting for transfers between devices, shards(): got_high = lax.ppermute(send_high, 'gx', backward)  7.67 us
    ppermute x2, starting transfers between devices, halo_x(): lows.append(lax.ppermute(array[..., width - need:, :, :], 'gx', forward))  6.53 us
    ppermute x2, starting transfers between devices, shards(): got_high = lax.ppermute(send_high, 'gx', backward)  5.74 us
    ppermute x1, waiting for transfers between devices, halo_y(): low = lax.ppermute(array[..., -depth:, :], 'gy', forward)  5.59 us
    ppermute x2, starting transfers between devices, halo_x(): highs.append(lax.ppermute(array[..., :need, :, :], 'gx', backward))  5.56 us
    another operation x21, other arithmetic, apply_ext(): return jnp.stack(results)  5.46 us
  transfers between devices with their start and end apart: 10, of which 4 were waited for; matrix products, arithmetic and copies ran while one was open for 7% of the time, Pallas kernels for 0%

profile of v8, /device:TPU:30, one launch (start us, length us, event | category | flops | bytes accessed | tf_op | source)
XLA Modules:
  0.0 121.3 jit_solution(1140312135143607355)
XLA Ops:
  0.6 0.9 pad_maximum_fusion.2
  1.6 4.6 %collective-permute-start = (f32[5,2,32,128]{3,2,1,0:T(8,128)S(1)}, f32[5,2,32,128]{3,2,1,0:T(8,128)S(1)}, u32[]{:S(2)}, u32[]{:S(2)}) collective-permute-start(f32[5,2,32,128]{3,2,1,0:T(8,128)S(1)} %pad_maximum_fusion.2), channel_id=1, source_target_pairs={{0,24},{12,36},{24,48},{36,60},{48,72},{60,84},{72,96},{84,108},{9... | collective-permute-start | bytes 491528 | tf_op jit(solution)/shard_map/ppermute | solution.py:216
  6.2 1.9 %collective-permute-start.1 = (f32[5,2,32,128]{3,2,1,0:T(8,128)S(1)}, f32[5,2,32,128]{3,2,1,0:T(8,128)S(1)}, u32[]{:S(2)}, u32[]{:S(2)}) collective-permute-start(f32[5,2,32,128]{3,2,1,0:T(8,128)S(1)} %pad_maximum_fusion.2), channel_id=1, source_target_pairs={{0,12},{12,24},{24,36},{36,48},{48,60},{60,72},{72,84},{84,96},{96... | collective-permute-start | bytes 491528 | tf_op jit(solution)/shard_map/ppermute | solution.py:216
  8.1 3.6 %collective-permute-start.2 = (f32[5,2,32,128]{3,2,1,0:T(8,128)S(1)}, f32[5,2,32,128]{3,2,1,0:T(8,128)S(1)}, u32[]{:S(2)}, u32[]{:S(2)}) collective-permute-start(f32[5,2,32,128]{3,2,1,0:T(8,128)S(1)} %pad_maximum_fusion.2), channel_id=1, source_target_pairs={{12,0},{24,12},{36,24},{48,36},{60,48},{72,60},{84,72},{96,84},{10... | collective-permute-start | bytes 491528 | tf_op jit(solution)/shard_map/ppermute | solution.py:217
  11.8 1.9 %collective-permute-start.3 = (f32[5,2,32,128]{3,2,1,0:T(8,128)S(1)}, f32[5,2,32,128]{3,2,1,0:T(8,128)S(1)}, u32[]{:S(2)}, u32[]{:S(2)}) collective-permute-start(f32[5,2,32,128]{3,2,1,0:T(8,128)S(1)} %pad_maximum_fusion.2), channel_id=1, source_target_pairs={{24,0},{36,12},{48,24},{60,36},{72,48},{84,60},{96,72},{108,84},{1... | collective-permute-start | bytes 491528 | tf_op jit(solution)/shard_map/ppermute | solution.py:217
  14.9 0.7 compare_select_fusion.7
  16.4 1.3 %constant_dynamic-slice_fusion.1 = (s32[1,1]{1,0:T(1,128)}, s32[1,1]{1,0:T(1,128)}) fusion(s32[1,12]{1,0:T(1,128)} %param.7, s32[]{:T(128)S(6)} %select_n.116, s32[]{:T(128)S(6)} %select_n.117), kind=kLoop, calls=%fused_computation.877 | loop fusion | bytes 24 | tf_op jit(solution)/shard_map/jit(dynamic_index_in_dim)/dynamic_slice | solution.py:345
  17.8 1.4 %compare_select_fusion.8 = f32[2]{0:T(128)S(1)} fusion(s32[1]{0:T(128)} %bitcast.32, s32[1]{0:T(128)} %bitcast.31), kind=kLoop, calls=%fused_computation.860 | loop fusion | flops 6 | bytes 16 | tf_op jit(solution)/shard_map/jit(_where)/select_n | solution.py:101
  19.3 0.9 constant_dynamic-update-slice_fusion.2
  20.3 3.1 %collective-permute-done.3 = f32[5,2,32,128]{3,2,1,0:T(8,128)S(1)} collective-permute-done((f32[5,2,32,128]{3,2,1,0:T(8,128)S(1)}, f32[5,2,32,128]{3,2,1,0:T(8,128)S(1)}, u32[]{:S(2)}, u32[]{:S(2)}) %collective-permute-start.3) | collective-permute-done | bytes 163872 | tf_op jit(solution)/shard_map/ppermute | solution.py:217
  23.5 4.3 %collective-permute-start.4 = (f32[5,10,14,128]{3,2,1,0:T(8,128)S(1)}, f32[5,10,14,128]{3,2,1,0:T(8,128)S(1)}, u32[]{:S(2)}, u32[]{:S(2)}) collective-permute-start(f32[5,10,14,128]{3,2,1,0:T(8,128)S(1)} %get-tuple-element.51), channel_id=1, source_target_pairs={{0,1},{1,2},{2,3},{3,4},{4,5},{5,6},{6,7},{7,8},{8,9},{9,10},{10,1... | collective-permute-start | bytes 1075208 | tf_op jit(solution)/shard_map/ppermute | solution.py:225
  27.8 1.3 %collective-permute-start.5 = (f32[5,10,14,128]{3,2,1,0:T(8,128)S(1)}, f32[5,10,14,128]{3,2,1,0:T(8,128)S(1)}, u32[]{:S(2)}, u32[]{:S(2)}) collective-permute-start(f32[5,10,14,128]{3,2,1,0:T(8,128)S(1)} %get-tuple-element.52), channel_id=1, source_target_pairs={{1,0},{2,1},{3,2},{4,3},{5,4},{6,5},{7,6},{8,7},{9,8},{10,9},{11,1... | collective-permute-start | bytes 1075208 | tf_op jit(solution)/shard_map/ppermute | solution.py:226
  30.4 5.6 %collective-permute-done.4 = f32[5,10,14,128]{3,2,1,0:T(8,128)S(1)} collective-permute-done((f32[5,10,14,128]{3,2,1,0:T(8,128)S(1)}, f32[5,10,14,128]{3,2,1,0:T(8,128)S(1)}, u32[]{:S(2)}, u32[]{:S(2)}) %collective-permute-start.4) | collective-permute-done | bytes 358432 | tf_op jit(solution)/shard_map/ppermute | solution.py:225
  36.0 4.8 %collective-permute-done.5 = f32[5,10,14,128]{3,2,1,0:T(8,128)S(1)} collective-permute-done((f32[5,10,14,128]{3,2,1,0:T(8,128)S(1)}, f32[5,10,14,128]{3,2,1,0:T(8,128)S(1)}, u32[]{:S(2)}, u32[]{:S(2)}) %collective-permute-start.5) | collective-permute-done | bytes 358432 | tf_op jit(solution)/shard_map/ppermute | solution.py:226
  50.3 0.8 fusion.369
  51.1 0.8 fusion.350
  51.8 0.7 fusion.332
  53.9 30.4 %psum.7 = f32[12,3]{0,1:T(4,128)} all-reduce(f32[12,3]{0,1:T(4,128)S(1)} %broadcast_select_fusion), channel_id=1, replica_groups=mesh['gx'=64,'gy'=12] {'gy'}, use_global_device_ids=true, to_apply=%region_6.7 | all-reduce | flops 36 | bytes 288 | tf_op jit(solution)/shard_map/psum | solution.py:334
  84.3 0.7 multiply_reduce_fusion
  85.8 0.7 gather_fusion
  86.5 0.7 select_bitcast_fusion
  87.6 0.8 pad_maximum_fusion.8
  88.4 0.7 multiply_add_fusion.1
  89.1 0.8 fusion.498
  89.9 0.9 convolution_bitcast_fusion
  90.9 1.9 %collective-permute-start.7 = (f32[3,2,56,128]{3,2,1,0:T(8,128)S(1)}, f32[3,2,56,128]{3,2,1,0:T(8,128)S(1)}, u32[]{:S(2)}, u32[]{:S(2)}) collective-permute-start(f32[3,2,56,128]{3,2,1,0:T(8,128)S(1)} %pad_maximum_fusion.1), channel_id=1, source_target_pairs={{0,12},{12,24},{24,36},{36,48},{48,60},{60,72},{72,84},{84,96},{96... | collective-permute-start | bytes 516104 | tf_op jit(solution)/shard_map/ppermute | solution.py:387
  92.8 3.6 %collective-permute-start.8 = (f32[3,2,56,128]{3,2,1,0:T(8,128)S(1)}, f32[3,2,56,128]{3,2,1,0:T(8,128)S(1)}, u32[]{:S(2)}, u32[]{:S(2)}) collective-permute-start(f32[3,2,56,128]{3,2,1,0:T(8,128)S(1)} %pad_maximum_fusion.1), channel_id=1, source_target_pairs={{12,0},{24,12},{36,24},{48,36},{60,48},{72,60},{84,72},{96,84},{10... | collective-permute-start | bytes 516104 | tf_op jit(solution)/shard_map/ppermute | solution.py:388
  96.8 7.7 %collective-permute-start.6 = (f32[3,1,72,128]{3,2,1,0:T(8,128)S(1)}, f32[3,1,72,128]{3,2,1,0:T(8,128)S(1)}, u32[]{:S(2)}, u32[]{:S(2)}) collective-permute-start(f32[3,1,72,128]{3,2,1,0:T(8,128)S(1)} %get-tuple-element.186), channel_id=1, source_target_pairs={{0,24},{12,36},{24,48},{36,60},{48,72},{60,84},{72,96},{84,108},{9... | collective-permute-start | bytes 331784 | tf_op jit(solution)/shard_map/ppermute | solution.py:387
  104.6 2.1 %collective-permute-start.9 = (f32[3,1,72,128]{3,2,1,0:T(8,128)S(1)}, f32[3,1,72,128]{3,2,1,0:T(8,128)S(1)}, u32[]{:S(2)}, u32[]{:S(2)}) collective-permute-start(f32[3,1,72,128]{3,2,1,0:T(8,128)S(1)} %get-tuple-element.185), channel_id=1, source_target_pairs={{24,0},{36,12},{48,24},{60,36},{72,48},{84,60},{96,72},{108,84},{1... | collective-permute-start | bytes 331784 | tf_op jit(solution)/shard_map/ppermute | solution.py:388
  106.9 7.7 %collective-permute-done.9 = f32[3,1,72,128]{3,2,1,0:T(8,128)S(1)} collective-permute-done((f32[3,1,72,128]{3,2,1,0:T(8,128)S(1)}, f32[3,1,72,128]{3,2,1,0:T(8,128)S(1)}, u32[]{:S(2)}, u32[]{:S(2)}) %collective-permute-start.9) | collective-permute-done | bytes 110624 | tf_op jit(solution)/shard_map/ppermute | solution.py:388
  119.5 0.7 slice_add_fusion.23
  120.6 0.7 slice_subtract_fusion.46
  (186 shorter events, 20.8 us)
Async XLA Ops:
  1.6 17.7 %collective-permute-start = (f32[5,2,32,128]{3,2,1,0:T(8,128)S(1)}, f32[5,2,32,128]{3,2,1,0:T(8,128)S(1)}, u32[]{:S(2)}, u32[]{:S(2)}) collective-permute-start(f32[5,2,32,128]{3,2,1,0:T(8,128)S(1)} %pad_maximum_fusion.2), channel_id=1, source_target_pairs={{0,24},{12,36},{24,48},{36,60},{48,72},{60,84},{72,96},{84,108},{9... | collective-permute-start | bytes 491528 | tf_op jit(solution)/shard_map/ppermute | solution.py:216
  6.2 13.1 %collective-permute-start.1 = (f32[5,2,32,128]{3,2,1,0:T(8,128)S(1)}, f32[5,2,32,128]{3,2,1,0:T(8,128)S(1)}, u32[]{:S(2)}, u32[]{:S(2)}) collective-permute-start(f32[5,2,32,128]{3,2,1,0:T(8,128)S(1)} %pad_maximum_fusion.2), channel_id=1, source_target_pairs={{0,12},{12,24},{24,36},{36,48},{48,60},{60,72},{72,84},{84,96},{96... | collective-permute-start | bytes 491528 | tf_op jit(solution)/shard_map/ppermute | solution.py:216
  8.1 12.1 %collective-permute-start.2 = (f32[5,2,32,128]{3,2,1,0:T(8,128)S(1)}, f32[5,2,32,128]{3,2,1,0:T(8,128)S(1)}, u32[]{:S(2)}, u32[]{:S(2)}) collective-permute-start(f32[5,2,32,128]{3,2,1,0:T(8,128)S(1)} %pad_maximum_fusion.2), channel_id=1, source_target_pairs={{12,0},{24,12},{36,24},{48,36},{60,48},{72,60},{84,72},{96,84},{10... | collective-permute-start | bytes 491528 | tf_op jit(solution)/shard_map/ppermute | solution.py:217
  11.8 11.6 %collective-permute-start.3 = (f32[5,2,32,128]{3,2,1,0:T(8,128)S(1)}, f32[5,2,32,128]{3,2,1,0:T(8,128)S(1)}, u32[]{:S(2)}, u32[]{:S(2)}) collective-permute-start(f32[5,2,32,128]{3,2,1,0:T(8,128)S(1)} %pad_maximum_fusion.2), channel_id=1, source_target_pairs={{24,0},{36,12},{48,24},{60,36},{72,48},{84,60},{96,72},{108,84},{1... | collective-permute-start | bytes 491528 | tf_op jit(solution)/shard_map/ppermute | solution.py:217
  13.7 33.0 %copy-start.6 = (s32[128]{0:T(128)}, s32[128]{0:T(128)S(1)}, u32[]{:S(2)}) copy-start(s32[128]{0:T(128)S(1)} %and_select_fusion) | copy-start | bytes 1540
  14.9 34.6 %copy-start.5 = (pred[3]{0:T(512)(128)(4,1)}, pred[3]{0:T(512)(128)(4,1)S(1)}, u32[]{:S(2)}) copy-start(pred[3]{0:T(512)(128)(4,1)S(1)} %get-tuple-element.202) | copy-start | bytes 13
  23.5 12.6 %collective-permute-start.4 = (f32[5,10,14,128]{3,2,1,0:T(8,128)S(1)}, f32[5,10,14,128]{3,2,1,0:T(8,128)S(1)}, u32[]{:S(2)}, u32[]{:S(2)}) collective-permute-start(f32[5,10,14,128]{3,2,1,0:T(8,128)S(1)} %get-tuple-element.51), channel_id=1, source_target_pairs={{0,1},{1,2},{2,3},{3,4},{4,5},{5,6},{6,7},{7,8},{8,9},{9,10},{10,1... | collective-permute-start | bytes 1075208 | tf_op jit(solution)/shard_map/ppermute | solution.py:225
  27.8 13.0 %collective-permute-start.5 = (f32[5,10,14,128]{3,2,1,0:T(8,128)S(1)}, f32[5,10,14,128]{3,2,1,0:T(8,128)S(1)}, u32[]{:S(2)}, u32[]{:S(2)}) collective-permute-start(f32[5,10,14,128]{3,2,1,0:T(8,128)S(1)} %get-tuple-element.52), channel_id=1, source_target_pairs={{1,0},{2,1},{3,2},{4,3},{5,4},{6,5},{7,6},{8,7},{9,8},{10,9},{11,1... | collective-permute-start | bytes 1075208 | tf_op jit(solution)/shard_map/ppermute | solution.py:226
  49.1 2.7 %copy-start.2 = (f32[3,1,16,64]{3,2,0,1:T(8,128)}, f32[3,1,16,64]{3,2,0,1:T(8,128)S(1)}, u32[]{:S(2)}) copy-start(f32[3,1,16,64]{3,2,0,1:T(8,128)S(1)} %get-tuple-element.23) | copy-start | bytes 36868
  49.3 0.6 copy-start.3
  49.4 0.6 copy-start.4
  49.6 4.3 %copy-start.7 = (pred[12]{0:T(512)(128)(4,1)S(1)}, pred[12]{0:T(512)(128)(4,1)}, u32[]{:S(2)}) copy-start(pred[12]{0:T(512)(128)(4,1)} %iota_compare_fusion.9) | copy-start | bytes 40
  87.5 3.3 %copy-start = (f32[3,2,40,128]{3,2,1,0:T(8,128)S(1)}, f32[3,2,40,128]{3,2,1,0:T(8,128)}, u32[]{:S(2)}) copy-start(f32[3,2,40,128]{3,2,1,0:T(8,128)} %slice.2646) | copy-start | bytes 368644
  88.4 8.4 %copy-start.1 = (f32[3,1,40,128]{3,2,1,0:T(8,128)S(1)}, f32[3,1,40,128]{3,2,1,0:T(8,128)}, u32[]{:S(2)}) copy-start(f32[3,1,40,128]{3,2,1,0:T(8,128)} %get-tuple-element.124) | copy-start | bytes 184324
  90.9 15.9 %collective-permute-start.7 = (f32[3,2,56,128]{3,2,1,0:T(8,128)S(1)}, f32[3,2,56,128]{3,2,1,0:T(8,128)S(1)}, u32[]{:S(2)}, u32[]{:S(2)}) collective-permute-start(f32[3,2,56,128]{3,2,1,0:T(8,128)S(1)} %pad_maximum_fusion.1), channel_id=1, source_target_pairs={{0,12},{12,24},{24,36},{36,48},{48,60},{60,72},{72,84},{84,96},{96... | collective-permute-start | bytes 516104 | tf_op jit(solution)/shard_map/ppermute | solution.py:387
  92.8 14.1 %collective-permute-start.8 = (f32[3,2,56,128]{3,2,1,0:T(8,128)S(1)}, f32[3,2,56,128]{3,2,1,0:T(8,128)S(1)}, u32[]{:S(2)}, u32[]{:S(2)}) collective-permute-start(f32[3,2,56,128]{3,2,1,0:T(8,128)S(1)} %pad_maximum_fusion.1), channel_id=1, source_target_pairs={{12,0},{24,12},{36,24},{48,36},{60,48},{72,60},{84,72},{96,84},{10... | collective-permute-start | bytes 516104 | tf_op jit(solution)/shard_map/ppermute | solution.py:388
  96.8 10.0 %collective-permute-start.6 = (f32[3,1,72,128]{3,2,1,0:T(8,128)S(1)}, f32[3,1,72,128]{3,2,1,0:T(8,128)S(1)}, u32[]{:S(2)}, u32[]{:S(2)}) collective-permute-start(f32[3,1,72,128]{3,2,1,0:T(8,128)S(1)} %get-tuple-element.186), channel_id=1, source_target_pairs={{0,24},{12,36},{24,48},{36,60},{48,72},{60,84},{72,96},{84,108},{9... | collective-permute-start | bytes 331784 | tf_op jit(solution)/shard_map/ppermute | solution.py:387
  104.6 10.0 %collective-permute-start.9 = (f32[3,1,72,128]{3,2,1,0:T(8,128)S(1)}, f32[3,1,72,128]{3,2,1,0:T(8,128)S(1)}, u32[]{:S(2)}, u32[]{:S(2)}) collective-permute-start(f32[3,1,72,128]{3,2,1,0:T(8,128)S(1)} %get-tuple-element.185), channel_id=1, source_target_pairs={{24,0},{36,12},{48,24},{60,36},{72,48},{84,60},{96,72},{108,84},{1... | collective-permute-start | bytes 331784 | tf_op jit(solution)/shard_map/ppermute | solution.py:388

commit v9 on v7

--- a/solution.py
+++ b/solution.py
@@ -218,6 +218,42 @@
     return jnp.concatenate(lows + [array] + highs[::-1], axis=-3)
 
 
+def halo_x_split(array, depth_rhs, depth_coef):
+    count = lax.axis_size("gx")
+    width = array.shape[-3]
+    reach = (depth_coef + width - 1) // width
+    lows, highs = [], []
+    for dx in range(reach, 0, -1):
+        need = min(width, depth_coef - (dx - 1) * width)
+        need_rhs = max(0, min(width, depth_rhs - (dx - 1) * width))
+        forward = [(i, i + dx) for i in range(count - dx)]
+        backward = [(i + dx, i) for i in range(count - dx)]
+        if need_rhs == need:
+            lows.append(lax.ppermute(array[..., width - need :, :, :], "gx", forward))
+            highs.append(lax.ppermute(array[..., :need, :, :], "gx", backward))
+            continue
+        rest = need - need_rhs
+
+        def pack(rhs_part, coef_part):
+            flat = coef_part.reshape((-1, 1) + coef_part.shape[2:])
+            return jnp.concatenate([rhs_part.reshape((-1, 1) + rhs_part.shape[2:]), flat], axis=0)
+
+        def unpack(got, rhs_first):
+            rhs_part = got[: 3 * need_rhs].reshape((3, need_rhs) + got.shape[2:])
+            coef_part = got[3 * need_rhs :].reshape((2, need) + got.shape[2:])
+            gap = jnp.zeros((3, rest) + got.shape[2:], got.dtype)
+            rhs_full = jnp.concatenate([gap, rhs_part] if rhs_first else [rhs_part, gap], axis=1)
+            return jnp.concatenate([rhs_full, coef_part], axis=0)
+
+        got_low = lax.ppermute(
+            pack(array[:3, width - need_rhs :], array[3:, width - need :]), "gx", forward
+        )
+        got_high = lax.ppermute(pack(array[:3, :need_rhs], array[3:, :need]), "gx", backward)
+        lows.append(unpack(got_low, True))
+        highs.append(unpack(got_high, False))
+    return jnp.concatenate(lows + [array] + highs[::-1], axis=-3)
+
+
 def halo_y(array, depth):
     count = lax.axis_size("gy")
     forward = [(i, i + 1) for i in range(count - 1)]
@@ -304,7 +340,7 @@
     deep_y = 2 * coef_rows
 
     stacked = jnp.concatenate([rhs_field, shear_modulus[None], lame_lambda[None]], axis=0)
-    stacked = halo_x(stacked, depth + 1)
+    stacked = halo_x_split(stacked, depth, depth + 1)
     stacked = halo_y(stacked, deep_y)
     mu_ext = stacked[3]
     lam_ext = stacked[4]

time: 114 us -> 115 us (level)
  starting transfers between devices: 31.3 us -> 34.7 us
  waiting for transfers between devices: 21.4 us -> 18.5 us
    ppermute x4, starting transfers between devices: 12.1 us -> 15.5 us  [the longest x1 8.06 us: halo_x_split(): lax.ppermute(pack(array[:3, width - need_rhs:], array[3:, width - need:])...]
    ppermute x1, waiting for transfers between devices: 7 us -> 3.88 us  [halo_y(): high = lax.ppermute(array[..., :depth, :], 'gy', backward)]
where the time goes in v9:
time: 115 us
  starting transfers between devices  34.7 us (30%)
  blocking collectives  33.9 us (29%)
  waiting for transfers between devices  18.5 us (16%)
  other arithmetic  17 us (15%)
  local copies, waits for them, and re-layouts  8.41 us (7%)
  between operations  1.74 us (2%)
    psum x1, blocking collectives, shards(): all_sums = lax.psum(slots, 'gy')  33.9 us
    ppermute x1, starting transfers between devices, halo_x_split(): lax.ppermute(pack(array[:3, width - need_rhs:], array[3:, width - need:])...  8.06 us
    ppermute x2, waiting for transfers between devices, shards(): got_high = lax.ppermute(send_high, 'gx', backward)  7.71 us
    ppermute x2, starting transfers between devices, shards(): got_low = lax.ppermute(send_low, 'gx', forward)  7.16 us
    ppermute x2, starting transfers between devices, shards(): got_high = lax.ppermute(send_high, 'gx', backward)  5.74 us
    another operation x21, other arithmetic, apply_ext(): return jnp.stack(results)  5.7 us
    ppermute x1, waiting for transfers between devices, halo_x_split(): lax.ppermute(pack(array[:3, :need_rhs], array[3:, :need]), 'gx', backward)  5.34 us
    ppermute x1, starting transfers between devices, halo_y(): low = lax.ppermute(array[..., -depth:, :], 'gy', forward)  4.93 us
  transfers between devices with their start and end apart: 10, of which 4 were waited for; matrix products, arithmetic and copies ran while one was open for 4% of the time, Pallas kernels for 0%

profile of v9, /device:TPU:30, one launch (start us, length us, event | category | flops | bytes accessed | tf_op | source)
XLA Modules:
  0.0 114.8 jit_solution(8018795077345941170)
XLA Ops:
  0.6 0.9 pad_maximum_fusion.1
  1.6 1.9 %collective-permute-start.1 = (f32[5,2,32,128]{3,2,1,0:T(8,128)S(1)}, f32[5,2,32,128]{3,2,1,0:T(8,128)S(1)}, u32[]{:S(2)}, u32[]{:S(2)}) collective-permute-start(f32[5,2,32,128]{3,2,1,0:T(8,128)S(1)} %pad_maximum_fusion.1), channel_id=1, source_target_pairs={{0,12},{12,24},{24,36},{36,48},{48,60},{60,72},{72,84},{84,96},{96... | collective-permute-start | bytes 491528 | tf_op jit(solution)/shard_map/ppermute | solution.py:232
  3.5 3.6 %collective-permute-start.2 = (f32[5,2,32,128]{3,2,1,0:T(8,128)S(1)}, f32[5,2,32,128]{3,2,1,0:T(8,128)S(1)}, u32[]{:S(2)}, u32[]{:S(2)}) collective-permute-start(f32[5,2,32,128]{3,2,1,0:T(8,128)S(1)} %pad_maximum_fusion.1), channel_id=1, source_target_pairs={{12,0},{24,12},{36,24},{48,36},{60,48},{72,60},{84,72},{96,84},{10... | collective-permute-start | bytes 491528 | tf_op jit(solution)/shard_map/ppermute | solution.py:233
  7.2 0.8 pad_maximum_fusion.10
  8.0 0.8 fusion.540
  8.8 8.1 %collective-permute-start = (f32[7,1,32,128]{3,2,1,0:T(8,128)S(1)}, f32[7,1,32,128]{3,2,1,0:T(8,128)S(1)}, u32[]{:S(2)}, u32[]{:S(2)}) collective-permute-start(f32[7,1,32,128]{3,2,1,0:T(8,128)S(1)} %get-tuple-element.188), channel_id=1, source_target_pairs={{0,24},{12,36},{24,48},{36,60},{48,72},{60,84},{72,96},{84,108},{9... | collective-permute-start | bytes 344072 | tf_op jit(solution)/shard_map/ppermute | solution.py:248
  16.9 1.9 %collective-permute-start.3 = (f32[7,1,32,128]{3,2,1,0:T(8,128)S(1)}, f32[7,1,32,128]{3,2,1,0:T(8,128)S(1)}, u32[]{:S(2)}, u32[]{:S(2)}) collective-permute-start(f32[7,1,32,128]{3,2,1,0:T(8,128)S(1)} %get-tuple-element.187), channel_id=1, source_target_pairs={{24,0},{36,12},{48,24},{60,36},{72,48},{84,60},{96,72},{108,84},{1... | collective-permute-start | bytes 344072 | tf_op jit(solution)/shard_map/ppermute | solution.py:251
  19.3 0.6 constant_dynamic-slice_fusion.1
  19.9 1.4 %compare_select_fusion.8 = f32[2]{0:T(128)S(1)} fusion(s32[1]{0:T(128)} %bitcast.35, s32[1]{0:T(128)} %bitcast.34), kind=kLoop, calls=%fused_computation.866 | loop fusion | flops 6 | bytes 16 | tf_op jit(solution)/shard_map/jit(_where)/select_n | solution.py:101
  21.6 5.3 %collective-permute-done.3 = f32[7,1,32,128]{3,2,1,0:T(8,128)S(1)} collective-permute-done((f32[7,1,32,128]{3,2,1,0:T(8,128)S(1)}, f32[7,1,32,128]{3,2,1,0:T(8,128)S(1)}, u32[]{:S(2)}, u32[]{:S(2)}) %collective-permute-start.3) | collective-permute-done | bytes 114720 | tf_op jit(solution)/shard_map/ppermute | solution.py:251
  27.2 1.3 %collective-permute-start.5 = (f32[5,10,16,128]{3,2,1,0:T(8,128)S(1)}, f32[5,10,16,128]{3,2,1,0:T(8,128)S(1)}, u32[]{:S(2)}, u32[]{:S(2)}) collective-permute-start(f32[5,10,16,128]{3,2,1,0:T(8,128)S(1)} %get-tuple-element.52), channel_id=1, source_target_pairs={{1,0},{2,1},{3,2},{4,3},{5,4},{6,5},{7,6},{8,7},{9,8},{10,9},{11,1... | collective-permute-start | bytes 1228808 | tf_op jit(solution)/shard_map/ppermute | solution.py:262
  28.5 4.9 %collective-permute-start.4 = (f32[5,10,16,128]{3,2,1,0:T(8,128)S(1)}, f32[5,10,16,128]{3,2,1,0:T(8,128)S(1)}, u32[]{:S(2)}, u32[]{:S(2)}) collective-permute-start(f32[5,10,16,128]{3,2,1,0:T(8,128)S(1)} %get-tuple-element.51), channel_id=1, source_target_pairs={{0,1},{1,2},{2,3},{3,4},{4,5},{5,6},{6,7},{7,8},{8,9},{9,10},{10,1... | collective-permute-start | bytes 1228808 | tf_op jit(solution)/shard_map/ppermute | solution.py:261
  33.5 3.9 %collective-permute-done.5 = f32[5,10,16,128]{3,2,1,0:T(8,128)S(1)} collective-permute-done((f32[5,10,16,128]{3,2,1,0:T(8,128)S(1)}, f32[5,10,16,128]{3,2,1,0:T(8,128)S(1)}, u32[]{:S(2)}, u32[]{:S(2)}) %collective-permute-start.5) | collective-permute-done | bytes 409632 | tf_op jit(solution)/shard_map/ppermute | solution.py:262
  37.4 1.5 %collective-permute-done.4 = f32[5,10,16,128]{3,2,1,0:T(8,128)S(1)} collective-permute-done((f32[5,10,16,128]{3,2,1,0:T(8,128)S(1)}, f32[5,10,16,128]{3,2,1,0:T(8,128)S(1)}, u32[]{:S(2)}, u32[]{:S(2)}) %collective-permute-start.4) | collective-permute-done | bytes 409632 | tf_op jit(solution)/shard_map/ppermute | solution.py:261
  40.6 0.5 fusion.62
  41.1 0.4 fusion.49
  41.4 0.5 fusion.41
  43.2 0.3 fusion.121
  44.1 0.4 copy-done.4
  49.1 33.9 %psum.7 = f32[12,3]{0,1:T(4,128)S(1)} all-reduce(f32[12,3]{0,1:T(4,128)S(1)} %broadcast_select_fusion), channel_id=1, replica_groups=mesh['gx'=64,'gy'=12] {'gy'}, use_global_device_ids=true, to_apply=%region_6.7 | all-reduce | flops 36 | bytes 288 | tf_op jit(solution)/shard_map/psum | solution.py:370
  83.2 0.6 gather_fusion
  84.5 0.5 slice-done
  85.1 1.9 %collective-permute-start.7 = (f32[3,2,56,128]{3,2,1,0:T(8,128)S(1)}, f32[3,2,56,128]{3,2,1,0:T(8,128)S(1)}, u32[]{:S(2)}, u32[]{:S(2)}) collective-permute-start(f32[3,2,56,128]{3,2,1,0:T(8,128)S(1)} %pad_maximum_fusion), channel_id=1, source_target_pairs={{0,12},{12,24},{24,36},{36,48},{48,60},{60,72},{72,84},{84,96},{96... | collective-permute-start | bytes 516104 | tf_op jit(solution)/shard_map/ppermute | solution.py:423
  87.0 3.6 %collective-permute-start.8 = (f32[3,2,56,128]{3,2,1,0:T(8,128)S(1)}, f32[3,2,56,128]{3,2,1,0:T(8,128)S(1)}, u32[]{:S(2)}, u32[]{:S(2)}) collective-permute-start(f32[3,2,56,128]{3,2,1,0:T(8,128)S(1)} %pad_maximum_fusion), channel_id=1, source_target_pairs={{12,0},{24,12},{36,24},{48,36},{60,48},{72,60},{84,72},{96,84},{10... | collective-permute-start | bytes 516104 | tf_op jit(solution)/shard_map/ppermute | solution.py:424
  91.0 5.2 %collective-permute-start.6 = (f32[3,1,72,128]{3,2,1,0:T(8,128)S(1)}, f32[3,1,72,128]{3,2,1,0:T(8,128)S(1)}, u32[]{:S(2)}, u32[]{:S(2)}) collective-permute-start(f32[3,1,72,128]{3,2,1,0:T(8,128)S(1)} %get-tuple-element.190), channel_id=1, source_target_pairs={{0,24},{12,36},{24,48},{36,60},{48,72},{60,84},{72,96},{84,108},{9... | collective-permute-start | bytes 331784 | tf_op jit(solution)/shard_map/ppermute | solution.py:423
  96.4 2.1 %collective-permute-start.9 = (f32[3,1,72,128]{3,2,1,0:T(8,128)S(1)}, f32[3,1,72,128]{3,2,1,0:T(8,128)S(1)}, u32[]{:S(2)}, u32[]{:S(2)}) collective-permute-start(f32[3,1,72,128]{3,2,1,0:T(8,128)S(1)} %get-tuple-element.189), channel_id=1, source_target_pairs={{24,0},{36,12},{48,24},{60,36},{72,48},{84,60},{96,72},{108,84},{1... | collective-permute-start | bytes 331784 | tf_op jit(solution)/shard_map/ppermute | solution.py:424
  98.6 7.7 %collective-permute-done.9 = f32[3,1,72,128]{3,2,1,0:T(8,128)S(1)} collective-permute-done((f32[3,1,72,128]{3,2,1,0:T(8,128)S(1)}, f32[3,1,72,128]{3,2,1,0:T(8,128)S(1)}, u32[]{:S(2)}, u32[]{:S(2)}) %collective-permute-start.9) | collective-permute-done | bytes 110624 | tf_op jit(solution)/shard_map/ppermute | solution.py:424
  107.0 0.7 copy-done.3
  107.7 0.4 fusion.101
  108.5 0.4 fusion.80
  111.8 1.8 %slice_add_fusion.23 = f32[3,2,32,128]{3,2,1,0:T(8,128)} fusion(f32[3,4,34,128]{3,2,1,0:T(8,128)S(1)} %get-tuple-element.4, f32[3,6,36,128]{3,2,1,0:T(8,128)S(1)} %get-tuple-element.8, f32[3,8,38,128]{3,2,1,0:T(8,128)S(1)} %get-tuple-element.12, f32[3,10,40,128]{3,2,1,0:T(8,128)S(1)} %bitcast.597, f32[3,4,58,128]{3,2,1,0:T(8,128)} %copy-done.4, ...), kind=kLoop, calls=%fused_computation.356 | loop fusion | flops 147456 | bytes 786432 | tf_op jit(solution)/shard_map/add | solution.py:304
  114.2 0.7 slice_subtract_fusion.45
  (194 shorter events, 14.5 us)
Async XLA Ops:
  0.6 18.3 %copy-start.8 = (s32[1,12]{1,0:T(1,128)S(1)}, s32[1,12]{1,0:T(1,128)}, u32[]{:S(2)}) copy-start(s32[1,12]{1,0:T(1,128)} %param.7) | copy-start | bytes 148
  1.6 25.4 %collective-permute-start.1 = (f32[5,2,32,128]{3,2,1,0:T(8,128)S(1)}, f32[5,2,32,128]{3,2,1,0:T(8,128)S(1)}, u32[]{:S(2)}, u32[]{:S(2)}) collective-permute-start(f32[5,2,32,128]{3,2,1,0:T(8,128)S(1)} %pad_maximum_fusion.1), channel_id=1, source_target_pairs={{0,12},{12,24},{24,36},{36,48},{48,60},{60,72},{72,84},{84,96},{96... | collective-permute-start | bytes 491528 | tf_op jit(solution)/shard_map/ppermute | solution.py:232
  3.5 23.5 %collective-permute-start.2 = (f32[5,2,32,128]{3,2,1,0:T(8,128)S(1)}, f32[5,2,32,128]{3,2,1,0:T(8,128)S(1)}, u32[]{:S(2)}, u32[]{:S(2)}) collective-permute-start(f32[5,2,32,128]{3,2,1,0:T(8,128)S(1)} %pad_maximum_fusion.1), channel_id=1, source_target_pairs={{12,0},{24,12},{36,24},{48,36},{60,48},{72,60},{84,72},{96,84},{10... | collective-permute-start | bytes 491528 | tf_op jit(solution)/shard_map/ppermute | solution.py:233
  8.8 18.2 %copy-start.5 = (f32[3,2,32,128]{3,2,1,0:T(8,128)S(1)}, f32[3,2,32,128]{3,2,1,0:T(8,128)}, u32[]{:S(2)}) copy-start(f32[3,2,32,128]{3,2,1,0:T(8,128)} %param.4) | copy-start | bytes 294916
  8.8 18.2 %copy-start.6 = (f32[2,32,128]{2,1,0:T(8,128)S(1)}, f32[2,32,128]{2,1,0:T(8,128)}, u32[]{:S(2)}) copy-start(f32[2,32,128]{2,1,0:T(8,128)} %param.6) | copy-start | bytes 98308
  8.8 18.2 %copy-start.7 = (f32[2,32,128]{2,1,0:T(8,128)S(1)}, f32[2,32,128]{2,1,0:T(8,128)}, u32[]{:S(2)}) copy-start(f32[2,32,128]{2,1,0:T(8,128)} %param.5) | copy-start | bytes 98308
  8.8 12.7 %collective-permute-start = (f32[7,1,32,128]{3,2,1,0:T(8,128)S(1)}, f32[7,1,32,128]{3,2,1,0:T(8,128)S(1)}, u32[]{:S(2)}, u32[]{:S(2)}) collective-permute-start(f32[7,1,32,128]{3,2,1,0:T(8,128)S(1)} %get-tuple-element.188), channel_id=1, source_target_pairs={{0,24},{12,36},{24,48},{36,60},{48,72},{60,84},{72,96},{84,108},{9... | collective-permute-start | bytes 344072 | tf_op jit(solution)/shard_map/ppermute | solution.py:248
  16.9 10.0 %collective-permute-start.3 = (f32[7,1,32,128]{3,2,1,0:T(8,128)S(1)}, f32[7,1,32,128]{3,2,1,0:T(8,128)S(1)}, u32[]{:S(2)}, u32[]{:S(2)}) collective-permute-start(f32[7,1,32,128]{3,2,1,0:T(8,128)S(1)} %get-tuple-element.187), channel_id=1, source_target_pairs={{24,0},{36,12},{48,24},{60,36},{72,48},{84,60},{96,72},{108,84},{1... | collective-permute-start | bytes 344072 | tf_op jit(solution)/shard_map/ppermute | solution.py:251
  27.2 10.2 %collective-permute-start.5 = (f32[5,10,16,128]{3,2,1,0:T(8,128)S(1)}, f32[5,10,16,128]{3,2,1,0:T(8,128)S(1)}, u32[]{:S(2)}, u32[]{:S(2)}) collective-permute-start(f32[5,10,16,128]{3,2,1,0:T(8,128)S(1)} %get-tuple-element.52), channel_id=1, source_target_pairs={{1,0},{2,1},{3,2},{4,3},{5,4},{6,5},{7,6},{8,7},{9,8},{10,9},{11,1... | collective-permute-start | bytes 1228808 | tf_op jit(solution)/shard_map/ppermute | solution.py:262
  28.5 10.4 %collective-permute-start.4 = (f32[5,10,16,128]{3,2,1,0:T(8,128)S(1)}, f32[5,10,16,128]{3,2,1,0:T(8,128)S(1)}, u32[]{:S(2)}, u32[]{:S(2)}) collective-permute-start(f32[5,10,16,128]{3,2,1,0:T(8,128)S(1)} %get-tuple-element.51), channel_id=1, source_target_pairs={{0,1},{1,2},{2,3},{3,4},{4,5},{5,6},{6,7},{7,8},{8,9},{9,10},{10,1... | collective-permute-start | bytes 1228808 | tf_op jit(solution)/shard_map/ppermute | solution.py:261
  40.0 1.9 %copy-start = (f32[3,8,62,128]{3,2,1,0:T(8,128)}, f32[3,8,62,128]{3,2,1,0:T(8,128)S(1)}, u32[]{:S(2)}) copy-start(f32[3,8,62,128]{3,2,1,0:T(8,128)S(1)} %get-tuple-element.37) | copy-start | bytes 2285572
  42.2 1.4 %copy-start.1 = (f32[3,6,60,128]{3,2,1,0:T(8,128)}, f32[3,6,60,128]{3,2,1,0:T(8,128)S(1)}, u32[]{:S(2)}) copy-start(f32[3,6,60,128]{3,2,1,0:T(8,128)S(1)} %get-tuple-element.33) | copy-start | bytes 1658884
  43.8 0.7 copy-start.4
  45.0 4.0 %copy-start.2 = (f32[3,2,56,128]{3,2,1,0:T(8,128)}, f32[3,2,56,128]{3,2,1,0:T(8,128)S(1)}, u32[]{:S(2)}) copy-start(f32[3,2,56,128]{3,2,1,0:T(8,128)S(1)} %slice_subtract_fusion.14) | copy-start | bytes 516100
  84.1 0.9 slice-start
  85.1 13.5 %collective-permute-start.7 = (f32[3,2,56,128]{3,2,1,0:T(8,128)S(1)}, f32[3,2,56,128]{3,2,1,0:T(8,128)S(1)}, u32[]{:S(2)}, u32[]{:S(2)}) collective-permute-start(f32[3,2,56,128]{3,2,1,0:T(8,128)S(1)} %pad_maximum_fusion), channel_id=1, source_target_pairs={{0,12},{12,24},{24,36},{36,48},{48,60},{60,72},{72,84},{84,96},{96... | collective-permute-start | bytes 516104 | tf_op jit(solution)/shard_map/ppermute | solution.py:423
  87.0 11.6 %collective-permute-start.8 = (f32[3,2,56,128]{3,2,1,0:T(8,128)S(1)}, f32[3,2,56,128]{3,2,1,0:T(8,128)S(1)}, u32[]{:S(2)}, u32[]{:S(2)}) collective-permute-start(f32[3,2,56,128]{3,2,1,0:T(8,128)S(1)} %pad_maximum_fusion), channel_id=1, source_target_pairs={{12,0},{24,12},{36,24},{48,36},{60,48},{72,60},{84,72},{96,84},{10... | collective-permute-start | bytes 516104 | tf_op jit(solution)/shard_map/ppermute | solution.py:424
  91.0 7.6 %collective-permute-start.6 = (f32[3,1,72,128]{3,2,1,0:T(8,128)S(1)}, f32[3,1,72,128]{3,2,1,0:T(8,128)S(1)}, u32[]{:S(2)}, u32[]{:S(2)}) collective-permute-start(f32[3,1,72,128]{3,2,1,0:T(8,128)S(1)} %get-tuple-element.190), channel_id=1, source_target_pairs={{0,24},{12,36},{24,48},{36,60},{48,72},{60,84},{72,96},{84,108},{9... | collective-permute-start | bytes 331784 | tf_op jit(solution)/shard_map/ppermute | solution.py:423
  96.4 10.0 %collective-permute-start.9 = (f32[3,1,72,128]{3,2,1,0:T(8,128)S(1)}, f32[3,1,72,128]{3,2,1,0:T(8,128)S(1)}, u32[]{:S(2)}, u32[]{:S(2)}) collective-permute-start(f32[3,1,72,128]{3,2,1,0:T(8,128)S(1)} %get-tuple-element.189), channel_id=1, source_target_pairs={{24,0},{36,12},{48,24},{60,36},{72,48},{84,60},{96,72},{108,84},{1... | collective-permute-start | bytes 331784 | tf_op jit(solution)/shard_map/ppermute | solution.py:424
  106.8 0.9 copy-start.3

commit v10 on v7

--- a/solution.py
+++ b/solution.py
@@ -305,10 +305,31 @@
 
     stacked = jnp.concatenate([rhs_field, shear_modulus[None], lame_lambda[None]], axis=0)
     stacked = halo_x(stacked, depth + 1)
-    stacked = halo_y(stacked, deep_y)
-    mu_ext = stacked[3]
-    lam_ext = stacked[4]
-    rhs_ext = crop(stacked[0:3], 1)
+    coef_x = stacked[3:5]
+    rhs_x = stacked[0:3, 1:-1]
+    count_y = lax.axis_size("gy")
+
+    def rows_of(part, pick):
+        return part[..., pick, :].reshape((-1,) + part[..., pick, :].shape[-2:])
+
+    low_rows = slice(width_y - deep_y, width_y)
+    high_rows = slice(0, deep_y)
+    send_low = jnp.concatenate([rows_of(coef_x, low_rows), rows_of(rhs_x, low_rows)], axis=0)
+    send_high = jnp.concatenate([rows_of(coef_x, high_rows), rows_of(rhs_x, high_rows)], axis=0)
+    got_low = lax.ppermute(send_low, "gy", [(i, i + 1) for i in range(count_y - 1)])
+    got_high = lax.ppermute(send_high, "gy", [(i + 1, i) for i in range(count_y - 1)])
+    split = coef_x.shape[0] * coef_x.shape[1]
+    coef_shape = coef_x.shape[:2] + (deep_y, width_z)
+    rhs_shape = rhs_x.shape[:2] + (deep_y, width_z)
+    coef_ext = jnp.concatenate(
+        [got_low[:split].reshape(coef_shape), coef_x, got_high[:split].reshape(coef_shape)], axis=2
+    )
+    rhs_full = jnp.concatenate(
+        [got_low[split:].reshape(rhs_shape), rhs_x, got_high[split:].reshape(rhs_shape)], axis=2
+    )
+    mu_ext = coef_ext[0]
+    lam_ext = coef_ext[1]
+    rhs_ext = rhs_full[:, :, 1:-1]
     inside = inside_mask(width_x, width_y, depth, deep_y - 1)
     inverse_diag = jnp.where(inside[None], 1.0 / diagonal_ext(mu_ext, lam_ext, 1.0), 0.0)
 

time: 114 us -> 123 us (1.079)
  local copies, waits for them, and re-layouts: 8.3 us -> 15.9 us
  other arithmetic: 16.9 us -> 21.6 us
  blocking collectives: 33.6 us -> 29.9 us
  waiting for transfers between devices: 21.4 us -> 19.4 us
  starting transfers between devices: 31.3 us -> 32.7 us
    unnamed x28 -> x76, local copies, waits for them, and re-layouts: 1.27 us -> 7.09 us
    psum x1, blocking collectives: 33.6 us -> 29.9 us  [shards(): all_sums = lax.psum(slots, 'gy')]
    ppermute x2, starting transfers between devices: 7.23 us -> 9.3 us  [shards(): got_low = lax.ppermute(send_low, 'gx', forward)]
    ppermute x2, waiting for transfers between devices: 5.45 us -> 3.38 us  [halo_x(): highs.append(lax.ppermute(array[..., :need, :, :], 'gx', backward))]
    mul x9, other arithmetic: 1.31 us -> 3.17 us  [operate(): results.append(scale * (-laplace[comp_id] - grad_term))]
  transfers between devices with their start and end apart: 10 -> 10, of which waited for: 4 -> 4; matrix products, arithmetic and copies ran while one was open for 4% -> 6% of each run, Pallas kernels for 0% -> 0%
where the time goes in v10:
time: 123 us; the launch traced here: 122 us
  starting transfers between devices  32.7 us (27%)
  blocking collectives  29.9 us (24%)
  other arithmetic  21.6 us (18%)
  waiting for transfers between devices  19.4 us (16%)
  local copies, waits for them, and re-layouts  15.9 us (13%)
  between operations  1.81 us (1%)
    psum x1, blocking collectives, shards(): all_sums = lax.psum(slots, 'gy')  29.9 us
    ppermute x2, starting transfers between devices, shards(): got_low = lax.ppermute(send_low, 'gx', forward)  9.3 us
    unnamed x76, local copies, waits for them, and re-layouts  7.09 us
    ppermute x2, waiting for transfers between devices, shards(): got_high = lax.ppermute(send_high, 'gx', backward)  6.79 us
    ppermute x2, starting transfers between devices, halo_x(): lows.append(lax.ppermute(array[..., width - need:, :, :], 'gx', forward))  6.53 us
    ppermute x2, starting transfers between devices, shards(): got_high = lax.ppermute(send_high, 'gx', backward)  5.74 us
    another operation x21, other arithmetic, apply_ext(): return jnp.stack(results)  5.67 us
    ppermute x2, starting transfers between devices, halo_x(): highs.append(lax.ppermute(array[..., :need, :, :], 'gx', backward))  5.56 us
  transfers between devices with their start and end apart: 10, of which 4 were waited for; matrix products, arithmetic and copies ran while one was open for 6% of the time, Pallas kernels for 0%

profile of v10, /device:TPU:30, one launch (start us, length us, event | category | flops | bytes accessed | tf_op | source)
XLA Modules:
  0.0 122.0 jit_solution(9097566957283404461)
XLA Ops:
  0.6 0.9 pad_maximum_fusion.5
  1.6 4.6 %collective-permute-start = (f32[5,2,32,128]{3,2,1,0:T(8,128)S(1)}, f32[5,2,32,128]{3,2,1,0:T(8,128)S(1)}, u32[]{:S(2)}, u32[]{:S(2)}) collective-permute-start(f32[5,2,32,128]{3,2,1,0:T(8,128)S(1)} %pad_maximum_fusion.5), channel_id=1, source_target_pairs={{0,24},{12,36},{24,48},{36,60},{48,72},{60,84},{72,96},{84,108},{9... | collective-permute-start | bytes 491528 | tf_op jit(solution)/shard_map/ppermute | solution.py:216
  6.2 1.9 %collective-permute-start.1 = (f32[5,2,32,128]{3,2,1,0:T(8,128)S(1)}, f32[5,2,32,128]{3,2,1,0:T(8,128)S(1)}, u32[]{:S(2)}, u32[]{:S(2)}) collective-permute-start(f32[5,2,32,128]{3,2,1,0:T(8,128)S(1)} %pad_maximum_fusion.5), channel_id=1, source_target_pairs={{0,12},{12,24},{24,36},{36,48},{48,60},{60,72},{72,84},{84,96},{96... | collective-permute-start | bytes 491528 | tf_op jit(solution)/shard_map/ppermute | solution.py:216
  8.1 3.6 %collective-permute-start.2 = (f32[5,2,32,128]{3,2,1,0:T(8,128)S(1)}, f32[5,2,32,128]{3,2,1,0:T(8,128)S(1)}, u32[]{:S(2)}, u32[]{:S(2)}) collective-permute-start(f32[5,2,32,128]{3,2,1,0:T(8,128)S(1)} %pad_maximum_fusion.5), channel_id=1, source_target_pairs={{12,0},{24,12},{36,24},{48,36},{60,48},{72,60},{84,72},{96,84},{10... | collective-permute-start | bytes 491528 | tf_op jit(solution)/shard_map/ppermute | solution.py:217
  11.8 1.9 %collective-permute-start.3 = (f32[5,2,32,128]{3,2,1,0:T(8,128)S(1)}, f32[5,2,32,128]{3,2,1,0:T(8,128)S(1)}, u32[]{:S(2)}, u32[]{:S(2)}) collective-permute-start(f32[5,2,32,128]{3,2,1,0:T(8,128)S(1)} %pad_maximum_fusion.5), channel_id=1, source_target_pairs={{24,0},{36,12},{48,24},{60,36},{72,48},{84,60},{96,72},{108,84},{1... | collective-permute-start | bytes 491528 | tf_op jit(solution)/shard_map/ppermute | solution.py:217
  15.1 0.8 fusion.485
  17.0 1.4 %compare_select_fusion.8 = f32[2]{0:T(128)S(1)} fusion(s32[1]{0:T(128)} %bitcast.40, s32[1]{0:T(128)} %bitcast.39), kind=kLoop, calls=%fused_computation.858 | loop fusion | flops 6 | bytes 16 | tf_op jit(solution)/shard_map/jit(_where)/select_n | solution.py:101
  19.1 0.8 copy-done.7
  20.0 3.4 %collective-permute-done.3 = f32[5,2,32,128]{3,2,1,0:T(8,128)S(1)} collective-permute-done((f32[5,2,32,128]{3,2,1,0:T(8,128)S(1)}, f32[5,2,32,128]{3,2,1,0:T(8,128)S(1)}, u32[]{:S(2)}, u32[]{:S(2)}) %collective-permute-start.3) | collective-permute-done | bytes 163872 | tf_op jit(solution)/shard_map/ppermute | solution.py:217
  23.5 4.3 %collective-permute-start.4 = (f32[44,16,128]{2,1,0:T(8,128)S(1)}, f32[44,16,128]{2,1,0:T(8,128)S(1)}, u32[]{:S(2)}, u32[]{:S(2)}) collective-permute-start(f32[44,16,128]{2,1,0:T(8,128)S(1)} %pad_maximum_fusion.2), channel_id=1, source_target_pairs={{0,1},{1,2},{2,3},{3,4},{4,5},{5,6},{6,7},{7,8},{8,9},{9,10},{10,1... | collective-permute-start | bytes 1081352 | tf_op jit(solution)/shard_map/ppermute | solution.py:319
  27.8 1.3 %collective-permute-start.5 = (f32[44,16,128]{2,1,0:T(8,128)S(1)}, f32[44,16,128]{2,1,0:T(8,128)S(1)}, u32[]{:S(2)}, u32[]{:S(2)}) collective-permute-start(f32[44,16,128]{2,1,0:T(8,128)S(1)} %pad_maximum_fusion.3), channel_id=1, source_target_pairs={{1,0},{2,1},{3,2},{4,3},{5,4},{6,5},{7,6},{8,7},{9,8},{10,9},{11,1... | collective-permute-start | bytes 1081352 | tf_op jit(solution)/shard_map/ppermute | solution.py:320
  30.6 4.4 %collective-permute-done.4 = f32[44,16,128]{2,1,0:T(8,128)S(1)} collective-permute-done((f32[44,16,128]{2,1,0:T(8,128)S(1)}, f32[44,16,128]{2,1,0:T(8,128)S(1)}, u32[]{:S(2)}, u32[]{:S(2)}) %collective-permute-start.4) | collective-permute-done | bytes 360480 | tf_op jit(solution)/shard_map/ppermute | solution.py:319
  35.0 4.8 %collective-permute-done.5 = f32[44,16,128]{2,1,0:T(8,128)S(1)} collective-permute-done((f32[44,16,128]{2,1,0:T(8,128)S(1)}, f32[44,16,128]{2,1,0:T(8,128)S(1)}, u32[]{:S(2)}, u32[]{:S(2)}) %collective-permute-start.5) | collective-permute-done | bytes 360480 | tf_op jit(solution)/shard_map/ppermute | solution.py:320
  41.1 0.9 slice-done.1
  52.5 0.8 fusion.364
  53.3 0.8 fusion.345
  54.1 0.7 fusion.327
  55.5 29.9 %psum.7 = f32[12,3]{0,1:T(4,128)S(1)} all-reduce(f32[12,3]{0,1:T(4,128)S(1)} %broadcast_select_fusion), channel_id=1, replica_groups=mesh['gx'=64,'gy'=12] {'gy'}, use_global_device_ids=true, to_apply=%region_6.7 | all-reduce | flops 36 | bytes 288 | tf_op jit(solution)/shard_map/psum | solution.py:355
  85.5 0.7 broadcast_divide_fusion
  86.2 0.8 gather_fusion
  87.1 0.7 select_bitcast_fusion
  88.2 0.7 copy-done.4
  90.5 0.7 slice-done
  91.2 1.9 %collective-permute-start.7 = (f32[3,2,56,128]{3,2,1,0:T(8,128)S(1)}, f32[3,2,56,128]{3,2,1,0:T(8,128)S(1)}, u32[]{:S(2)}, u32[]{:S(2)}) collective-permute-start(f32[3,2,56,128]{3,2,1,0:T(8,128)S(1)} %pad_maximum_fusion.4), channel_id=1, source_target_pairs={{0,12},{12,24},{24,36},{36,48},{48,60},{60,72},{72,84},{84,96},{96... | collective-permute-start | bytes 516104 | tf_op jit(solution)/shard_map/ppermute | solution.py:408
  93.1 3.6 %collective-permute-start.8 = (f32[3,2,56,128]{3,2,1,0:T(8,128)S(1)}, f32[3,2,56,128]{3,2,1,0:T(8,128)S(1)}, u32[]{:S(2)}, u32[]{:S(2)}) collective-permute-start(f32[3,2,56,128]{3,2,1,0:T(8,128)S(1)} %pad_maximum_fusion.4), channel_id=1, source_target_pairs={{12,0},{24,12},{36,24},{48,36},{60,48},{72,60},{84,72},{96,84},{10... | collective-permute-start | bytes 516104 | tf_op jit(solution)/shard_map/ppermute | solution.py:409
  97.1 0.7 copy-done.8
  97.9 7.4 %collective-permute-start.6 = (f32[3,1,72,128]{3,2,1,0:T(8,128)S(1)}, f32[3,1,72,128]{3,2,1,0:T(8,128)S(1)}, u32[]{:S(2)}, u32[]{:S(2)}) collective-permute-start(f32[3,1,72,128]{3,2,1,0:T(8,128)S(1)} %get-tuple-element.188), channel_id=1, source_target_pairs={{0,24},{12,36},{24,48},{36,60},{48,72},{60,84},{72,96},{84,108},{9... | collective-permute-start | bytes 331784 | tf_op jit(solution)/shard_map/ppermute | solution.py:408
  105.4 2.1 %collective-permute-start.9 = (f32[3,1,72,128]{3,2,1,0:T(8,128)S(1)}, f32[3,1,72,128]{3,2,1,0:T(8,128)S(1)}, u32[]{:S(2)}, u32[]{:S(2)}) collective-permute-start(f32[3,1,72,128]{3,2,1,0:T(8,128)S(1)} %get-tuple-element.187), channel_id=1, source_target_pairs={{24,0},{36,12},{48,24},{60,36},{72,48},{84,60},{96,72},{108,84},{1... | collective-permute-start | bytes 331784 | tf_op jit(solution)/shard_map/ppermute | solution.py:409
  107.7 0.9 copy-done.1
  108.6 6.8 %collective-permute-done.9 = f32[3,1,72,128]{3,2,1,0:T(8,128)S(1)} collective-permute-done((f32[3,1,72,128]{3,2,1,0:T(8,128)S(1)}, f32[3,1,72,128]{3,2,1,0:T(8,128)S(1)}, u32[]{:S(2)}, u32[]{:S(2)}) %collective-permute-start.9) | collective-permute-done | bytes 110624 | tf_op jit(solution)/shard_map/ppermute | solution.py:409
  120.3 0.7 slice_add_fusion.23
  121.4 0.7 slice_subtract_fusion.46
  (245 shorter events, 24.6 us)
Async XLA Ops:
  1.6 17.4 %collective-permute-start = (f32[5,2,32,128]{3,2,1,0:T(8,128)S(1)}, f32[5,2,32,128]{3,2,1,0:T(8,128)S(1)}, u32[]{:S(2)}, u32[]{:S(2)}) collective-permute-start(f32[5,2,32,128]{3,2,1,0:T(8,128)S(1)} %pad_maximum_fusion.5), channel_id=1, source_target_pairs={{0,24},{12,36},{24,48},{36,60},{48,72},{60,84},{72,96},{84,108},{9... | collective-permute-start | bytes 491528 | tf_op jit(solution)/shard_map/ppermute | solution.py:216
  6.2 12.9 %collective-permute-start.1 = (f32[5,2,32,128]{3,2,1,0:T(8,128)S(1)}, f32[5,2,32,128]{3,2,1,0:T(8,128)S(1)}, u32[]{:S(2)}, u32[]{:S(2)}) collective-permute-start(f32[5,2,32,128]{3,2,1,0:T(8,128)S(1)} %pad_maximum_fusion.5), channel_id=1, source_target_pairs={{0,12},{12,24},{24,36},{36,48},{48,60},{60,72},{72,84},{84,96},{96... | collective-permute-start | bytes 491528 | tf_op jit(solution)/shard_map/ppermute | solution.py:216
  8.1 11.8 %collective-permute-start.2 = (f32[5,2,32,128]{3,2,1,0:T(8,128)S(1)}, f32[5,2,32,128]{3,2,1,0:T(8,128)S(1)}, u32[]{:S(2)}, u32[]{:S(2)}) collective-permute-start(f32[5,2,32,128]{3,2,1,0:T(8,128)S(1)} %pad_maximum_fusion.5), channel_id=1, source_target_pairs={{12,0},{24,12},{36,24},{48,36},{60,48},{72,60},{84,72},{96,84},{10... | collective-permute-start | bytes 491528 | tf_op jit(solution)/shard_map/ppermute | solution.py:217
  11.8 11.6 %collective-permute-start.3 = (f32[5,2,32,128]{3,2,1,0:T(8,128)S(1)}, f32[5,2,32,128]{3,2,1,0:T(8,128)S(1)}, u32[]{:S(2)}, u32[]{:S(2)}) collective-permute-start(f32[5,2,32,128]{3,2,1,0:T(8,128)S(1)} %pad_maximum_fusion.5), channel_id=1, source_target_pairs={{24,0},{36,12},{48,24},{60,36},{72,48},{84,60},{96,72},{108,84},{1... | collective-permute-start | bytes 491528 | tf_op jit(solution)/shard_map/ppermute | solution.py:217
  13.7 33.2 %copy-start.27 = (s32[128]{0:T(128)}, s32[128]{0:T(128)S(1)}, u32[]{:S(2)}) copy-start(s32[128]{0:T(128)S(1)} %and_select_fusion) | copy-start | bytes 1540
  14.9 14.3 %copy-start.25 = (pred[3]{0:T(512)(128)(4,1)}, pred[3]{0:T(512)(128)(4,1)S(1)}, u32[]{:S(2)}) copy-start(pred[3]{0:T(512)(128)(4,1)S(1)} %get-tuple-element.204) | copy-start | bytes 13
  19.0 28.4 %copy-start.22 = (f32[3]{0:T(128)}, f32[3]{0:T(128)S(1)}, u32[]{:S(2)}) copy-start(f32[3]{0:T(128)S(1)} %get-tuple-element.199) | copy-start | bytes 40
  19.0 0.9 copy-start.7
  19.0 0.9 copy-start.16
  19.1 0.9 copy-start.17
  23.5 11.5 %collective-permute-start.4 = (f32[44,16,128]{2,1,0:T(8,128)S(1)}, f32[44,16,128]{2,1,0:T(8,128)S(1)}, u32[]{:S(2)}, u32[]{:S(2)}) collective-permute-start(f32[44,16,128]{2,1,0:T(8,128)S(1)} %pad_maximum_fusion.2), channel_id=1, source_target_pairs={{0,1},{1,2},{2,3},{3,4},{4,5},{5,6},{6,7},{7,8},{8,9},{9,10},{10,1... | collective-permute-start | bytes 1081352 | tf_op jit(solution)/shard_map/ppermute | solution.py:319
  27.8 12.0 %collective-permute-start.5 = (f32[44,16,128]{2,1,0:T(8,128)S(1)}, f32[44,16,128]{2,1,0:T(8,128)S(1)}, u32[]{:S(2)}, u32[]{:S(2)}) collective-permute-start(f32[44,16,128]{2,1,0:T(8,128)S(1)} %pad_maximum_fusion.3), channel_id=1, source_target_pairs={{1,0},{2,1},{3,2},{4,3},{5,4},{6,5},{7,6},{8,7},{9,8},{10,9},{11,1... | collective-permute-start | bytes 1081352 | tf_op jit(solution)/shard_map/ppermute | solution.py:320
  35.0 6.0 %copy-start.2 = (f32[44,16,128]{2,1,0:T(8,128)}, f32[44,16,128]{2,1,0:T(8,128)S(1)}, u32[]{:S(2)}) copy-start(f32[44,16,128]{2,1,0:T(8,128)S(1)} %collective-permute-done.4) | copy-start | bytes 1081348
  41.1 0.9 slice-start.1
  46.9 7.9 %copy-start = (f32[3,2,56,128]{3,2,1,0:T(8,128)}, f32[3,2,56,128]{3,2,1,0:T(8,128)S(1)}, u32[]{:S(2)}) copy-start(f32[3,2,56,128]{3,2,1,0:T(8,128)S(1)} %slice_subtract_fusion.15) | copy-start | bytes 516100
  50.5 1.1 copy-start.3
  50.7 0.9 copy-start.5
  54.1 1.4 %copy-start.30 = (pred[12]{0:T(512)(128)(4,1)S(1)}, pred[12]{0:T(512)(128)(4,1)}, u32[]{:S(2)}) copy-start(pred[12]{0:T(512)(128)(4,1)} %iota_compare_fusion.9) | copy-start | bytes 40
  55.4 29.9 %copy-start.21 = (f32[12,12]{1,0:T(8,128)S(1)}, f32[12,12]{1,0:T(8,128)}, u32[]{:S(2)}) copy-start(f32[12,12]{1,0:T(8,128)} %get-tuple-element.198) | copy-start | bytes 1732
  85.4 2.7 %copy-start.20 = (f32[3,1,16,64]{3,2,1,0:T(8,128)S(1)}, f32[3,1,16,64]{3,2,1,0:T(8,128)}, u32[]{:S(2)}) copy-start(f32[3,1,16,64]{3,2,1,0:T(8,128)} %fusion.327) | copy-start | bytes 36868
  86.2 1.9 %copy-start.18 = (f32[3,1,16,64]{3,2,1,0:T(8,128)S(1)}, f32[3,1,16,64]{3,2,1,0:T(8,128)}, u32[]{:S(2)}) copy-start(f32[3,1,16,64]{3,2,1,0:T(8,128)} %get-tuple-element.21) | copy-start | bytes 36868
  86.2 1.9 %copy-start.19 = (f32[3,1,16,64]{3,2,1,0:T(8,128)S(1)}, f32[3,1,16,64]{3,2,1,0:T(8,128)}, u32[]{:S(2)}) copy-start(f32[3,1,16,64]{3,2,1,0:T(8,128)} %fusion.345) | copy-start | bytes 36868
  88.9 0.8 copy-start.13
  88.9 0.8 copy-start.15
  90.3 0.9 slice-start
  91.2 16.4 %collective-permute-start.7 = (f32[3,2,56,128]{3,2,1,0:T(8,128)S(1)}, f32[3,2,56,128]{3,2,1,0:T(8,128)S(1)}, u32[]{:S(2)}, u32[]{:S(2)}) collective-permute-start(f32[3,2,56,128]{3,2,1,0:T(8,128)S(1)} %pad_maximum_fusion.4), channel_id=1, source_target_pairs={{0,12},{12,24},{24,36},{36,48},{48,60},{60,72},{72,84},{84,96},{96... | collective-permute-start | bytes 516104 | tf_op jit(solution)/shard_map/ppermute | solution.py:408
  93.1 15.4 %collective-permute-start.8 = (f32[3,2,56,128]{3,2,1,0:T(8,128)S(1)}, f32[3,2,56,128]{3,2,1,0:T(8,128)S(1)}, u32[]{:S(2)}, u32[]{:S(2)}) collective-permute-start(f32[3,2,56,128]{3,2,1,0:T(8,128)S(1)} %pad_maximum_fusion.4), channel_id=1, source_target_pairs={{12,0},{24,12},{36,24},{48,36},{60,48},{72,60},{84,72},{96,84},{10... | collective-permute-start | bytes 516104 | tf_op jit(solution)/shard_map/ppermute | solution.py:409
  97.0 0.8 copy-start.8
  97.0 0.9 copy-start.9
  97.9 9.7 %collective-permute-start.6 = (f32[3,1,72,128]{3,2,1,0:T(8,128)S(1)}, f32[3,1,72,128]{3,2,1,0:T(8,128)S(1)}, u32[]{:S(2)}, u32[]{:S(2)}) collective-permute-start(f32[3,1,72,128]{3,2,1,0:T(8,128)S(1)} %get-tuple-element.188), channel_id=1, source_target_pairs={{0,24},{12,36},{24,48},{36,60},{48,72},{60,84},{72,96},{84,108},{9... | collective-permute-start | bytes 331784 | tf_op jit(solution)/shard_map/ppermute | solution.py:408
  105.4 10.0 %collective-permute-start.9 = (f32[3,1,72,128]{3,2,1,0:T(8,128)S(1)}, f32[3,1,72,128]{3,2,1,0:T(8,128)S(1)}, u32[]{:S(2)}, u32[]{:S(2)}) collective-permute-start(f32[3,1,72,128]{3,2,1,0:T(8,128)S(1)} %get-tuple-element.187), channel_id=1, source_target_pairs={{24,0},{36,12},{48,24},{60,36},{72,48},{84,60},{96,72},{108,84},{1... | collective-permute-start | bytes 331784 | tf_op jit(solution)/shard_map/ppermute | solution.py:409
  107.6 0.9 copy-start.1
  (12 other events, 8.0 us)
